TPU v7x, 256 devices: a whole 4x4x8 slice. The times are simulated.
256 devices in a mesh: ctx: 32 (over z, x_lo, core), heads: 8 (over x_hi, y).
Axes of the slice: x: 4 (x_hi: 2, x_lo: 2; x = x_hi * 2 + x_lo), y: 4, z: 8, core: 2. Of those that a mesh axis runs over, the one named last changes fastest.
Arguments:
- hidden: bfloat16 [16384, 5376], P(('ctx', 'heads')), may hold values from -8 to 8
- query_weight: bfloat16 [5376, 2048], P(None, 'heads'), may hold values from -0.5 to 0.5
- key_weight: bfloat16 [5376, 1024], P(None, 'heads'), may hold values from -0.5 to 0.5
- value_weight: bfloat16 [5376, 1024], P(None, 'heads'), may hold values from -0.078125 to 0.078125
- query_gain: float32 [128], replicated, may hold values from 0.5 to 6
- key_gain: float32 [128], replicated, may hold values from 0.5 to 6
- out_grad: bfloat16 [16384, 2048], P('ctx', 'heads'), may hold values from -6 to 6
Outputs:
- attention: bfloat16 [16384, 2048], P('ctx', 'heads')
- input_grad: bfloat16 [16384, 5376], P(('ctx', 'heads'))
- query_weight_grad: float32 [5376, 2048], P('ctx', 'heads')
- key_weight_grad: float32 [5376, 1024], P('ctx', 'heads')
- value_weight_grad: float32 [5376, 1024], P('ctx', 'heads')
All inputs are finite; a program needn't handle non-finite values.
Results may differ from a plain program's by a relative error of at most 0.039.
Values may be sent and summed in bfloat16 or wider, within the bound.
No kernel may reach another device: no remote copies, remote signals or barrier semaphores. Data moves between devices by JAX's collectives and lax.ppermute only.
A program may use at most 128 MiB of HBM per device.

v0:
```python
import math

import jax
import jax.numpy as jnp
from jax import lax
from jax.sharding import PartitionSpec as P

HEAD_DIM = 128
WINDOW = 1024
SCALAR = 168
HEADS = 16
KV_HEADS = 8


def passed_along(block, axis, distance):
    devices = range(lax.axis_size(axis))
    route = [(i - distance, i) for i in devices if i - distance in devices]
    return lax.ppermute(block, axis, route)


def torus_shifts(axis):
    size = lax.axis_size(axis)
    inner = size // 2 if size >= 4 else size
    outer = size // inner
    me = lax.axis_index(axis)

    def moved(index, dx, dy):
        return ((index // inner + dx) % outer) * inner + (index % inner + dy) % inner

    shifts = [(dx, dy) for dx in range(outer) for dy in range(inner)][1:]
    routes = [[(i, moved(i, dx, dy)) for i in range(size)] for dx, dy in shifts]
    targets = [moved(me, dx, dy) for dx, dy in shifts]
    slot_of = [
        ((me // inner - j // inner) % outer) * inner + (me % inner - j % inner) % inner
        for j in range(size)
    ]
    return (size, me, routes, targets, slot_of)


def gather_over(block, axis):
    size, me, routes, targets, slot_of = torus_shifts(axis)
    slots = jnp.stack([block] + [lax.ppermute(block, axis, route) for route in routes])
    order = jnp.stack([jnp.asarray(s, jnp.int32) for s in slot_of])
    return jnp.take(slots, order, axis=0).reshape((size * block.shape[0],) + block.shape[1:])


def scatter_sum_over(full, axis):
    size, me, routes, targets, slot_of = torus_shifts(axis)
    pieces = full.reshape((size, full.shape[0] // size) + full.shape[1:])
    total = lax.dynamic_index_in_dim(pieces, me, 0, keepdims=False).astype(jnp.float32)
    for route, target in zip(routes, targets):
        piece = lax.dynamic_index_in_dim(pieces, target, 0, keepdims=False)
        total = total + lax.ppermute(piece, axis, route).astype(jnp.float32)
    return total


def ring_scatter_sum(blocks, axis, count, stride):
    size = lax.axis_size(axis)
    me = lax.axis_index(axis)
    digit = (me // stride) % count
    half = blocks.shape[-1] // 2

    def route(step):
        return [
            (i, i - ((i // stride) % count) * stride + (((i // stride) % count + step) % count) * stride)
            for i in range(size)
        ]

    def chunk(k, step, lo):
        block = lax.dynamic_index_in_dim(blocks, (digit - step * (k + 1)) % count, 0, keepdims=False)
        return block[..., lo : lo + half]

    def advance(k, carry):
        up, down = carry
        up = lax.ppermute(up.astype(jnp.bfloat16), axis, route(1)).astype(jnp.float32)
        down = lax.ppermute(down.astype(jnp.bfloat16), axis, route(-1)).astype(jnp.float32)
        return (up + chunk(k + 1, 1, 0), down + chunk(k + 1, -1, half))

    up, down = lax.fori_loop(0, count - 1, advance, (chunk(0, 1, 0), chunk(0, -1, half)))
    return jnp.concatenate([up, down], axis=-1)


def pair_scatter_sum(blocks, axis, stride):
    size = lax.axis_size(axis)
    me = lax.axis_index(axis)
    digit = (me // stride) % 2
    route = [(i, i + stride if (i // stride) % 2 == 0 else i - stride) for i in range(size)]
    own = lax.dynamic_index_in_dim(blocks, digit, 0, keepdims=False).astype(jnp.float32)
    other = lax.dynamic_index_in_dim(blocks, 1 - digit, 0, keepdims=False)
    return own + lax.ppermute(other.astype(jnp.bfloat16), axis, route).astype(jnp.float32)


def ctx_scatter_sum(full, axis, levels):
    outer, middle, inner = levels
    width = full.shape[1]
    grid = full.reshape(outer, middle, inner, -1, width)
    grid = jnp.moveaxis(grid, 2, 0)
    grid = pair_scatter_sum(grid, axis, 1)
    grid = ring_scatter_sum(grid, axis, outer, middle * inner)
    return pair_scatter_sum(grid, axis, inner)


def gather_all(block, axis):
    size = lax.axis_size(axis)
    copies = jnp.broadcast_to(block[None], (size,) + block.shape)
    received = lax.all_to_all(copies, axis, 0, 0)
    return received.reshape((size * block.shape[0],) + block.shape[1:])


def exchange_sum(full, axis):
    size = lax.axis_size(axis)
    pieces = full.reshape((size, full.shape[0] // size) + full.shape[1:])
    received = lax.all_to_all(pieces, axis, 0, 0)
    return jnp.sum(received.astype(jnp.float32), axis=0)


def rope_tables(positions, head_size):
    half_size = head_size // 2
    indices = jnp.arange(half_size, dtype=jnp.float32)
    inverse = jnp.exp(indices * (-2.0 * math.log(10000.0) / head_size))
    angles = positions.astype(jnp.float32)[:, None] * inverse[None, :]
    return (jnp.cos(angles), jnp.sin(angles))


def prepare(projected, cosine, sine_table, channel_gain, factor):
    row_count = projected.shape[0]
    head_size = channel_gain.shape[0]
    pieces = projected.reshape(row_count, -1, head_size)
    normed = (
        pieces * lax.rsqrt(jnp.mean(pieces * pieces, axis=-1, keepdims=True) + 1e-06) * channel_gain
    )
    half_size = head_size // 2
    leading = normed[..., :half_size]
    trailing = normed[..., half_size:]
    cos_rows = cosine[:, None, :]
    sin_rows = sine_table[:, None, :]
    turned = jnp.concatenate(
        [leading * cos_rows - trailing * sin_rows, trailing * cos_rows + leading * sin_rows],
        axis=-1,
    )
    return (turned * factor).reshape(row_count, -1)


def band_mask(query_pos, key_pos):
    separation = query_pos[:, None] - key_pos[None, :]
    return (separation >= 0) & (separation < WINDOW) & (key_pos[None, :] >= 0)


def head_grids(query_block, key_window, value_window, group_size):
    query_grid = query_block.reshape(query_block.shape[0], -1, group_size, HEAD_DIM)
    key_grid = key_window.reshape(key_window.shape[0], -1, HEAD_DIM)
    value_grid = value_window.reshape(value_window.shape[0], -1, HEAD_DIM)
    return (query_grid, key_grid, value_grid)


def attend_forward(query_block, key_window, value_window, allowed, group_size):
    query_grid, key_grid, value_grid = head_grids(query_block, key_window, value_window, group_size)
    scores = jnp.einsum("qkgd,jkd->kgqj", query_grid, key_grid, preferred_element_type=jnp.float32)
    masked = jnp.where(allowed, scores, -1e30)
    highest = jnp.max(masked, axis=-1, keepdims=True)
    total = jnp.sum(jnp.exp(masked - highest), axis=-1, keepdims=True)
    log_total = highest + jnp.log(total)
    weights = jnp.where(allowed, jnp.exp(masked - log_total), 0.0)
    output = jnp.einsum(
        "kgqj,jkd->qkgd",
        weights.astype(jnp.bfloat16),
        value_grid,
        preferred_element_type=jnp.float32,
    )
    return (output.reshape(query_block.shape[0], -1), log_total[..., 0])


def attend_backward(
    query_block,
    key_window,
    value_window,
    allowed,
    log_total,
    out_block,
    attention_block,
    group_size,
):
    query_grid, key_grid, value_grid = head_grids(query_block, key_window, value_window, group_size)
    row_count = query_block.shape[0]
    grad_grid = out_block.reshape(row_count, -1, group_size, HEAD_DIM)
    attention_grid = attention_block.reshape(row_count, -1, group_size, HEAD_DIM)
    scores = jnp.einsum("qkgd,jkd->kgqj", query_grid, key_grid, preferred_element_type=jnp.float32)
    masked = jnp.where(allowed, scores, -1e30)
    weights = jnp.where(allowed, jnp.exp(masked - log_total[..., None]), 0.0)
    delta = jnp.einsum(
        "qkgd,qkgd->kgq", grad_grid, attention_grid, preferred_element_type=jnp.float32
    )
    products = jnp.einsum(
        "qkgd,jkd->kgqj", grad_grid, value_grid, preferred_element_type=jnp.float32
    )
    shifts = (weights * (products - delta[..., None])).astype(jnp.bfloat16)
    query_cot = jnp.einsum(
        "kgqj,jkd->qkgd", shifts, key_grid, preferred_element_type=jnp.float32
    ).reshape(row_count, -1)
    key_cot = jnp.einsum(
        "kgqj,qkgd->jkd", shifts, query_grid, preferred_element_type=jnp.float32
    ).reshape(key_window.shape[0], -1)
    value_cot = jnp.einsum(
        "kgqj,qkgd->jkd",
        weights.astype(jnp.bfloat16),
        grad_grid,
        preferred_element_type=jnp.float32,
    ).reshape(key_window.shape[0], -1)
    return (query_cot, key_cot, value_cot)


def per_device(hidden, query_weight, key_weight, value_weight, query_gain, key_gain, out_grad):
    token_count = out_grad.shape[0]
    group_size = HEADS // KV_HEADS
    block_rows = min(token_count, 512)
    block_count = token_count // block_rows
    window_rows = block_rows + WINDOW
    reach_blocks = (WINDOW - 2) // token_count + 1
    position_base = lax.axis_index("ctx") * token_count
    gathered = gather_all(hidden, "heads")
    query_width = query_weight.shape[1]
    key_width = key_weight.shape[1]
    weight_cat = jnp.concatenate([query_weight, key_weight, value_weight], axis=1)
    projected = jnp.dot(gathered, weight_cat, preferred_element_type=jnp.float32)
    query_proj = projected[:, :query_width]
    key_proj = projected[:, query_width : query_width + key_width]
    value_proj = projected[:, query_width + key_width :]
    positions = position_base + jnp.arange(token_count, dtype=jnp.int32)
    cosine, sine_table = rope_tables(positions, HEAD_DIM)
    query_full, query_back = jax.vjp(
        lambda projected: prepare(projected, cosine, sine_table, query_gain, SCALAR ** (-0.5)),
        query_proj,
    )
    key_full, key_back = jax.vjp(
        lambda projected: prepare(projected, cosine, sine_table, key_gain, 1.0), key_proj
    )
    query_cast = query_full.astype(jnp.bfloat16)
    key_value = jnp.stack([key_full.astype(jnp.bfloat16), value_proj.astype(jnp.bfloat16)])
    received = [passed_along(key_value, "ctx", distance) for distance in range(1, reach_blocks + 1)]
    window_pair = jnp.concatenate(received[::-1] + [key_value], axis=1)
    key_span = window_pair[0]
    value_span = window_pair[1]

    def window_of(block_index):
        block_start = block_index * block_rows
        query_pos = position_base + block_start + jnp.arange(block_rows, dtype=jnp.int32)
        key_pos = position_base - WINDOW + block_start + jnp.arange(window_rows, dtype=jnp.int32)
        return (query_cast, key_span, value_span, band_mask(query_pos, key_pos))

    def forward_block(block_index):
        query_block, key_window, value_window, allowed = window_of(block_index)
        return attend_forward(query_block, key_window, value_window, allowed, group_size)

    outputs, log_totals = lax.map(forward_block, jnp.arange(block_count, dtype=jnp.int32))
    attention = outputs.reshape(token_count, -1).astype(jnp.bfloat16)

    def backward_block(block_index, carry):
        query_acc, pair_acc = carry
        query_block, key_window, value_window, allowed = window_of(block_index)
        block_start = block_index * block_rows
        query_cot, key_cot, value_cot = attend_backward(
            query_block,
            key_window,
            value_window,
            allowed,
            log_totals[block_index],
            out_grad,
            attention,
            group_size,
        )
        query_acc = query_cot
        region = pair_acc + jnp.stack([key_cot, value_cot])
        pair_acc = region
        return (query_acc, pair_acc)

    query_zero = jnp.zeros((token_count, query_weight.shape[1]), jnp.float32)
    pair_zero = jnp.zeros((2, (reach_blocks + 1) * token_count, key_weight.shape[1]), jnp.float32)
    query_acc, pair_acc = lax.fori_loop(0, block_count, backward_block, (query_zero, pair_zero))
    grad_query = query_back(query_acc)[0].astype(jnp.bfloat16)
    grad_scale = float(lax.axis_size("ctx") * token_count) ** (-0.5)
    contract = (((0,), (0,)), ((), ()))
    own_pair = pair_acc[:, reach_blocks * token_count :]
    for distance in range(1, reach_blocks + 1):
        lower_row = (reach_blocks - distance) * token_count
        own_pair = own_pair + passed_along(
            pair_acc[:, lower_row : lower_row + token_count], "ctx", -distance
        )
    grad_key = key_back(own_pair[0])[0].astype(jnp.bfloat16)
    grad_value = own_pair[1].astype(jnp.bfloat16)
    grad_cat = jnp.concatenate([grad_query, grad_key, grad_value], axis=1)
    summed = ctx_scatter_sum(
        (
            lax.dot_general(gathered, grad_cat, contract, preferred_element_type=jnp.float32)
            * grad_scale
        ).astype(jnp.bfloat16),
        "ctx",
        (lax.axis_size("ctx") // 4, 2, 2),
    )
    query_weight_grad = summed[:, :query_width]
    key_weight_grad = summed[:, query_width : query_width + key_width]
    value_weight_grad = summed[:, query_width + key_width :]
    back_contract = (((1,), (1,)), ((), ()))
    input_grad = exchange_sum(
        lax.dot_general(
            grad_cat, weight_cat, back_contract, preferred_element_type=jnp.float32
        ).astype(jnp.bfloat16),
        "heads",
    ).astype(jnp.bfloat16)
    return (attention, input_grad, query_weight_grad, key_weight_grad, value_weight_grad)


def solution(mesh):
    return jax.shard_map(
        per_device,
        mesh=mesh,
        in_specs=(
            P(("ctx", "heads"), None),
            P(None, "heads"),
            P(None, "heads"),
            P(None, "heads"),
            P(),
            P(),
            P("ctx", "heads"),
        ),
        out_specs=(
            P("ctx", "heads"),
            P(("ctx", "heads"), None),
            P("ctx", "heads"),
            P("ctx", "heads"),
            P("ctx", "heads"),
        ),
        check_vma=False,
    )
```

profile of v0, /device:TPU:96, one launch (start us, length us, event | category | flops | bytes accessed | tf_op | source)
XLA Modules:
  0.0 247.1 jit_solution(3371671248199669249)
XLA Ops:
  0.6 3.9 %broadcast_in_dim.71 = bf16[8,64,5376]{2,1,0:T(8,128)(2,1)} broadcast(bf16[64,5376]{1,0:T(8,128)(2,1)} %param.9), dimensions={1,2} | broadcast | bytes 6193152 | tf_op jit(solution)/shard_map/broadcast_in_dim | solution.py:105
  4.5 7.1 %all-to-all-start = ((bf16[8,64,5376]{2,1,0:T(8,128)(2,1)}), bf16[8,64,5376]{2,1,0:T(8,128)(2,1)}, u32[]{:S(2)}, u32[]{:S(2)}) async-start(bf16[8,64,5376]{2,1,0:T(8,128)(2,1)} %broadcast_in_dim.71), calls=%async_computation | async-start | bytes 11010048 | tf_op jit(solution)/shard_map/all_to_all | solution.py:106
  13.6 1.2 fusion.8
  14.8 3.5 %constant_dynamic-update-slice_fusion.2 = bf16[5376,512]{1,0:T(8,128)(2,1)} fusion(bf16[5376,256]{1,0:T(8,128)(2,1)} %param.10), kind=kLoop, calls=%fused_computation.97 | loop fusion | bytes 5505024
  18.3 1.2 constant_dynamic-update-slice_fusion.1
  19.6 2.6 %constant_dynamic-update-slice_fusion = bf16[5376,512]{1,0:T(8,128)(2,1)} fusion(bf16[5376,512]{1,0:T(8,128)(2,1)} %constant_dynamic-update-slice_fusion.1, bf16[5376,128]{1,0:T(8,128)(2,1)} %param.12), kind=kLoop, calls=%fused_computation.95 | loop fusion | bytes 2752512 | tf_op jit(solution)/shard_map/concatenate | solution.py:223
  22.2 52.4 %all-to-all-done = bf16[8,64,5376]{2,1,0:T(8,128)(2,1)} async-done(((bf16[8,64,5376]{2,1,0:T(8,128)(2,1)}), bf16[8,64,5376]{2,1,0:T(8,128)(2,1)}, u32[]{:S(2)}, u32[]{:S(2)}) %all-to-all-start) | async-done | bytes 5505056 | tf_op jit(solution)/shard_map/all_to_all | solution.py:106
  74.6 6.8 %convolution_bitcast_fusion.2 = f32[512,512]{0,1:T(8,128)S(1)} fusion(bf16[5376,512]{1,0:T(8,128)(2,1)} %constant_dynamic-update-slice_fusion, bf16[512,5376]{1,0:T(8,128)(2,1)} %bitcast.4), kind=kOutput, calls=%fused_computation.29 | convolution fusion | flops 2818572288 | bytes 12058624 | tf_op jit(solution)/shard_map/dot_general | solution.py:224
  82.9 2.5 %collective-permute-start.2 = (bf16[2,512,128]{1,2,0:T(8,128)(2,1)}, bf16[2,512,128]{1,2,0:T(8,128)(2,1)}, u32[]{:S(2)}, u32[]{:S(2)}) collective-permute-start(bf16[2,512,128]{1,2,0:T(8,128)(2,1)} %pad_maximum_fusion.2), channel_id=1, source_target_pairs={{0,16},{8,24},{16,32},{24,40},{32,48},{40,56},{48,64},{56,72},{64,... | collective-permute-start | bytes 786440 | tf_op jit(solution)/shard_map/ppermute | solution.py:18
  85.4 2.1 collective-permute-start.3
  88.6 6.6 %collective-permute-done.2 = bf16[2,512,128]{1,2,0:T(8,128)(2,1)} collective-permute-done((bf16[2,512,128]{1,2,0:T(8,128)(2,1)}, bf16[2,512,128]{1,2,0:T(8,128)(2,1)}, u32[]{:S(2)}, u32[]{:S(2)}) %collective-permute-start.2) | collective-permute-done | bytes 262176 | tf_op jit(solution)/shard_map/ppermute | solution.py:18
  95.2 1.2 collective-permute-done.3
  97.5 1.2 fusion.3
  98.7 1.3 exponential_reduce_fusion
  100.0 2.7 %bitcast_convert_fusion = (f32[2,512,128]{1,2,0:T(8,128)S(1)}, bf16[128,2,512]{2,0,1:T(8,128)(2,1)}) fusion(f32[1536,512,2]{1,0,2:T(8,128)S(1)} %get-tuple-element.234, f32[2,512]{1,0:T(2,128)S(1)} %log_add_fusion, pred[512,1536]{0,1:T(8,128)(4,1)S(1)} %fusion.8, bf16[2,1536,128]{1,2,0:T(8,128)(2,1)S(1)} %maximum_maximum_fusion), kind=kOutput, calls=%fused_computation.70 | convolution fusion | flops 409206784 | bytes 8261632 | tf_op jit(solution)/shard_map/while/body/eval_jaxpr/kgqj,jkd->qkgd/dot_general | solution.py:164
  103.0 1.3 multiply_reduce_fusion
  104.3 1.2 copy.55
  105.5 4.9 %convolution_bitcast_fusion = f32[1,1536,128]{1,2,0:T(8,128)S(1)} fusion(bf16[512,2,128]{0,2,1:T(8,128)(2,1)} %copy.43, f32[1536,512,2]{1,0,2:T(8,128)} %copy-done.1, f32[2,512]{1,0:T(2,128)S(1)} %log_add_fusion, pred[512,1536]{0,1:T(8,128)(4,1)S(1)} %fusion.8), kind=kOutput, calls=%fused_computation.23 | convolution fusion | flops 408944640 | bytes 8130560 | tf_op jit(solution)/shard_map/while/body/eval_jaxpr/kgqj,qkgd->jkd/dot_general | solution.py:203
  110.5 2.5 fusion.5
  113.0 1.4 fusion.9
  116.8 1.9 collective-permute-start.4
  118.7 2.1 collective-permute-start.5
  121.9 7.9 %collective-permute-done.4 = f32[2,512,128]{1,2,0:T(8,128)} collective-permute-done((f32[2,512,128]{1,2,0:T(8,128)}, f32[2,512,128]{1,2,0:T(8,128)}, u32[]{:S(2)}, u32[]{:S(2)}) %collective-permute-start.4) | collective-permute-done | bytes 524320 | tf_op jit(solution)/shard_map/ppermute | solution.py:18
  129.8 8.6 %collective-permute-done.5 = f32[2,512,128]{1,2,0:T(8,128)} collective-permute-done((f32[2,512,128]{1,2,0:T(8,128)S(1)}, f32[2,512,128]{1,2,0:T(8,128)}, u32[]{:S(2)}, u32[]{:S(2)}) %collective-permute-start.5) | collective-permute-done | bytes 524320 | tf_op jit(solution)/shard_map/ppermute | solution.py:18
  138.4 1.4 fusion.14
  140.7 7.8 %fusion = bf16[5376,512]{0,1:T(8,128)(2,1)} fusion(bf16[512,5376]{1,0:T(8,128)(2,1)} %bitcast.4, bf16[512,128]{0,1:T(8,128)(2,1)S(1)} %fusion.35, bf16[512,128]{0,1:T(8,128)(2,1)S(1)} %fusion.36, bf16[512,256]{0,1:T(8,128)(2,1)S(1)} %bitcast.159), kind=kOutput, calls=%fused_computation.6 | convolution fusion | flops 2825650176 | bytes 11534336 | tf_op jit(solution)/shard_map/dot_general | solution.py:293
  148.5 8.3 %copy.44 = bf16[5376,512]{1,0:T(8,128)(2,1)} copy(bf16[5376,512]{0,1:T(8,128)(2,1)} %fusion) | data formatting | bytes 11010048 | tf_op jit(solution)/shard_map/convert_element_type | solution.py:295
  156.7 3.5 %dynamic-slice_bitcast_fusion.2 = bf16[8,2,168,512]{3,2,1,0:T(8,128)(2,1)} fusion(bf16[8,2,2,168,512]{4,3,2,1,0:T(8,128)(2,1)} %bitcast.154, s32[]{:T(128)S(6)} %select_n.119), kind=kLoop, calls=%fused_computation.22 | loop fusion | bytes 5505028 | tf_op jit(solution)/shard_map/jit(dynamic_index_in_dim)/squeeze | solution.py:89
  160.3 7.5 %convolution_convert_fusion = bf16[512,5376]{1,0:T(8,128)(2,1)} fusion(bf16[5376,512]{1,0:T(8,128)(2,1)} %constant_dynamic-update-slice_fusion, bf16[512,128]{0,1:T(8,128)(2,1)S(1)} %fusion.35, bf16[512,128]{0,1:T(8,128)(2,1)S(1)} %fusion.36, bf16[512,256]{0,1:T(8,128)(2,1)S(1)} %bitcast.160), kind=kOutput, calls=%fused_computation.5 | convolution fusion | flops 2822897664 | bytes 11534336 | tf_op jit(solution)/shard_map/dot_general | solution.py:304
  167.7 4.8 %all-to-all-start.1 = ((bf16[8,64,5376]{2,1,0:T(8,128)(2,1)}), bf16[8,64,5376]{2,1,0:T(8,128)(2,1)}, u32[]{:S(2)}, u32[]{:S(2)}) async-start(bf16[8,64,5376]{2,1,0:T(8,128)(2,1)} %bitcast.156), calls=%async_computation.1 | async-start | bytes 11010048 | tf_op jit(solution)/shard_map/all_to_all | solution.py:113
  172.5 2.6 %convert_add_fusion = f32[8,2,168,512]{3,2,1,0:T(8,128)S(1)} fusion(bf16[8,2,168,512]{3,2,1,0:T(8,128)(2,1)S(1)} %collective-permute-done.6, bf16[8,2,2,168,512]{4,3,2,1,0:T(8,128)(2,1)} %bitcast.155, s32[]{:T(128)S(6)} %select_n.118), kind=kLoop, calls=%fused_computation.14 | loop fusion | flops 4128768 | bytes 11010052 | tf_op jit(solution)/shard_map/add | solution.py:90
  175.3 2.3 copy-done
  177.5 54.3 %while.11 = (s32[]{:T(128)}, f32[2,168,256]{2,1,0:T(8,128)S(1)}, f32[2,168,256]{2,1,0:T(8,128)S(1)}, s32[]{:T(128)}, f32[8,2,168,512]{3,2,1,0:T(8,128)}, /*index...) while((s32[]{:T(128)}, f32[2,168,256]{2,1,0:T(8,128)S(1)}, ...), condition=%wide.region_8.9_spmd, body=%wide.region_7.8_spmd.sunk | while | flops 516130 | bytes 6881811 | solution.py:79
  177.6 3.5 %collective-permute-start = (bf16[2,168,256]{2,1,0:T(8,128)(2,1)S(1)}, bf16[2,168,256]{2,1,0:T(8,128)(2,1)S(1)}, u32[]{:S(2)}, u32[]{:S(2)}) collective-permute-start(bf16[2,168,256]{2,1,0:T(8,128)(2,1)S(1)} %convert_element_type.193), channel_id=1, source_target_pairs={{0,32},{8,40},{16,48},{24,56},{32,64},{40,72},{48,80},{56,88},{64,... | collective-permute-start | bytes 516104 | tf_op jit(solution)/shard_map/while/body/eval_jaxpr/ppermute | solution.py:75
  181.2 1.4 dynamic-slice_bitcast_fusion.6
  182.6 2.4 collective-permute-done
  185.1 3.5 %collective-permute-done.1 = bf16[2,168,256]{2,1,0:T(8,128)(2,1)S(1)} collective-permute-done((bf16[2,168,256]{2,1,0:T(8,128)(2,1)S(1)}, bf16[2,168,256]{2,1,0:T(8,128)(2,1)S(1)}, u32[]{:S(2)}, u32[]{:S(2)}) %collective-permute-start.1) | collective-permute-done | bytes 172064 | tf_op jit(solution)/shard_map/while/body/eval_jaxpr/ppermute | solution.py:76
  189.0 1.9 collective-permute-start.1
  190.9 1.4 dynamic-slice_bitcast_fusion.6
  192.3 1.9 collective-permute-done
  194.3 1.5 collective-permute-done.1
  196.2 1.9 collective-permute-start.1
  198.1 1.4 dynamic-slice_bitcast_fusion.6
  199.5 1.9 collective-permute-done
  201.4 1.5 collective-permute-done.1
  203.1 2.1 collective-permute-start.1
  205.2 1.4 dynamic-slice_bitcast_fusion.6
  206.6 1.9 collective-permute-done
  208.5 1.3 collective-permute-done.1
  210.0 2.1 collective-permute-start.1
  212.1 1.4 dynamic-slice_bitcast_fusion.6
  213.5 1.9 collective-permute-done
  215.4 1.3 collective-permute-done.1
  216.9 2.1 collective-permute-start.1
  219.0 1.4 dynamic-slice_bitcast_fusion.6
  220.4 2.3 collective-permute-done
  222.8 1.3 collective-permute-done.1
  225.1 1.3 collective-permute-start.1
  226.4 1.5 dynamic-slice_bitcast_fusion.6
  227.9 1.8 collective-permute-done
  229.7 2.1 collective-permute-done.1
  232.0 2.8 %collective-permute-start.7 = (bf16[168,512]{1,0:T(8,128)(2,1)S(1)}, bf16[168,512]{1,0:T(8,128)(2,1)S(1)}, u32[]{:S(2)}, u32[]{:S(2)}) collective-permute-start(bf16[168,512]{1,0:T(8,128)(2,1)S(1)} %fusion.27), channel_id=1, source_target_pairs={{0,16},{8,24},{16,0},{24,8},{32,48},{40,56},{48,32},{56,40},{64,80... | collective-permute-start | bytes 516104 | tf_op jit(solution)/shard_map/ppermute | solution.py:90
  235.6 5.8 %collective-permute-done.7 = bf16[168,512]{1,0:T(8,128)(2,1)S(1)} collective-permute-done((bf16[168,512]{1,0:T(8,128)(2,1)S(1)}, bf16[168,512]{1,0:T(8,128)(2,1)S(1)}, u32[]{:S(2)}, u32[]{:S(2)}) %collective-permute-start.7) | collective-permute-done | bytes 172064 | tf_op jit(solution)/shard_map/ppermute | solution.py:90
  242.8 4.4 %reduce_sum.71 = bf16[64,5376]{1,0:T(8,128)(2,1)} reduce(bf16[8,64,5376]{2,1,0:T(8,128)(2,1)} %all-to-all-done.1, bf16[]{:T(256)} %constant.224.clone.1), dimensions={0}, to_apply=%region_6.7 | reduce | flops 2408448 | bytes 6193154 | tf_op jit(solution)/shard_map/reduce_sum | solution.py:114
  (128 shorter events, 15.2 us)
Async XLA Ops:
  4.5 7.1 %copy-start.14 = (bf16[512,256]{1,0:T(8,128)(2,1)S(1)}, bf16[512,256]{1,0:T(8,128)(2,1)}, u32[]{:S(2)}) copy-start(bf16[512,256]{1,0:T(8,128)(2,1)} %param.15) | copy-start | bytes 786436
  4.5 70.1 %all-to-all-start = ((bf16[8,64,5376]{2,1,0:T(8,128)(2,1)}), bf16[8,64,5376]{2,1,0:T(8,128)(2,1)}, u32[]{:S(2)}, u32[]{:S(2)}) async-start(bf16[8,64,5376]{2,1,0:T(8,128)(2,1)} %broadcast_in_dim.71), calls=%async_computation | async-start | bytes 11010048 | tf_op jit(solution)/shard_map/all_to_all | solution.py:106
  11.5 6.8 %copy-start.13 = (bf16[5376,128]{1,0:T(8,128)(2,1)S(1)}, bf16[5376,128]{1,0:T(8,128)(2,1)}, u32[]{:S(2)}) copy-start(bf16[5376,128]{1,0:T(8,128)(2,1)} %param.11) | copy-start | bytes 4128772
  13.6 74.5 %copy-start.7 = (f32[512,64]{1,0:T(8,128)}, f32[512,64]{1,0:T(8,128)S(1)}, u32[]{:S(2)}) copy-start(f32[512,64]{1,0:T(8,128)S(1)} %get-tuple-element.231) | copy-start | bytes 393220
  13.6 74.5 %copy-start.9 = (f32[512,64]{1,0:T(8,128)}, f32[512,64]{1,0:T(8,128)S(1)}, u32[]{:S(2)}) copy-start(f32[512,64]{1,0:T(8,128)S(1)} %get-tuple-element.232) | copy-start | bytes 393220
  74.6 6.9 %copy-start.17 = (f32[128]{0:T(128)S(1)}, f32[128]{0:T(128)}, u32[]{:S(2)}) copy-start(f32[128]{0:T(128)} %param.14) | copy-start | bytes 1540
  74.6 13.3 %copy-start.18 = (f32[128]{0:T(128)S(1)}, f32[128]{0:T(128)}, u32[]{:S(2)}) copy-start(f32[128]{0:T(128)} %param.13) | copy-start | bytes 1540
  81.4 6.2 %copy-start.2 = (f32[512,512]{0,1:T(8,128)}, f32[512,512]{0,1:T(8,128)S(1)}, u32[]{:S(2)}) copy-start(f32[512,512]{0,1:T(8,128)S(1)} %convolution_bitcast_fusion.2) | copy-start | bytes 3145732
  82.9 12.3 %collective-permute-start.2 = (bf16[2,512,128]{1,2,0:T(8,128)(2,1)}, bf16[2,512,128]{1,2,0:T(8,128)(2,1)}, u32[]{:S(2)}, u32[]{:S(2)}) collective-permute-start(bf16[2,512,128]{1,2,0:T(8,128)(2,1)} %pad_maximum_fusion.2), channel_id=1, source_target_pairs={{0,16},{8,24},{16,32},{24,40},{32,48},{40,56},{48,64},{56,72},{64,... | collective-permute-start | bytes 786440 | tf_op jit(solution)/shard_map/ppermute | solution.py:18
  85.4 11.0 %collective-permute-start.3 = (bf16[2,512,128]{1,2,0:T(8,128)(2,1)}, bf16[2,512,128]{1,2,0:T(8,128)(2,1)}, u32[]{:S(2)}, u32[]{:S(2)}) collective-permute-start(bf16[2,512,128]{1,2,0:T(8,128)(2,1)} %pad_maximum_fusion.2), channel_id=1, source_target_pairs={{0,8},{8,16},{16,24},{24,32},{32,40},{40,48},{48,56},{56,64},{64,7... | collective-permute-start | bytes 786440 | tf_op jit(solution)/shard_map/ppermute | solution.py:18
  88.5 8.9 %copy-start.11 = (bf16[512,2,128]{2,0,1:T(8,128)(2,1)}, bf16[512,2,128]{2,0,1:T(8,128)(2,1)S(1)}, u32[]{:S(2)}) copy-start(bf16[512,2,128]{2,0,1:T(8,128)(2,1)S(1)} %fusion.15) | copy-start | bytes 786436
  97.4 2.6 %copy-start.4 = (bf16[2,1536,128]{1,2,0:T(8,128)(2,1)}, bf16[2,1536,128]{1,2,0:T(8,128)(2,1)S(1)}, u32[]{:S(2)}) copy-start(bf16[2,1536,128]{1,2,0:T(8,128)(2,1)S(1)} %maximum_maximum_fusion) | copy-start | bytes 2359300
  98.7 4.0 %copy-start.1 = (f32[1536,512,2]{1,0,2:T(8,128)}, f32[1536,512,2]{1,0,2:T(8,128)S(1)}, u32[]{:S(2)}) copy-start(f32[1536,512,2]{1,0,2:T(8,128)S(1)} %get-tuple-element.234) | copy-start | bytes 18874372
  104.3 6.2 %slice-start = ((s8[6291456]{0:T(1024)(128)(4,1)}), s8[2097152]{0:T(1024)(128)(4,1)S(1)}, s32[]{:S(2)}) async-start(s8[6291456]{0:T(1024)(128)(4,1)} %bitcast.152), calls=%async_computation.2 | async-start | bytes 4194304
  105.5 5.0 %slice-start.1 = ((s8[6291456]{0:T(1024)(128)(4,1)}), s8[4194304]{0:T(1024)(128)(4,1)S(1)}, s32[]{:S(2)}) async-start(s8[6291456]{0:T(1024)(128)(4,1)} %bitcast.152), calls=%async_computation.3 | async-start | bytes 8388608
  105.5 5.0 %copy-start.5 = (bf16[2,1536,128]{1,2,0:T(8,128)(2,1)S(1)}, bf16[2,1536,128]{1,2,0:T(8,128)(2,1)}, u32[]{:S(2)}) copy-start(bf16[2,1536,128]{1,2,0:T(8,128)(2,1)} %copy-done.4) | copy-start | bytes 2359300
  105.5 5.0 %copy-start.16 = (bf16[512,2,128]{0,2,1:T(8,128)(2,1)S(1)}, bf16[512,2,128]{0,2,1:T(8,128)(2,1)}, u32[]{:S(2)}) copy-start(bf16[512,2,128]{0,2,1:T(8,128)(2,1)} %copy.43) | copy-start | bytes 786436
  110.5 5.4 %copy-start.6 = (f32[1,1536,128]{1,2,0:T(8,128)}, f32[1,1536,128]{1,2,0:T(8,128)S(1)}, u32[]{:S(2)}) copy-start(f32[1,1536,128]{1,2,0:T(8,128)S(1)} %convolution_bitcast_fusion) | copy-start | bytes 2359300
  110.5 3.9 %copy-start.12 = (bf16[512,2,128]{2,0,1:T(8,128)(2,1)S(1)}, bf16[512,2,128]{2,0,1:T(8,128)(2,1)}, u32[]{:S(2)}) copy-start(bf16[512,2,128]{2,0,1:T(8,128)(2,1)} %copy-done.11) | copy-start | bytes 786436
  113.0 2.6 %copy-start.8 = (f32[512,64]{1,0:T(8,128)S(1)}, f32[512,64]{1,0:T(8,128)}, u32[]{:S(2)}) copy-start(f32[512,64]{1,0:T(8,128)} %copy-done.7) | copy-start | bytes 393220
  113.0 2.6 %copy-start.10 = (f32[512,64]{1,0:T(8,128)S(1)}, f32[512,64]{1,0:T(8,128)}, u32[]{:S(2)}) copy-start(f32[512,64]{1,0:T(8,128)} %copy-done.9) | copy-start | bytes 393220
  115.9 24.6 %copy-start.3 = (f32[512,512]{0,1:T(8,128)S(1)}, f32[512,512]{0,1:T(8,128)}, u32[]{:S(2)}) copy-start(f32[512,512]{0,1:T(8,128)} %copy-done.2) | copy-start | bytes 3145732
  116.8 13.0 %collective-permute-start.4 = (f32[2,512,128]{1,2,0:T(8,128)}, f32[2,512,128]{1,2,0:T(8,128)}, u32[]{:S(2)}, u32[]{:S(2)}) collective-permute-start(f32[2,512,128]{1,2,0:T(8,128)} %get-tuple-element.219), channel_id=1, source_target_pairs={{8,0},{16,8},{24,16},{32,24},{40,32},{48,40},{56,48},{64,56},{72,6... | collective-permute-start | bytes 1572872 | tf_op jit(solution)/shard_map/ppermute | solution.py:18
  118.7 19.7 %collective-permute-start.5 = (f32[2,512,128]{1,2,0:T(8,128)S(1)}, f32[2,512,128]{1,2,0:T(8,128)}, u32[]{:S(2)}, u32[]{:S(2)}) collective-permute-start(f32[2,512,128]{1,2,0:T(8,128)S(1)} %get-tuple-element.220), channel_id=1, source_target_pairs={{16,0},{24,8},{32,16},{40,24},{48,32},{56,40},{64,48},{72,56},{80,... | collective-permute-start | bytes 1572872 | tf_op jit(solution)/shard_map/ppermute | solution.py:18
  160.3 12.2 %collective-permute-start.6 = (bf16[8,2,168,512]{3,2,1,0:T(8,128)(2,1)}, bf16[8,2,168,512]{3,2,1,0:T(8,128)(2,1)S(1)}, u32[]{:S(2)}, u32[]{:S(2)}) collective-permute-start(bf16[8,2,168,512]{3,2,1,0:T(8,128)(2,1)} %dynamic-slice_bitcast_fusion.2), channel_id=1, source_target_pairs={{0,8},{8,0},{16,24},{24,16},{32,40},{40,32},{48,56},{56,48},{64,72... | collective-permute-start | bytes 8257544 | tf_op jit(solution)/shard_map/ppermute | solution.py:90
  167.7 75.0 %all-to-all-start.1 = ((bf16[8,64,5376]{2,1,0:T(8,128)(2,1)}), bf16[8,64,5376]{2,1,0:T(8,128)(2,1)}, u32[]{:S(2)}, u32[]{:S(2)}) async-start(bf16[8,64,5376]{2,1,0:T(8,128)(2,1)} %bitcast.156), calls=%async_computation.1 | async-start | bytes 11010048 | tf_op jit(solution)/shard_map/all_to_all | solution.py:113
  175.1 2.5 copy-start
  177.5 57.2 %copy-start.15 = (bf16[128,2,512]{2,0,1:T(8,128)(2,1)S(1)}, bf16[128,2,512]{2,0,1:T(8,128)(2,1)}, u32[]{:S(2)}) copy-start(bf16[128,2,512]{2,0,1:T(8,128)(2,1)} %get-tuple-element.236) | copy-start | bytes 786436
  177.6 7.5 %collective-permute-start = (bf16[2,168,256]{2,1,0:T(8,128)(2,1)S(1)}, bf16[2,168,256]{2,1,0:T(8,128)(2,1)S(1)}, u32[]{:S(2)}, u32[]{:S(2)}) collective-permute-start(bf16[2,168,256]{2,1,0:T(8,128)(2,1)S(1)} %convert_element_type.193), channel_id=1, source_target_pairs={{0,32},{8,40},{16,48},{24,56},{32,64},{40,72},{48,80},{56,88},{64,... | collective-permute-start | bytes 516104 | tf_op jit(solution)/shard_map/while/body/eval_jaxpr/ppermute | solution.py:75
  181.1 7.5 %collective-permute-start.1 = (bf16[2,168,256]{2,1,0:T(8,128)(2,1)S(1)}, bf16[2,168,256]{2,1,0:T(8,128)(2,1)S(1)}, u32[]{:S(2)}, u32[]{:S(2)}) collective-permute-start(bf16[2,168,256]{2,1,0:T(8,128)(2,1)S(1)} %convert_element_type.194), channel_id=1, source_target_pairs={{0,224},{8,232},{16,240},{24,248},{32,0},{40,8},{48,16},{56,24},{6... | collective-permute-start | bytes 516104 | tf_op jit(solution)/shard_map/while/body/eval_jaxpr/ppermute | solution.py:76
  188.7 5.6 %collective-permute-start = (bf16[2,168,256]{2,1,0:T(8,128)(2,1)S(1)}, bf16[2,168,256]{2,1,0:T(8,128)(2,1)S(1)}, u32[]{:S(2)}, u32[]{:S(2)}) collective-permute-start(bf16[2,168,256]{2,1,0:T(8,128)(2,1)S(1)} %convert_element_type.193), channel_id=1, source_target_pairs={{0,32},{8,40},{16,48},{24,56},{32,64},{40,72},{48,80},{56,88},{64,... | collective-permute-start | bytes 516104 | tf_op jit(solution)/shard_map/while/body/eval_jaxpr/ppermute | solution.py:75
  189.0 6.8 %collective-permute-start.1 = (bf16[2,168,256]{2,1,0:T(8,128)(2,1)S(1)}, bf16[2,168,256]{2,1,0:T(8,128)(2,1)S(1)}, u32[]{:S(2)}, u32[]{:S(2)}) collective-permute-start(bf16[2,168,256]{2,1,0:T(8,128)(2,1)S(1)} %convert_element_type.194), channel_id=1, source_target_pairs={{0,224},{8,232},{16,240},{24,248},{32,0},{40,8},{48,16},{56,24},{6... | collective-permute-start | bytes 516104 | tf_op jit(solution)/shard_map/while/body/eval_jaxpr/ppermute | solution.py:76
  195.9 5.5 %collective-permute-start = (bf16[2,168,256]{2,1,0:T(8,128)(2,1)S(1)}, bf16[2,168,256]{2,1,0:T(8,128)(2,1)S(1)}, u32[]{:S(2)}, u32[]{:S(2)}) collective-permute-start(bf16[2,168,256]{2,1,0:T(8,128)(2,1)S(1)} %convert_element_type.193), channel_id=1, source_target_pairs={{0,32},{8,40},{16,48},{24,56},{32,64},{40,72},{48,80},{56,88},{64,... | collective-permute-start | bytes 516104 | tf_op jit(solution)/shard_map/while/body/eval_jaxpr/ppermute | solution.py:75
  196.2 6.7 %collective-permute-start.1 = (bf16[2,168,256]{2,1,0:T(8,128)(2,1)S(1)}, bf16[2,168,256]{2,1,0:T(8,128)(2,1)S(1)}, u32[]{:S(2)}, u32[]{:S(2)}) collective-permute-start(bf16[2,168,256]{2,1,0:T(8,128)(2,1)S(1)} %convert_element_type.194), channel_id=1, source_target_pairs={{0,224},{8,232},{16,240},{24,248},{32,0},{40,8},{48,16},{56,24},{6... | collective-permute-start | bytes 516104 | tf_op jit(solution)/shard_map/while/body/eval_jaxpr/ppermute | solution.py:76
  203.0 5.5 %collective-permute-start = (bf16[2,168,256]{2,1,0:T(8,128)(2,1)S(1)}, bf16[2,168,256]{2,1,0:T(8,128)(2,1)S(1)}, u32[]{:S(2)}, u32[]{:S(2)}) collective-permute-start(bf16[2,168,256]{2,1,0:T(8,128)(2,1)S(1)} %convert_element_type.193), channel_id=1, source_target_pairs={{0,32},{8,40},{16,48},{24,56},{32,64},{40,72},{48,80},{56,88},{64,... | collective-permute-start | bytes 516104 | tf_op jit(solution)/shard_map/while/body/eval_jaxpr/ppermute | solution.py:75
  203.1 6.7 %collective-permute-start.1 = (bf16[2,168,256]{2,1,0:T(8,128)(2,1)S(1)}, bf16[2,168,256]{2,1,0:T(8,128)(2,1)S(1)}, u32[]{:S(2)}, u32[]{:S(2)}) collective-permute-start(bf16[2,168,256]{2,1,0:T(8,128)(2,1)S(1)} %convert_element_type.194), channel_id=1, source_target_pairs={{0,224},{8,232},{16,240},{24,248},{32,0},{40,8},{48,16},{56,24},{6... | collective-permute-start | bytes 516104 | tf_op jit(solution)/shard_map/while/body/eval_jaxpr/ppermute | solution.py:76
  209.9 5.5 %collective-permute-start = (bf16[2,168,256]{2,1,0:T(8,128)(2,1)S(1)}, bf16[2,168,256]{2,1,0:T(8,128)(2,1)S(1)}, u32[]{:S(2)}, u32[]{:S(2)}) collective-permute-start(bf16[2,168,256]{2,1,0:T(8,128)(2,1)S(1)} %convert_element_type.193), channel_id=1, source_target_pairs={{0,32},{8,40},{16,48},{24,56},{32,64},{40,72},{48,80},{56,88},{64,... | collective-permute-start | bytes 516104 | tf_op jit(solution)/shard_map/while/body/eval_jaxpr/ppermute | solution.py:75
  210.0 6.7 %collective-permute-start.1 = (bf16[2,168,256]{2,1,0:T(8,128)(2,1)S(1)}, bf16[2,168,256]{2,1,0:T(8,128)(2,1)S(1)}, u32[]{:S(2)}, u32[]{:S(2)}) collective-permute-start(bf16[2,168,256]{2,1,0:T(8,128)(2,1)S(1)} %convert_element_type.194), channel_id=1, source_target_pairs={{0,224},{8,232},{16,240},{24,248},{32,0},{40,8},{48,16},{56,24},{6... | collective-permute-start | bytes 516104 | tf_op jit(solution)/shard_map/while/body/eval_jaxpr/ppermute | solution.py:76
  216.8 6.0 %collective-permute-start = (bf16[2,168,256]{2,1,0:T(8,128)(2,1)S(1)}, bf16[2,168,256]{2,1,0:T(8,128)(2,1)S(1)}, u32[]{:S(2)}, u32[]{:S(2)}) collective-permute-start(bf16[2,168,256]{2,1,0:T(8,128)(2,1)S(1)} %convert_element_type.193), channel_id=1, source_target_pairs={{0,32},{8,40},{16,48},{24,56},{32,64},{40,72},{48,80},{56,88},{64,... | collective-permute-start | bytes 516104 | tf_op jit(solution)/shard_map/while/body/eval_jaxpr/ppermute | solution.py:75
  216.9 7.2 %collective-permute-start.1 = (bf16[2,168,256]{2,1,0:T(8,128)(2,1)S(1)}, bf16[2,168,256]{2,1,0:T(8,128)(2,1)S(1)}, u32[]{:S(2)}, u32[]{:S(2)}) collective-permute-start(bf16[2,168,256]{2,1,0:T(8,128)(2,1)S(1)} %convert_element_type.194), channel_id=1, source_target_pairs={{0,224},{8,232},{16,240},{24,248},{32,0},{40,8},{48,16},{56,24},{6... | collective-permute-start | bytes 516104 | tf_op jit(solution)/shard_map/while/body/eval_jaxpr/ppermute | solution.py:76
  224.2 5.5 %collective-permute-start = (bf16[2,168,256]{2,1,0:T(8,128)(2,1)S(1)}, bf16[2,168,256]{2,1,0:T(8,128)(2,1)S(1)}, u32[]{:S(2)}, u32[]{:S(2)}) collective-permute-start(bf16[2,168,256]{2,1,0:T(8,128)(2,1)S(1)} %convert_element_type.193), channel_id=1, source_target_pairs={{0,32},{8,40},{16,48},{24,56},{32,64},{40,72},{48,80},{56,88},{64,... | collective-permute-start | bytes 516104 | tf_op jit(solution)/shard_map/while/body/eval_jaxpr/ppermute | solution.py:75
  225.1 6.7 %collective-permute-start.1 = (bf16[2,168,256]{2,1,0:T(8,128)(2,1)S(1)}, bf16[2,168,256]{2,1,0:T(8,128)(2,1)S(1)}, u32[]{:S(2)}, u32[]{:S(2)}) collective-permute-start(bf16[2,168,256]{2,1,0:T(8,128)(2,1)S(1)} %convert_element_type.194), channel_id=1, source_target_pairs={{0,224},{8,232},{16,240},{24,248},{32,0},{40,8},{48,16},{56,24},{6... | collective-permute-start | bytes 516104 | tf_op jit(solution)/shard_map/while/body/eval_jaxpr/ppermute | solution.py:76
  232.0 9.4 %collective-permute-start.7 = (bf16[168,512]{1,0:T(8,128)(2,1)S(1)}, bf16[168,512]{1,0:T(8,128)(2,1)S(1)}, u32[]{:S(2)}, u32[]{:S(2)}) collective-permute-start(bf16[168,512]{1,0:T(8,128)(2,1)S(1)} %fusion.27), channel_id=1, source_target_pairs={{0,16},{8,24},{16,0},{24,8},{32,48},{40,56},{48,32},{56,40},{64,80... | collective-permute-start | bytes 516104 | tf_op jit(solution)/shard_map/ppermute | solution.py:90
where the time goes:
time: 249 us; the launch traced here: 247 us
  waiting for transfers between devices  109 us (44%)
  local copies, waits for them, and re-layouts  40.6 us (16%)
  starting transfers between devices  39.9 us (16%)
  matrix products  35.9 us (14%)
  other arithmetic  20.2 us (8%)
    all_to_all x1, waiting for transfers between devices, gather_all(): received = lax.all_to_all(copies, axis, 0, 0)  52.4 us
    ppermute x4, waiting for transfers between devices, passed_along(): return lax.ppermute(block, axis, route)  24.3 us
    ppermute x7, waiting for transfers between devices, advance(): lax.ppermute(up.astype(jnp.bfloat16), axis, route(1)).astype(jnp.float32)  14.1 us
    ppermute x7, waiting for transfers between devices, advance(): lax.ppermute(down.astype(jnp.bfloat16), axis, route(-1)).astype(jnp.float32)  12.4 us
    ppermute x7, starting transfers between devices, advance(): lax.ppermute(down.astype(jnp.bfloat16), axis, route(-1)).astype(jnp.float32)  11.3 us
    squeeze x8, local copies, waits for them, and re-layouts, chunk(): lax.dynamic_index_in_dim(blocks, (digit - step * (k + 1)) % count, 0, kee...  10.1 us
    ppermute x4, starting transfers between devices, passed_along(): return lax.ppermute(block, axis, route)  8.63 us
    convert_element_type x1, local copies, waits for them, and re-layouts, per_device(): summed = ctx_scatter_sum((lax.dot_general(gathered, grad_cat, contract, p...  8.28 us
  transfers between devices with their start and end apart: 22, of which 20 were waited for; matrix products, arithmetic and copies ran while one was open for 15% of the time, Pallas kernels for 0%

commit v1 on v0

--- a/solution.py
+++ b/solution.py
@@ -283,8 +283,8 @@
     for distance in range(1, reach_blocks + 1):
         lower_row = (reach_blocks - distance) * token_count
         own_pair = own_pair + passed_along(
-            pair_acc[:, lower_row : lower_row + token_count], "ctx", -distance
-        )
+            pair_acc[:, lower_row : lower_row + token_count].astype(jnp.bfloat16), "ctx", -distance
+        ).astype(jnp.float32)
     grad_key = key_back(own_pair[0])[0].astype(jnp.bfloat16)
     grad_value = own_pair[1].astype(jnp.bfloat16)
     grad_cat = jnp.concatenate([grad_query, grad_key, grad_value], axis=1)

time: 249 us -> 240 us (0.964)
  waiting for transfers between devices: 109 us -> 101 us
    ppermute x4, waiting for transfers between devices: 24.3 us -> 15.9 us  [passed_along(): return lax.ppermute(block, axis, route)]
    unnamed x47 -> x53, local copies, waits for them, and re-layouts: 8.2 us -> 8.31 us
where the time goes in v1:
time: 240 us; the launch traced here: 239 us
  waiting for transfers between devices  101 us (42%)
  local copies, waits for them, and re-layouts  41.5 us (17%)
  starting transfers between devices  39.9 us (17%)
  matrix products  35.8 us (15%)
  other arithmetic  19.2 us (8%)
    all_to_all x1, waiting for transfers between devices, gather_all(): received = lax.all_to_all(copies, axis, 0, 0)  52.4 us
    ppermute x4, waiting for transfers between devices, passed_along(): return lax.ppermute(block, axis, route)  15.9 us
    ppermute x7, waiting for transfers between devices, advance(): lax.ppermute(up.astype(jnp.bfloat16), axis, route(1)).astype(jnp.float32)  14.1 us
    ppermute x7, waiting for transfers between devices, advance(): lax.ppermute(down.astype(jnp.bfloat16), axis, route(-1)).astype(jnp.float32)  12.4 us
    ppermute x7, starting transfers between devices, advance(): lax.ppermute(down.astype(jnp.bfloat16), axis, route(-1)).astype(jnp.float32)  11.3 us
    squeeze x8, local copies, waits for them, and re-layouts, chunk(): lax.dynamic_index_in_dim(blocks, (digit - step * (k + 1)) % count, 0, kee...  10.1 us
    ppermute x4, starting transfers between devices, passed_along(): return lax.ppermute(block, axis, route)  8.63 us
    unnamed x53, local copies, waits for them, and re-layouts  8.31 us
  transfers between devices with their start and end apart: 22, of which 20 were waited for; matrix products, arithmetic and copies ran while one was open for 15% of the time, Pallas kernels for 0%

profile of v1, /device:TPU:96, one launch (start us, length us, event | category | flops | bytes accessed | tf_op | source)
XLA Modules:
  0.0 238.5 jit_solution(6004562698138631326)
XLA Ops:
  0.6 3.8 %broadcast_in_dim.71 = bf16[8,64,5376]{2,1,0:T(8,128)(2,1)} broadcast(bf16[64,5376]{1,0:T(8,128)(2,1)} %param.9), dimensions={1,2} | broadcast | bytes 6193152 | tf_op jit(solution)/shard_map/broadcast_in_dim | solution.py:105
  4.4 7.1 %all-to-all-start = ((bf16[8,64,5376]{2,1,0:T(8,128)(2,1)}), bf16[8,64,5376]{2,1,0:T(8,128)(2,1)}, u32[]{:S(2)}, u32[]{:S(2)}) async-start(bf16[8,64,5376]{2,1,0:T(8,128)(2,1)} %broadcast_in_dim.71), calls=%async_computation | async-start | bytes 11010048 | tf_op jit(solution)/shard_map/all_to_all | solution.py:106
  13.5 1.2 fusion.8
  14.8 3.5 %constant_dynamic-update-slice_fusion.2 = bf16[5376,512]{1,0:T(8,128)(2,1)} fusion(bf16[5376,256]{1,0:T(8,128)(2,1)} %param.10), kind=kLoop, calls=%fused_computation.95 | loop fusion | bytes 5505024
  18.3 1.3 constant_dynamic-update-slice_fusion.1
  19.6 2.6 %constant_dynamic-update-slice_fusion = bf16[5376,512]{1,0:T(8,128)(2,1)} fusion(bf16[5376,512]{1,0:T(8,128)(2,1)} %constant_dynamic-update-slice_fusion.1, bf16[5376,128]{1,0:T(8,128)(2,1)} %param.12), kind=kLoop, calls=%fused_computation.93 | loop fusion | bytes 2752512 | tf_op jit(solution)/shard_map/concatenate | solution.py:223
  22.2 52.4 %all-to-all-done = bf16[8,64,5376]{2,1,0:T(8,128)(2,1)} async-done(((bf16[8,64,5376]{2,1,0:T(8,128)(2,1)}), bf16[8,64,5376]{2,1,0:T(8,128)(2,1)}, u32[]{:S(2)}, u32[]{:S(2)}) %all-to-all-start) | async-done | bytes 5505056 | tf_op jit(solution)/shard_map/all_to_all | solution.py:106
  74.5 6.8 %convolution_bitcast_fusion.2 = f32[512,512]{0,1:T(8,128)S(1)} fusion(bf16[5376,512]{1,0:T(8,128)(2,1)} %constant_dynamic-update-slice_fusion, bf16[512,5376]{1,0:T(8,128)(2,1)} %bitcast.4), kind=kOutput, calls=%fused_computation.29 | convolution fusion | flops 2818572288 | bytes 12058624 | tf_op jit(solution)/shard_map/dot_general | solution.py:224
  82.9 2.5 %collective-permute-start.2 = (bf16[2,512,128]{1,2,0:T(8,128)(2,1)}, bf16[2,512,128]{1,2,0:T(8,128)(2,1)}, u32[]{:S(2)}, u32[]{:S(2)}) collective-permute-start(bf16[2,512,128]{1,2,0:T(8,128)(2,1)} %pad_maximum_fusion.2), channel_id=1, source_target_pairs={{0,16},{8,24},{16,32},{24,40},{32,48},{40,56},{48,64},{56,72},{64,... | collective-permute-start | bytes 786440 | tf_op jit(solution)/shard_map/ppermute | solution.py:18
  85.3 2.1 collective-permute-start.3
  88.5 6.6 %collective-permute-done.2 = bf16[2,512,128]{1,2,0:T(8,128)(2,1)} collective-permute-done((bf16[2,512,128]{1,2,0:T(8,128)(2,1)}, bf16[2,512,128]{1,2,0:T(8,128)(2,1)}, u32[]{:S(2)}, u32[]{:S(2)}) %collective-permute-start.2) | collective-permute-done | bytes 262176 | tf_op jit(solution)/shard_map/ppermute | solution.py:18
  95.1 1.2 collective-permute-done.3
  97.4 1.2 fusion.3
  98.7 1.3 exponential_reduce_fusion
  100.0 2.7 %bitcast_convert_fusion = (f32[2,512,128]{1,2,0:T(8,128)S(1)}, bf16[128,2,512]{2,0,1:T(8,128)(2,1)}) fusion(f32[1536,512,2]{1,0,2:T(8,128)S(1)} %get-tuple-element.234, f32[2,512]{1,0:T(2,128)S(1)} %log_add_fusion, pred[512,1536]{0,1:T(8,128)(4,1)S(1)} %fusion.8, bf16[2,1536,128]{1,2,0:T(8,128)(2,1)S(1)} %maximum_maximum_fusion), kind=kOutput, calls=%fused_computation.68 | convolution fusion | flops 409206784 | bytes 8261632 | tf_op jit(solution)/shard_map/while/body/eval_jaxpr/kgqj,jkd->qkgd/dot_general | solution.py:164
  102.9 1.3 multiply_reduce_fusion
  104.3 1.2 copy.55
  105.5 4.9 %convolution_bitcast_fusion = f32[1,1536,128]{1,2,0:T(8,128)S(1)} fusion(bf16[512,2,128]{0,2,1:T(8,128)(2,1)} %copy.43, f32[1536,512,2]{1,0,2:T(8,128)} %copy-done.1, f32[2,512]{1,0:T(2,128)S(1)} %log_add_fusion, pred[512,1536]{0,1:T(8,128)(4,1)S(1)} %fusion.8), kind=kOutput, calls=%fused_computation.23 | convolution fusion | flops 408944640 | bytes 8130560 | tf_op jit(solution)/shard_map/while/body/eval_jaxpr/kgqj,qkgd->jkd/dot_general | solution.py:203
  110.5 2.5 %fusion.5 = bf16[2,512,1536]{1,2,0:T(8,128)(2,1)S(1)} fusion(bf16[512,2,128]{0,2,1:T(8,128)(2,1)S(1)} %copy-done.19, f32[1536,512,2]{1,0,2:T(8,128)S(1)} %bitcast.153, f32[2,512]{1,0:T(2,128)S(1)} %copy.55, f32[2,512]{1,0:T(2,128)S(1)} %log_add_fusion, pred[512,1536]{0,1:T(8,128)(4,1)S(1)} %fusion.8, bf16[2,1536,128]{1,2,0:T(8,128)(2,1)S(1)} %copy-done.5), kind=kOutput, calls=%fused_computation.18 | convolution fusion | flops 412090368 | bytes 10887168 | tf_op jit(solution)/shard_map/while/body/eval_jaxpr/qkgd,jkd->kgqj/dot_general | solution.py:193
  113.0 1.4 fusion.10
  114.4 1.2 convolution_bitcast_fusion.1
  116.8 1.9 collective-permute-start.4
  118.8 2.1 collective-permute-start.5
  122.0 2.1 collective-permute-done.4
  124.0 6.0 %collective-permute-done.5 = bf16[2,512,128]{1,2,0:T(8,128)(2,1)} collective-permute-done((bf16[2,512,128]{1,2,0:T(8,128)(2,1)}, bf16[2,512,128]{1,2,0:T(8,128)(2,1)}, u32[]{:S(2)}, u32[]{:S(2)}) %collective-permute-start.5) | collective-permute-done | bytes 262176 | tf_op jit(solution)/shard_map/ppermute | solution.py:18
  132.1 7.7 %fusion = bf16[5376,512]{0,1:T(8,128)(2,1)} fusion(bf16[512,5376]{1,0:T(8,128)(2,1)} %bitcast.4, bf16[512,128]{0,1:T(8,128)(2,1)S(1)} %fusion.35, bf16[512,128]{0,1:T(8,128)(2,1)S(1)} %fusion.36, bf16[512,256]{0,1:T(8,128)(2,1)S(1)} %bitcast.159), kind=kOutput, calls=%fused_computation.6 | convolution fusion | flops 2825650176 | bytes 11534336 | tf_op jit(solution)/shard_map/dot_general | solution.py:293
  139.8 8.3 %copy.44 = bf16[5376,512]{1,0:T(8,128)(2,1)} copy(bf16[5376,512]{0,1:T(8,128)(2,1)} %fusion) | data formatting | bytes 11010048 | tf_op jit(solution)/shard_map/convert_element_type | solution.py:295
  148.1 3.6 %dynamic-slice_bitcast_fusion.2 = bf16[8,2,168,512]{3,2,1,0:T(8,128)(2,1)} fusion(bf16[8,2,2,168,512]{4,3,2,1,0:T(8,128)(2,1)} %bitcast.154, s32[]{:T(128)S(6)} %select_n.119), kind=kLoop, calls=%fused_computation.22 | loop fusion | bytes 5505028 | tf_op jit(solution)/shard_map/jit(dynamic_index_in_dim)/squeeze | solution.py:89
  151.7 7.4 %convolution_convert_fusion = bf16[512,5376]{1,0:T(8,128)(2,1)} fusion(bf16[5376,512]{1,0:T(8,128)(2,1)} %constant_dynamic-update-slice_fusion, bf16[512,128]{0,1:T(8,128)(2,1)S(1)} %fusion.35, bf16[512,128]{0,1:T(8,128)(2,1)S(1)} %fusion.36, bf16[512,256]{0,1:T(8,128)(2,1)S(1)} %bitcast.160), kind=kOutput, calls=%fused_computation.5 | convolution fusion | flops 2822897664 | bytes 11534336 | tf_op jit(solution)/shard_map/dot_general | solution.py:304
  159.1 5.1 %all-to-all-start.1 = ((bf16[8,64,5376]{2,1,0:T(8,128)(2,1)}), bf16[8,64,5376]{2,1,0:T(8,128)(2,1)}, u32[]{:S(2)}, u32[]{:S(2)}) async-start(bf16[8,64,5376]{2,1,0:T(8,128)(2,1)} %bitcast.156), calls=%async_computation.1 | async-start | bytes 11010048 | tf_op jit(solution)/shard_map/all_to_all | solution.py:113
  164.2 2.6 %convert_add_fusion = f32[8,2,168,512]{3,2,1,0:T(8,128)S(1)} fusion(bf16[8,2,168,512]{3,2,1,0:T(8,128)(2,1)S(1)} %collective-permute-done.6, bf16[8,2,2,168,512]{4,3,2,1,0:T(8,128)(2,1)} %bitcast.155, s32[]{:T(128)S(6)} %select_n.118), kind=kLoop, calls=%fused_computation.14 | loop fusion | flops 4128768 | bytes 11010052 | tf_op jit(solution)/shard_map/add | solution.py:90
  167.0 2.3 copy-done
  169.3 55.2 %while.11 = (s32[]{:T(128)}, f32[2,168,256]{2,1,0:T(8,128)S(1)}, f32[2,168,256]{2,1,0:T(8,128)S(1)}, s32[]{:T(128)}, f32[8,2,168,512]{3,2,1,0:T(8,128)}, /*index...) while((s32[]{:T(128)}, f32[2,168,256]{2,1,0:T(8,128)S(1)}, ...), condition=%wide.region_8.9_spmd, body=%wide.region_7.8_spmd.sunk | while | flops 516130 | bytes 6881811 | solution.py:79
  169.3 4.4 %collective-permute-start = (bf16[2,168,256]{2,1,0:T(8,128)(2,1)S(1)}, bf16[2,168,256]{2,1,0:T(8,128)(2,1)S(1)}, u32[]{:S(2)}, u32[]{:S(2)}) collective-permute-start(bf16[2,168,256]{2,1,0:T(8,128)(2,1)S(1)} %convert_element_type.205), channel_id=1, source_target_pairs={{0,32},{8,40},{16,48},{24,56},{32,64},{40,72},{48,80},{56,88},{64,... | collective-permute-start | bytes 516104 | tf_op jit(solution)/shard_map/while/body/eval_jaxpr/ppermute | solution.py:75
  173.9 1.4 dynamic-slice_bitcast_fusion.6
  175.3 2.4 %collective-permute-done = bf16[2,168,256]{2,1,0:T(8,128)(2,1)S(1)} collective-permute-done((bf16[2,168,256]{2,1,0:T(8,128)(2,1)S(1)}, bf16[2,168,256]{2,1,0:T(8,128)(2,1)S(1)}, u32[]{:S(2)}, u32[]{:S(2)}) %collective-permute-start) | collective-permute-done | bytes 172064 | tf_op jit(solution)/shard_map/while/body/eval_jaxpr/ppermute | solution.py:75
  177.8 3.5 %collective-permute-done.1 = bf16[2,168,256]{2,1,0:T(8,128)(2,1)S(1)} collective-permute-done((bf16[2,168,256]{2,1,0:T(8,128)(2,1)S(1)}, bf16[2,168,256]{2,1,0:T(8,128)(2,1)S(1)}, u32[]{:S(2)}, u32[]{:S(2)}) %collective-permute-start.1) | collective-permute-done | bytes 172064 | tf_op jit(solution)/shard_map/while/body/eval_jaxpr/ppermute | solution.py:76
  181.6 1.9 collective-permute-start.1
  183.5 1.4 dynamic-slice_bitcast_fusion.6
  184.9 1.9 collective-permute-done
  186.9 1.5 collective-permute-done.1
  188.8 1.9 collective-permute-start.1
  190.7 1.4 dynamic-slice_bitcast_fusion.6
  192.1 1.9 collective-permute-done
  194.0 1.5 collective-permute-done.1
  195.7 2.1 collective-permute-start.1
  197.8 1.4 dynamic-slice_bitcast_fusion.6
  199.2 1.9 collective-permute-done
  201.1 1.3 collective-permute-done.1
  202.6 2.1 collective-permute-start.1
  204.7 1.4 dynamic-slice_bitcast_fusion.6
  206.1 1.9 collective-permute-done
  208.0 1.3 collective-permute-done.1
  209.5 2.1 collective-permute-start.1
  211.6 1.4 dynamic-slice_bitcast_fusion.6
  213.0 2.4 collective-permute-done
  215.4 1.3 collective-permute-done.1
  217.7 1.3 collective-permute-start.1
  219.0 1.5 dynamic-slice_bitcast_fusion.6
  220.5 1.8 collective-permute-done
  222.3 2.1 collective-permute-done.1
  224.6 1.6 collective-permute-start.7
  227.0 5.7 %collective-permute-done.7 = bf16[168,512]{1,0:T(8,128)(2,1)S(1)} collective-permute-done((bf16[168,512]{1,0:T(8,128)(2,1)S(1)}, bf16[168,512]{1,0:T(8,128)(2,1)S(1)}, u32[]{:S(2)}, u32[]{:S(2)}) %collective-permute-start.7) | collective-permute-done | bytes 172064 | tf_op jit(solution)/shard_map/ppermute | solution.py:90
  234.2 4.4 %reduce_sum.71 = bf16[64,5376]{1,0:T(8,128)(2,1)} reduce(bf16[8,64,5376]{2,1,0:T(8,128)(2,1)} %all-to-all-done.1, bf16[]{:T(256)} %constant.224.clone.1), dimensions={0}, to_apply=%region_6.7 | reduce | flops 2408448 | bytes 6193154 | tf_op jit(solution)/shard_map/reduce_sum | solution.py:114
  (135 shorter events, 15.3 us)
Async XLA Ops:
  4.4 7.1 %copy-start.15 = (bf16[512,256]{1,0:T(8,128)(2,1)S(1)}, bf16[512,256]{1,0:T(8,128)(2,1)}, u32[]{:S(2)}) copy-start(bf16[512,256]{1,0:T(8,128)(2,1)} %param.15) | copy-start | bytes 786436
  4.4 70.1 %all-to-all-start = ((bf16[8,64,5376]{2,1,0:T(8,128)(2,1)}), bf16[8,64,5376]{2,1,0:T(8,128)(2,1)}, u32[]{:S(2)}, u32[]{:S(2)}) async-start(bf16[8,64,5376]{2,1,0:T(8,128)(2,1)} %broadcast_in_dim.71), calls=%async_computation | async-start | bytes 11010048 | tf_op jit(solution)/shard_map/all_to_all | solution.py:106
  11.5 6.8 %copy-start.14 = (bf16[5376,128]{1,0:T(8,128)(2,1)S(1)}, bf16[5376,128]{1,0:T(8,128)(2,1)}, u32[]{:S(2)}) copy-start(bf16[5376,128]{1,0:T(8,128)(2,1)} %param.11) | copy-start | bytes 4128772
  13.5 74.5 %copy-start.8 = (f32[512,64]{1,0:T(8,128)}, f32[512,64]{1,0:T(8,128)S(1)}, u32[]{:S(2)}) copy-start(f32[512,64]{1,0:T(8,128)S(1)} %get-tuple-element.231) | copy-start | bytes 393220
  13.5 74.5 %copy-start.10 = (f32[512,64]{1,0:T(8,128)}, f32[512,64]{1,0:T(8,128)S(1)}, u32[]{:S(2)}) copy-start(f32[512,64]{1,0:T(8,128)S(1)} %get-tuple-element.232) | copy-start | bytes 393220
  74.5 6.9 %copy-start.20 = (f32[128]{0:T(128)S(1)}, f32[128]{0:T(128)}, u32[]{:S(2)}) copy-start(f32[128]{0:T(128)} %param.14) | copy-start | bytes 1540
  74.5 13.3 %copy-start.21 = (f32[128]{0:T(128)S(1)}, f32[128]{0:T(128)}, u32[]{:S(2)}) copy-start(f32[128]{0:T(128)} %param.13) | copy-start | bytes 1540
  81.4 6.2 %copy-start.2 = (f32[512,512]{0,1:T(8,128)}, f32[512,512]{0,1:T(8,128)S(1)}, u32[]{:S(2)}) copy-start(f32[512,512]{0,1:T(8,128)S(1)} %convolution_bitcast_fusion.2) | copy-start | bytes 3145732
  82.9 12.3 %collective-permute-start.2 = (bf16[2,512,128]{1,2,0:T(8,128)(2,1)}, bf16[2,512,128]{1,2,0:T(8,128)(2,1)}, u32[]{:S(2)}, u32[]{:S(2)}) collective-permute-start(bf16[2,512,128]{1,2,0:T(8,128)(2,1)} %pad_maximum_fusion.2), channel_id=1, source_target_pairs={{0,16},{8,24},{16,32},{24,40},{32,48},{40,56},{48,64},{56,72},{64,... | collective-permute-start | bytes 786440 | tf_op jit(solution)/shard_map/ppermute | solution.py:18
  85.3 11.0 %collective-permute-start.3 = (bf16[2,512,128]{1,2,0:T(8,128)(2,1)}, bf16[2,512,128]{1,2,0:T(8,128)(2,1)}, u32[]{:S(2)}, u32[]{:S(2)}) collective-permute-start(bf16[2,512,128]{1,2,0:T(8,128)(2,1)} %pad_maximum_fusion.2), channel_id=1, source_target_pairs={{0,8},{8,16},{16,24},{24,32},{32,40},{40,48},{48,56},{56,64},{64,7... | collective-permute-start | bytes 786440 | tf_op jit(solution)/shard_map/ppermute | solution.py:18
  88.5 8.9 %copy-start.12 = (bf16[512,2,128]{2,0,1:T(8,128)(2,1)}, bf16[512,2,128]{2,0,1:T(8,128)(2,1)S(1)}, u32[]{:S(2)}) copy-start(bf16[512,2,128]{2,0,1:T(8,128)(2,1)S(1)} %fusion.15) | copy-start | bytes 786436
  97.4 2.6 %copy-start.4 = (bf16[2,1536,128]{1,2,0:T(8,128)(2,1)}, bf16[2,1536,128]{1,2,0:T(8,128)(2,1)S(1)}, u32[]{:S(2)}) copy-start(bf16[2,1536,128]{1,2,0:T(8,128)(2,1)S(1)} %maximum_maximum_fusion) | copy-start | bytes 2359300
  98.6 4.0 %copy-start.1 = (f32[1536,512,2]{1,0,2:T(8,128)}, f32[1536,512,2]{1,0,2:T(8,128)S(1)}, u32[]{:S(2)}) copy-start(f32[1536,512,2]{1,0,2:T(8,128)S(1)} %get-tuple-element.234) | copy-start | bytes 18874372
  104.3 6.2 %slice-start = ((s8[6291456]{0:T(1024)(128)(4,1)}), s8[2097152]{0:T(1024)(128)(4,1)S(1)}, s32[]{:S(2)}) async-start(s8[6291456]{0:T(1024)(128)(4,1)} %bitcast.152), calls=%async_computation.2 | async-start | bytes 4194304
  105.5 5.0 %slice-start.1 = ((s8[6291456]{0:T(1024)(128)(4,1)}), s8[4194304]{0:T(1024)(128)(4,1)S(1)}, s32[]{:S(2)}) async-start(s8[6291456]{0:T(1024)(128)(4,1)} %bitcast.152), calls=%async_computation.3 | async-start | bytes 8388608
  105.5 5.0 %copy-start.5 = (bf16[2,1536,128]{1,2,0:T(8,128)(2,1)S(1)}, bf16[2,1536,128]{1,2,0:T(8,128)(2,1)}, u32[]{:S(2)}) copy-start(bf16[2,1536,128]{1,2,0:T(8,128)(2,1)} %copy-done.4) | copy-start | bytes 2359300
  105.5 5.0 %copy-start.19 = (bf16[512,2,128]{0,2,1:T(8,128)(2,1)S(1)}, bf16[512,2,128]{0,2,1:T(8,128)(2,1)}, u32[]{:S(2)}) copy-start(bf16[512,2,128]{0,2,1:T(8,128)(2,1)} %copy.43) | copy-start | bytes 786436
  110.5 5.4 %copy-start.6 = (f32[1,1536,128]{1,2,0:T(8,128)}, f32[1,1536,128]{1,2,0:T(8,128)S(1)}, u32[]{:S(2)}) copy-start(f32[1,1536,128]{1,2,0:T(8,128)S(1)} %convolution_bitcast_fusion) | copy-start | bytes 2359300
  110.5 3.9 %copy-start.13 = (bf16[512,2,128]{2,0,1:T(8,128)(2,1)S(1)}, bf16[512,2,128]{2,0,1:T(8,128)(2,1)}, u32[]{:S(2)}) copy-start(bf16[512,2,128]{2,0,1:T(8,128)(2,1)} %copy-done.12) | copy-start | bytes 786436
  113.0 2.6 %copy-start.9 = (f32[512,64]{1,0:T(8,128)S(1)}, f32[512,64]{1,0:T(8,128)}, u32[]{:S(2)}) copy-start(f32[512,64]{1,0:T(8,128)} %copy-done.8) | copy-start | bytes 393220
  113.0 2.6 %copy-start.11 = (f32[512,64]{1,0:T(8,128)S(1)}, f32[512,64]{1,0:T(8,128)}, u32[]{:S(2)}) copy-start(f32[512,64]{1,0:T(8,128)} %copy-done.10) | copy-start | bytes 393220
  115.8 16.0 %copy-start.3 = (f32[512,512]{0,1:T(8,128)S(1)}, f32[512,512]{0,1:T(8,128)}, u32[]{:S(2)}) copy-start(f32[512,512]{0,1:T(8,128)} %copy-done.2) | copy-start | bytes 3145732
  116.0 14.1 %copy-start.7 = (f32[1,1536,128]{1,2,0:T(8,128)S(1)}, f32[1,1536,128]{1,2,0:T(8,128)}, u32[]{:S(2)}) copy-start(f32[1,1536,128]{1,2,0:T(8,128)} %copy-done.6) | copy-start | bytes 2359300
  116.8 7.2 %collective-permute-start.4 = (bf16[2,512,128]{1,2,0:T(8,128)(2,1)}, bf16[2,512,128]{1,2,0:T(8,128)(2,1)}, u32[]{:S(2)}, u32[]{:S(2)}) collective-permute-start(bf16[2,512,128]{1,2,0:T(8,128)(2,1)} %get-tuple-element.223), channel_id=1, source_target_pairs={{8,0},{16,8},{24,16},{32,24},{40,32},{48,40},{56,48},{64,56},{72,6... | collective-permute-start | bytes 786440 | tf_op jit(solution)/shard_map/ppermute | solution.py:18
  118.8 11.3 %collective-permute-start.5 = (bf16[2,512,128]{1,2,0:T(8,128)(2,1)}, bf16[2,512,128]{1,2,0:T(8,128)(2,1)}, u32[]{:S(2)}, u32[]{:S(2)}) collective-permute-start(bf16[2,512,128]{1,2,0:T(8,128)(2,1)} %get-tuple-element.224), channel_id=1, source_target_pairs={{16,0},{24,8},{32,16},{40,24},{48,32},{56,40},{64,48},{72,56},{80,... | collective-permute-start | bytes 786440 | tf_op jit(solution)/shard_map/ppermute | solution.py:18
  121.9 17.9 %copy-start.17 = (bf16[512,2,128]{0,2,1:T(8,128)(2,1)}, bf16[512,2,128]{0,2,1:T(8,128)(2,1)S(1)}, u32[]{:S(2)}) copy-start(bf16[512,2,128]{0,2,1:T(8,128)(2,1)S(1)} %copy.39) | copy-start | bytes 786436
  148.1 3.6 %copy-start.18 = (bf16[512,2,128]{0,2,1:T(8,128)(2,1)S(1)}, bf16[512,2,128]{0,2,1:T(8,128)(2,1)}, u32[]{:S(2)}) copy-start(bf16[512,2,128]{0,2,1:T(8,128)(2,1)} %copy-done.17) | copy-start | bytes 786436
  151.7 12.5 %collective-permute-start.6 = (bf16[8,2,168,512]{3,2,1,0:T(8,128)(2,1)}, bf16[8,2,168,512]{3,2,1,0:T(8,128)(2,1)S(1)}, u32[]{:S(2)}, u32[]{:S(2)}) collective-permute-start(bf16[8,2,168,512]{3,2,1,0:T(8,128)(2,1)} %dynamic-slice_bitcast_fusion.2), channel_id=1, source_target_pairs={{0,8},{8,0},{16,24},{24,16},{32,40},{40,32},{48,56},{56,48},{64,72... | collective-permute-start | bytes 8257544 | tf_op jit(solution)/shard_map/ppermute | solution.py:90
  159.1 75.0 %all-to-all-start.1 = ((bf16[8,64,5376]{2,1,0:T(8,128)(2,1)}), bf16[8,64,5376]{2,1,0:T(8,128)(2,1)}, u32[]{:S(2)}, u32[]{:S(2)}) async-start(bf16[8,64,5376]{2,1,0:T(8,128)(2,1)} %bitcast.156), calls=%async_computation.1 | async-start | bytes 11010048 | tf_op jit(solution)/shard_map/all_to_all | solution.py:113
  166.8 2.5 %copy-start = (f32[8,2,168,512]{3,2,1,0:T(8,128)}, f32[8,2,168,512]{3,2,1,0:T(8,128)S(1)}, u32[]{:S(2)}) copy-start(f32[8,2,168,512]{3,2,1,0:T(8,128)S(1)} %convert_add_fusion) | copy-start | bytes 16515076
  169.3 56.9 %copy-start.16 = (bf16[128,2,512]{2,0,1:T(8,128)(2,1)S(1)}, bf16[128,2,512]{2,0,1:T(8,128)(2,1)}, u32[]{:S(2)}) copy-start(bf16[128,2,512]{2,0,1:T(8,128)(2,1)} %get-tuple-element.236) | copy-start | bytes 786436
  169.3 8.4 %collective-permute-start = (bf16[2,168,256]{2,1,0:T(8,128)(2,1)S(1)}, bf16[2,168,256]{2,1,0:T(8,128)(2,1)S(1)}, u32[]{:S(2)}, u32[]{:S(2)}) collective-permute-start(bf16[2,168,256]{2,1,0:T(8,128)(2,1)S(1)} %convert_element_type.205), channel_id=1, source_target_pairs={{0,32},{8,40},{16,48},{24,56},{32,64},{40,72},{48,80},{56,88},{64,... | collective-permute-start | bytes 516104 | tf_op jit(solution)/shard_map/while/body/eval_jaxpr/ppermute | solution.py:75
  173.7 7.5 %collective-permute-start.1 = (bf16[2,168,256]{2,1,0:T(8,128)(2,1)S(1)}, bf16[2,168,256]{2,1,0:T(8,128)(2,1)S(1)}, u32[]{:S(2)}, u32[]{:S(2)}) collective-permute-start(bf16[2,168,256]{2,1,0:T(8,128)(2,1)S(1)} %convert_element_type.206), channel_id=1, source_target_pairs={{0,224},{8,232},{16,240},{24,248},{32,0},{40,8},{48,16},{56,24},{6... | collective-permute-start | bytes 516104 | tf_op jit(solution)/shard_map/while/body/eval_jaxpr/ppermute | solution.py:76
  181.3 5.5 %collective-permute-start = (bf16[2,168,256]{2,1,0:T(8,128)(2,1)S(1)}, bf16[2,168,256]{2,1,0:T(8,128)(2,1)S(1)}, u32[]{:S(2)}, u32[]{:S(2)}) collective-permute-start(bf16[2,168,256]{2,1,0:T(8,128)(2,1)S(1)} %convert_element_type.205), channel_id=1, source_target_pairs={{0,32},{8,40},{16,48},{24,56},{32,64},{40,72},{48,80},{56,88},{64,... | collective-permute-start | bytes 516104 | tf_op jit(solution)/shard_map/while/body/eval_jaxpr/ppermute | solution.py:75
  181.6 6.7 %collective-permute-start.1 = (bf16[2,168,256]{2,1,0:T(8,128)(2,1)S(1)}, bf16[2,168,256]{2,1,0:T(8,128)(2,1)S(1)}, u32[]{:S(2)}, u32[]{:S(2)}) collective-permute-start(bf16[2,168,256]{2,1,0:T(8,128)(2,1)S(1)} %convert_element_type.206), channel_id=1, source_target_pairs={{0,224},{8,232},{16,240},{24,248},{32,0},{40,8},{48,16},{56,24},{6... | collective-permute-start | bytes 516104 | tf_op jit(solution)/shard_map/while/body/eval_jaxpr/ppermute | solution.py:76
  188.5 5.5 %collective-permute-start = (bf16[2,168,256]{2,1,0:T(8,128)(2,1)S(1)}, bf16[2,168,256]{2,1,0:T(8,128)(2,1)S(1)}, u32[]{:S(2)}, u32[]{:S(2)}) collective-permute-start(bf16[2,168,256]{2,1,0:T(8,128)(2,1)S(1)} %convert_element_type.205), channel_id=1, source_target_pairs={{0,32},{8,40},{16,48},{24,56},{32,64},{40,72},{48,80},{56,88},{64,... | collective-permute-start | bytes 516104 | tf_op jit(solution)/shard_map/while/body/eval_jaxpr/ppermute | solution.py:75
  188.8 6.7 %collective-permute-start.1 = (bf16[2,168,256]{2,1,0:T(8,128)(2,1)S(1)}, bf16[2,168,256]{2,1,0:T(8,128)(2,1)S(1)}, u32[]{:S(2)}, u32[]{:S(2)}) collective-permute-start(bf16[2,168,256]{2,1,0:T(8,128)(2,1)S(1)} %convert_element_type.206), channel_id=1, source_target_pairs={{0,224},{8,232},{16,240},{24,248},{32,0},{40,8},{48,16},{56,24},{6... | collective-permute-start | bytes 516104 | tf_op jit(solution)/shard_map/while/body/eval_jaxpr/ppermute | solution.py:76
  195.6 5.5 %collective-permute-start = (bf16[2,168,256]{2,1,0:T(8,128)(2,1)S(1)}, bf16[2,168,256]{2,1,0:T(8,128)(2,1)S(1)}, u32[]{:S(2)}, u32[]{:S(2)}) collective-permute-start(bf16[2,168,256]{2,1,0:T(8,128)(2,1)S(1)} %convert_element_type.205), channel_id=1, source_target_pairs={{0,32},{8,40},{16,48},{24,56},{32,64},{40,72},{48,80},{56,88},{64,... | collective-permute-start | bytes 516104 | tf_op jit(solution)/shard_map/while/body/eval_jaxpr/ppermute | solution.py:75
  195.7 6.7 %collective-permute-start.1 = (bf16[2,168,256]{2,1,0:T(8,128)(2,1)S(1)}, bf16[2,168,256]{2,1,0:T(8,128)(2,1)S(1)}, u32[]{:S(2)}, u32[]{:S(2)}) collective-permute-start(bf16[2,168,256]{2,1,0:T(8,128)(2,1)S(1)} %convert_element_type.206), channel_id=1, source_target_pairs={{0,224},{8,232},{16,240},{24,248},{32,0},{40,8},{48,16},{56,24},{6... | collective-permute-start | bytes 516104 | tf_op jit(solution)/shard_map/while/body/eval_jaxpr/ppermute | solution.py:76
  202.5 5.5 %collective-permute-start = (bf16[2,168,256]{2,1,0:T(8,128)(2,1)S(1)}, bf16[2,168,256]{2,1,0:T(8,128)(2,1)S(1)}, u32[]{:S(2)}, u32[]{:S(2)}) collective-permute-start(bf16[2,168,256]{2,1,0:T(8,128)(2,1)S(1)} %convert_element_type.205), channel_id=1, source_target_pairs={{0,32},{8,40},{16,48},{24,56},{32,64},{40,72},{48,80},{56,88},{64,... | collective-permute-start | bytes 516104 | tf_op jit(solution)/shard_map/while/body/eval_jaxpr/ppermute | solution.py:75
  202.6 6.7 %collective-permute-start.1 = (bf16[2,168,256]{2,1,0:T(8,128)(2,1)S(1)}, bf16[2,168,256]{2,1,0:T(8,128)(2,1)S(1)}, u32[]{:S(2)}, u32[]{:S(2)}) collective-permute-start(bf16[2,168,256]{2,1,0:T(8,128)(2,1)S(1)} %convert_element_type.206), channel_id=1, source_target_pairs={{0,224},{8,232},{16,240},{24,248},{32,0},{40,8},{48,16},{56,24},{6... | collective-permute-start | bytes 516104 | tf_op jit(solution)/shard_map/while/body/eval_jaxpr/ppermute | solution.py:76
  209.4 6.0 %collective-permute-start = (bf16[2,168,256]{2,1,0:T(8,128)(2,1)S(1)}, bf16[2,168,256]{2,1,0:T(8,128)(2,1)S(1)}, u32[]{:S(2)}, u32[]{:S(2)}) collective-permute-start(bf16[2,168,256]{2,1,0:T(8,128)(2,1)S(1)} %convert_element_type.205), channel_id=1, source_target_pairs={{0,32},{8,40},{16,48},{24,56},{32,64},{40,72},{48,80},{56,88},{64,... | collective-permute-start | bytes 516104 | tf_op jit(solution)/shard_map/while/body/eval_jaxpr/ppermute | solution.py:75
  209.5 7.2 %collective-permute-start.1 = (bf16[2,168,256]{2,1,0:T(8,128)(2,1)S(1)}, bf16[2,168,256]{2,1,0:T(8,128)(2,1)S(1)}, u32[]{:S(2)}, u32[]{:S(2)}) collective-permute-start(bf16[2,168,256]{2,1,0:T(8,128)(2,1)S(1)} %convert_element_type.206), channel_id=1, source_target_pairs={{0,224},{8,232},{16,240},{24,248},{32,0},{40,8},{48,16},{56,24},{6... | collective-permute-start | bytes 516104 | tf_op jit(solution)/shard_map/while/body/eval_jaxpr/ppermute | solution.py:76
  216.8 5.5 %collective-permute-start = (bf16[2,168,256]{2,1,0:T(8,128)(2,1)S(1)}, bf16[2,168,256]{2,1,0:T(8,128)(2,1)S(1)}, u32[]{:S(2)}, u32[]{:S(2)}) collective-permute-start(bf16[2,168,256]{2,1,0:T(8,128)(2,1)S(1)} %convert_element_type.205), channel_id=1, source_target_pairs={{0,32},{8,40},{16,48},{24,56},{32,64},{40,72},{48,80},{56,88},{64,... | collective-permute-start | bytes 516104 | tf_op jit(solution)/shard_map/while/body/eval_jaxpr/ppermute | solution.py:75
  217.7 6.7 %collective-permute-start.1 = (bf16[2,168,256]{2,1,0:T(8,128)(2,1)S(1)}, bf16[2,168,256]{2,1,0:T(8,128)(2,1)S(1)}, u32[]{:S(2)}, u32[]{:S(2)}) collective-permute-start(bf16[2,168,256]{2,1,0:T(8,128)(2,1)S(1)} %convert_element_type.206), channel_id=1, source_target_pairs={{0,224},{8,232},{16,240},{24,248},{32,0},{40,8},{48,16},{56,24},{6... | collective-permute-start | bytes 516104 | tf_op jit(solution)/shard_map/while/body/eval_jaxpr/ppermute | solution.py:76
  224.6 8.1 %collective-permute-start.7 = (bf16[168,512]{1,0:T(8,128)(2,1)S(1)}, bf16[168,512]{1,0:T(8,128)(2,1)S(1)}, u32[]{:S(2)}, u32[]{:S(2)}) collective-permute-start(bf16[168,512]{1,0:T(8,128)(2,1)S(1)} %fusion.27), channel_id=1, source_target_pairs={{0,16},{8,24},{16,0},{24,8},{32,48},{40,56},{48,32},{56,40},{64,80... | collective-permute-start | bytes 516104 | tf_op jit(solution)/shard_map/ppermute | solution.py:90

commit v2 on v1

--- a/solution.py
+++ b/solution.py
@@ -288,9 +288,15 @@
     grad_key = key_back(own_pair[0])[0].astype(jnp.bfloat16)
     grad_value = own_pair[1].astype(jnp.bfloat16)
     grad_cat = jnp.concatenate([grad_query, grad_key, grad_value], axis=1)
+    back_contract = (((1,), (1,)), ((), ()))
+    input_partial = lax.dot_general(
+        grad_cat, weight_cat, back_contract, preferred_element_type=jnp.float32
+    ).astype(jnp.bfloat16)
+    input_partial, hidden_late = lax.optimization_barrier((input_partial, gathered))
+    input_grad = exchange_sum(input_partial, "heads").astype(jnp.bfloat16)
     summed = ctx_scatter_sum(
         (
-            lax.dot_general(gathered, grad_cat, contract, preferred_element_type=jnp.float32)
+            lax.dot_general(hidden_late, grad_cat, contract, preferred_element_type=jnp.float32)
             * grad_scale
         ).astype(jnp.bfloat16),
         "ctx",
@@ -299,13 +305,6 @@
     query_weight_grad = summed[:, :query_width]
     key_weight_grad = summed[:, query_width : query_width + key_width]
     value_weight_grad = summed[:, query_width + key_width :]
-    back_contract = (((1,), (1,)), ((), ()))
-    input_grad = exchange_sum(
-        lax.dot_general(
-            grad_cat, weight_cat, back_contract, preferred_element_type=jnp.float32
-        ).astype(jnp.bfloat16),
-        "heads",
-    ).astype(jnp.bfloat16)
     return (attention, input_grad, query_weight_grad, key_weight_grad, value_weight_grad)
 
 

time: 240 us -> 231 us (0.963)
  local copies, waits for them, and re-layouts: 41.5 us -> 33.5 us
    convert_element_type x1 -> x0, local copies, waits for them, and re-layouts: 8.3 us -> none  [per_device(): summed = ctx_scatter_sum((lax.dot_general(gathered, grad_cat, contract, p...]
    unnamed x53 -> x51, local copies, waits for them, and re-layouts: 8.31 us -> 10.5 us
  transfers between devices with their start and end apart: 22 -> 22, of which waited for: 20 -> 21; matrix products, arithmetic and copies ran while one was open for 15% -> 12% of each run, Pallas kernels for 0% -> 0%
where the time goes in v2:
time: 231 us; the launch traced here: 229 us
  waiting for transfers between devices  101 us (44%)
  starting transfers between devices  40.1 us (17%)
  matrix products  34.5 us (15%)
  local copies, waits for them, and re-layouts  33.5 us (15%)
  other arithmetic  19.1 us (8%)
    all_to_all x1, waiting for transfers between devices, gather_all(): received = lax.all_to_all(copies, axis, 0, 0)  52.4 us
    ppermute x4, waiting for transfers between devices, passed_along(): return lax.ppermute(block, axis, route)  15.9 us
    ppermute x7, waiting for transfers between devices, advance(): lax.ppermute(up.astype(jnp.bfloat16), axis, route(1)).astype(jnp.float32)  14.2 us
    ppermute x7, waiting for transfers between devices, advance(): lax.ppermute(down.astype(jnp.bfloat16), axis, route(-1)).astype(jnp.float32)  12.4 us
    ppermute x7, starting transfers between devices, advance(): lax.ppermute(down.astype(jnp.bfloat16), axis, route(-1)).astype(jnp.float32)  11.3 us
    unnamed x51, local copies, waits for them, and re-layouts  10.5 us
    squeeze x8, local copies, waits for them, and re-layouts, chunk(): lax.dynamic_index_in_dim(blocks, (digit - step * (k + 1)) % count, 0, kee...  9.98 us
    ppermute x4, starting transfers between devices, passed_along(): return lax.ppermute(block, axis, route)  8.65 us
  transfers between devices with their start and end apart: 22, of which 21 were waited for; matrix products, arithmetic and copies ran while one was open for 12% of the time, Pallas kernels for 0%

profile of v2, /device:TPU:96, one launch (start us, length us, event | category | flops | bytes accessed | tf_op | source)
XLA Modules:
  0.0 229.4 jit_solution(13109898620802447427)
XLA Ops:
  0.6 3.8 %broadcast_in_dim.71 = bf16[8,64,5376]{2,1,0:T(8,128)(2,1)} broadcast(bf16[64,5376]{1,0:T(8,128)(2,1)} %param.9), dimensions={1,2} | broadcast | bytes 6193152 | tf_op jit(solution)/shard_map/broadcast_in_dim | solution.py:105
  4.5 7.1 %all-to-all-start = ((bf16[8,64,5376]{2,1,0:T(8,128)(2,1)}), bf16[8,64,5376]{2,1,0:T(8,128)(2,1)}, u32[]{:S(2)}, u32[]{:S(2)}) async-start(bf16[8,64,5376]{2,1,0:T(8,128)(2,1)} %broadcast_in_dim.71), calls=%async_computation | async-start | bytes 11010048 | tf_op jit(solution)/shard_map/all_to_all | solution.py:106
  13.6 1.2 fusion.7
  14.8 3.5 %constant_dynamic-update-slice_fusion.2 = bf16[5376,512]{1,0:T(8,128)(2,1)} fusion(bf16[5376,256]{1,0:T(8,128)(2,1)} %param.10), kind=kLoop, calls=%fused_computation.94 | loop fusion | bytes 5505024
  18.3 1.2 constant_dynamic-update-slice_fusion.1
  19.5 2.6 %constant_dynamic-update-slice_fusion = bf16[5376,512]{1,0:T(8,128)(2,1)} fusion(bf16[5376,512]{1,0:T(8,128)(2,1)} %constant_dynamic-update-slice_fusion.1, bf16[5376,128]{1,0:T(8,128)(2,1)} %param.12), kind=kLoop, calls=%fused_computation.92 | loop fusion | bytes 2752512 | tf_op jit(solution)/shard_map/concatenate | solution.py:223
  22.2 52.4 %all-to-all-done = bf16[8,64,5376]{2,1,0:T(8,128)(2,1)} async-done(((bf16[8,64,5376]{2,1,0:T(8,128)(2,1)}), bf16[8,64,5376]{2,1,0:T(8,128)(2,1)}, u32[]{:S(2)}, u32[]{:S(2)}) %all-to-all-start) | async-done | bytes 5505056 | tf_op jit(solution)/shard_map/all_to_all | solution.py:106
  74.6 6.8 %convolution_bitcast_fusion.2 = f32[512,512]{0,1:T(8,128)S(1)} fusion(bf16[5376,512]{1,0:T(8,128)(2,1)} %constant_dynamic-update-slice_fusion, bf16[512,5376]{1,0:T(8,128)(2,1)} %bitcast.4), kind=kOutput, calls=%fused_computation.28 | convolution fusion | flops 2818572288 | bytes 12058624 | tf_op jit(solution)/shard_map/dot_general | solution.py:224
  82.9 2.5 %collective-permute-start.2 = (bf16[2,512,128]{1,2,0:T(8,128)(2,1)}, bf16[2,512,128]{1,2,0:T(8,128)(2,1)}, u32[]{:S(2)}, u32[]{:S(2)}) collective-permute-start(bf16[2,512,128]{1,2,0:T(8,128)(2,1)} %pad_maximum_fusion.2), channel_id=1, source_target_pairs={{0,16},{8,24},{16,32},{24,40},{32,48},{40,56},{48,64},{56,72},{64,... | collective-permute-start | bytes 786440 | tf_op jit(solution)/shard_map/ppermute | solution.py:18
  85.4 2.1 collective-permute-start.3
  88.6 6.6 %collective-permute-done.2 = bf16[2,512,128]{1,2,0:T(8,128)(2,1)} collective-permute-done((bf16[2,512,128]{1,2,0:T(8,128)(2,1)}, bf16[2,512,128]{1,2,0:T(8,128)(2,1)}, u32[]{:S(2)}, u32[]{:S(2)}) %collective-permute-start.2) | collective-permute-done | bytes 262176 | tf_op jit(solution)/shard_map/ppermute | solution.py:18
  95.2 1.2 collective-permute-done.3
  97.4 1.2 fusion.2
  98.7 1.3 exponential_reduce_fusion
  100.0 2.7 %bitcast_convert_fusion = (f32[2,512,128]{1,2,0:T(8,128)S(1)}, bf16[128,2,512]{2,0,1:T(8,128)(2,1)}) fusion(f32[1536,512,2]{1,0,2:T(8,128)S(1)} %get-tuple-element.238, f32[2,512]{1,0:T(2,128)S(1)} %log_add_fusion, pred[512,1536]{0,1:T(8,128)(4,1)S(1)} %fusion.7, bf16[2,1536,128]{1,2,0:T(8,128)(2,1)S(1)} %maximum_maximum_fusion), kind=kOutput, calls=%fused_computation.67 | convolution fusion | flops 409206784 | bytes 8261632 | tf_op jit(solution)/shard_map/while/body/eval_jaxpr/kgqj,jkd->qkgd/dot_general | solution.py:164
  103.0 1.3 multiply_reduce_fusion
  104.3 1.2 copy.54
  105.5 4.9 %convolution_bitcast_fusion = f32[1,1536,128]{1,2,0:T(8,128)S(1)} fusion(bf16[512,2,128]{0,2,1:T(8,128)(2,1)} %copy.42, f32[1536,512,2]{1,0,2:T(8,128)} %copy-done.1, f32[2,512]{1,0:T(2,128)S(1)} %log_add_fusion, pred[512,1536]{0,1:T(8,128)(4,1)S(1)} %fusion.7), kind=kOutput, calls=%fused_computation.22 | convolution fusion | flops 408944640 | bytes 8130560 | tf_op jit(solution)/shard_map/while/body/eval_jaxpr/kgqj,qkgd->jkd/dot_general | solution.py:203
  110.5 2.4 %fusion.4 = bf16[2,512,1536]{1,2,0:T(8,128)(2,1)S(1)} fusion(bf16[512,2,128]{0,2,1:T(8,128)(2,1)S(1)} %copy-done.18, f32[1536,512,2]{1,0,2:T(8,128)S(1)} %bitcast.153, f32[2,512]{1,0:T(2,128)S(1)} %copy.54, f32[2,512]{1,0:T(2,128)S(1)} %log_add_fusion, pred[512,1536]{0,1:T(8,128)(4,1)S(1)} %fusion.7, bf16[2,1536,128]{1,2,0:T(8,128)(2,1)S(1)} %copy-done.6), kind=kOutput, calls=%fused_computation.17 | convolution fusion | flops 412090368 | bytes 10887168 | tf_op jit(solution)/shard_map/while/body/eval_jaxpr/qkgd,jkd->kgqj/dot_general | solution.py:193
  113.0 1.4 fusion.9
  114.4 1.2 convolution_bitcast_fusion.1
  116.8 1.9 collective-permute-start.4
  118.7 2.1 collective-permute-start.5
  121.9 2.1 collective-permute-done.4
  124.0 6.1 %collective-permute-done.5 = bf16[2,512,128]{1,2,0:T(8,128)(2,1)} collective-permute-done((bf16[2,512,128]{1,2,0:T(8,128)(2,1)}, bf16[2,512,128]{1,2,0:T(8,128)(2,1)}, u32[]{:S(2)}, u32[]{:S(2)}) %collective-permute-start.5) | collective-permute-done | bytes 262176 | tf_op jit(solution)/shard_map/ppermute | solution.py:18
  132.1 7.5 %convolution_convert_fusion = bf16[512,5376]{1,0:T(8,128)(2,1)} fusion(bf16[5376,512]{1,0:T(8,128)(2,1)} %constant_dynamic-update-slice_fusion, bf16[512,128]{0,1:T(8,128)(2,1)S(1)} %fusion.34, bf16[512,128]{0,1:T(8,128)(2,1)S(1)} %fusion.35, bf16[512,256]{0,1:T(8,128)(2,1)S(1)} %bitcast.159), kind=kOutput, calls=%fused_computation.5 | convolution fusion | flops 2822897664 | bytes 11534336 | tf_op jit(solution)/shard_map/dot_general | solution.py:292
  139.6 6.4 %multiply_convert_fusion = bf16[5376,512]{1,0:T(8,128)(2,1)S(1)} fusion(bf16[512,5376]{1,0:T(8,128)(2,1)} %bitcast.4, bf16[512,128]{0,1:T(8,128)(2,1)S(1)} %fusion.34, bf16[512,128]{0,1:T(8,128)(2,1)S(1)} %fusion.35, bf16[512,256]{0,1:T(8,128)(2,1)S(1)} %bitcast.160), kind=kOutput, calls=%fused_computation.4 | convolution fusion | flops 2825650176 | bytes 11534336 | tf_op jit(solution)/shard_map/dot_general | solution.py:299
  145.9 2.4 %copy-done.2 = bf16[5376,512]{1,0:T(8,128)(2,1)} copy-done((bf16[5376,512]{1,0:T(8,128)(2,1)}, bf16[5376,512]{1,0:T(8,128)(2,1)S(1)}, u32[]{:S(2)}) %copy-start.2) | copy-done | bytes 5505048
  148.3 1.7 dynamic-slice_bitcast_fusion.2
  150.0 5.0 %all-to-all-start.1 = ((bf16[8,64,5376]{2,1,0:T(8,128)(2,1)}), bf16[8,64,5376]{2,1,0:T(8,128)(2,1)}, u32[]{:S(2)}, u32[]{:S(2)}) async-start(bf16[8,64,5376]{2,1,0:T(8,128)(2,1)} %bitcast.154), calls=%async_computation.1 | async-start | bytes 11010048 | tf_op jit(solution)/shard_map/all_to_all | solution.py:113
  155.3 2.6 %convert_add_fusion = f32[8,2,168,512]{3,2,1,0:T(8,128)S(1)} fusion(bf16[8,2,168,512]{3,2,1,0:T(8,128)(2,1)S(1)} %collective-permute-done.6, bf16[8,2,2,168,512]{4,3,2,1,0:T(8,128)(2,1)} %bitcast.156, s32[]{:T(128)S(6)} %select_n.118), kind=kLoop, calls=%fused_computation.13 | loop fusion | flops 4128768 | bytes 11010052 | tf_op jit(solution)/shard_map/add | solution.py:90
  158.1 2.2 copy-done
  160.3 55.0 %while.11 = (s32[]{:T(128)}, f32[2,168,256]{2,1,0:T(8,128)S(1)}, f32[2,168,256]{2,1,0:T(8,128)S(1)}, s32[]{:T(128)}, f32[8,2,168,512]{3,2,1,0:T(8,128)}, /*index...) while((s32[]{:T(128)}, f32[2,168,256]{2,1,0:T(8,128)S(1)}, ...), condition=%wide.region_8.9_spmd, body=%wide.region_7.8_spmd.sunk | while | flops 516130 | bytes 6881811 | solution.py:79
  160.3 4.2 %collective-permute-start = (bf16[2,168,256]{2,1,0:T(8,128)(2,1)S(1)}, bf16[2,168,256]{2,1,0:T(8,128)(2,1)S(1)}, u32[]{:S(2)}, u32[]{:S(2)}) collective-permute-start(bf16[2,168,256]{2,1,0:T(8,128)(2,1)S(1)} %convert_element_type.199), channel_id=1, source_target_pairs={{0,32},{8,40},{16,48},{24,56},{32,64},{40,72},{48,80},{56,88},{64,... | collective-permute-start | bytes 516104 | tf_op jit(solution)/shard_map/while/body/eval_jaxpr/ppermute | solution.py:75
  164.6 1.4 dynamic-slice_bitcast_fusion.6
  166.0 2.5 %collective-permute-done = bf16[2,168,256]{2,1,0:T(8,128)(2,1)S(1)} collective-permute-done((bf16[2,168,256]{2,1,0:T(8,128)(2,1)S(1)}, bf16[2,168,256]{2,1,0:T(8,128)(2,1)S(1)}, u32[]{:S(2)}, u32[]{:S(2)}) %collective-permute-start) | collective-permute-done | bytes 172064 | tf_op jit(solution)/shard_map/while/body/eval_jaxpr/ppermute | solution.py:75
  168.5 3.5 %collective-permute-done.1 = bf16[2,168,256]{2,1,0:T(8,128)(2,1)S(1)} collective-permute-done((bf16[2,168,256]{2,1,0:T(8,128)(2,1)S(1)}, bf16[2,168,256]{2,1,0:T(8,128)(2,1)S(1)}, u32[]{:S(2)}, u32[]{:S(2)}) %collective-permute-start.1) | collective-permute-done | bytes 172064 | tf_op jit(solution)/shard_map/while/body/eval_jaxpr/ppermute | solution.py:76
  172.4 1.9 collective-permute-start.1
  174.3 1.4 dynamic-slice_bitcast_fusion.6
  175.7 1.9 collective-permute-done
  177.7 1.5 collective-permute-done.1
  179.6 1.9 collective-permute-start.1
  181.5 1.4 dynamic-slice_bitcast_fusion.6
  182.9 1.9 collective-permute-done
  184.8 1.5 collective-permute-done.1
  186.5 2.1 collective-permute-start.1
  188.6 1.4 dynamic-slice_bitcast_fusion.6
  190.0 1.9 collective-permute-done
  192.0 1.3 collective-permute-done.1
  193.4 2.1 collective-permute-start.1
  195.5 1.4 dynamic-slice_bitcast_fusion.6
  196.9 1.9 collective-permute-done
  198.8 1.3 collective-permute-done.1
  200.3 2.1 collective-permute-start.1
  202.4 1.4 dynamic-slice_bitcast_fusion.6
  203.8 2.3 %collective-permute-done = bf16[2,168,256]{2,1,0:T(8,128)(2,1)S(1)} collective-permute-done((bf16[2,168,256]{2,1,0:T(8,128)(2,1)S(1)}, bf16[2,168,256]{2,1,0:T(8,128)(2,1)S(1)}, u32[]{:S(2)}, u32[]{:S(2)}) %collective-permute-start) | collective-permute-done | bytes 172064 | tf_op jit(solution)/shard_map/while/body/eval_jaxpr/ppermute | solution.py:75
  206.2 1.3 collective-permute-done.1
  208.5 1.3 collective-permute-start.1
  209.8 1.4 dynamic-slice_bitcast_fusion.6
  211.2 1.9 collective-permute-done
  213.1 2.1 collective-permute-done.1
  215.4 2.1 collective-permute-start.7
  218.3 5.3 %collective-permute-done.7 = bf16[168,512]{1,0:T(8,128)(2,1)S(1)} collective-permute-done((bf16[168,512]{1,0:T(8,128)(2,1)S(1)}, bf16[168,512]{1,0:T(8,128)(2,1)S(1)}, u32[]{:S(2)}, u32[]{:S(2)}) %collective-permute-start.7) | collective-permute-done | bytes 172064 | tf_op jit(solution)/shard_map/ppermute | solution.py:90
  225.1 4.4 %reduce_sum.71 = bf16[64,5376]{1,0:T(8,128)(2,1)} reduce(bf16[8,64,5376]{2,1,0:T(8,128)(2,1)} %all-to-all-done.1, bf16[]{:T(256)} %constant.224.clone.1), dimensions={0}, to_apply=%region_6.7 | reduce | flops 2408448 | bytes 6193154 | tf_op jit(solution)/shard_map/reduce_sum | solution.py:114
  (132 shorter events, 15.5 us)
Async XLA Ops:
  4.5 7.1 %copy-start.16 = (bf16[512,256]{1,0:T(8,128)(2,1)S(1)}, bf16[512,256]{1,0:T(8,128)(2,1)}, u32[]{:S(2)}) copy-start(bf16[512,256]{1,0:T(8,128)(2,1)} %param.15) | copy-start | bytes 786436
  4.5 70.1 %all-to-all-start = ((bf16[8,64,5376]{2,1,0:T(8,128)(2,1)}), bf16[8,64,5376]{2,1,0:T(8,128)(2,1)}, u32[]{:S(2)}, u32[]{:S(2)}) async-start(bf16[8,64,5376]{2,1,0:T(8,128)(2,1)} %broadcast_in_dim.71), calls=%async_computation | async-start | bytes 11010048 | tf_op jit(solution)/shard_map/all_to_all | solution.py:106
  11.5 6.8 %copy-start.15 = (bf16[5376,128]{1,0:T(8,128)(2,1)S(1)}, bf16[5376,128]{1,0:T(8,128)(2,1)}, u32[]{:S(2)}) copy-start(bf16[5376,128]{1,0:T(8,128)(2,1)} %param.11) | copy-start | bytes 4128772
  13.5 74.5 %copy-start.9 = (f32[512,64]{1,0:T(8,128)}, f32[512,64]{1,0:T(8,128)S(1)}, u32[]{:S(2)}) copy-start(f32[512,64]{1,0:T(8,128)S(1)} %get-tuple-element.235) | copy-start | bytes 393220
  13.6 74.5 %copy-start.11 = (f32[512,64]{1,0:T(8,128)}, f32[512,64]{1,0:T(8,128)S(1)}, u32[]{:S(2)}) copy-start(f32[512,64]{1,0:T(8,128)S(1)} %get-tuple-element.236) | copy-start | bytes 393220
  74.6 6.9 %copy-start.19 = (f32[128]{0:T(128)S(1)}, f32[128]{0:T(128)}, u32[]{:S(2)}) copy-start(f32[128]{0:T(128)} %param.14) | copy-start | bytes 1540
  74.6 13.3 %copy-start.20 = (f32[128]{0:T(128)S(1)}, f32[128]{0:T(128)}, u32[]{:S(2)}) copy-start(f32[128]{0:T(128)} %param.13) | copy-start | bytes 1540
  81.4 6.2 %copy-start.3 = (f32[512,512]{0,1:T(8,128)}, f32[512,512]{0,1:T(8,128)S(1)}, u32[]{:S(2)}) copy-start(f32[512,512]{0,1:T(8,128)S(1)} %convolution_bitcast_fusion.2) | copy-start | bytes 3145732
  82.9 12.3 %collective-permute-start.2 = (bf16[2,512,128]{1,2,0:T(8,128)(2,1)}, bf16[2,512,128]{1,2,0:T(8,128)(2,1)}, u32[]{:S(2)}, u32[]{:S(2)}) collective-permute-start(bf16[2,512,128]{1,2,0:T(8,128)(2,1)} %pad_maximum_fusion.2), channel_id=1, source_target_pairs={{0,16},{8,24},{16,32},{24,40},{32,48},{40,56},{48,64},{56,72},{64,... | collective-permute-start | bytes 786440 | tf_op jit(solution)/shard_map/ppermute | solution.py:18
  85.4 11.0 %collective-permute-start.3 = (bf16[2,512,128]{1,2,0:T(8,128)(2,1)}, bf16[2,512,128]{1,2,0:T(8,128)(2,1)}, u32[]{:S(2)}, u32[]{:S(2)}) collective-permute-start(bf16[2,512,128]{1,2,0:T(8,128)(2,1)} %pad_maximum_fusion.2), channel_id=1, source_target_pairs={{0,8},{8,16},{16,24},{24,32},{32,40},{40,48},{48,56},{56,64},{64,7... | collective-permute-start | bytes 786440 | tf_op jit(solution)/shard_map/ppermute | solution.py:18
  88.5 8.9 %copy-start.13 = (bf16[512,2,128]{2,0,1:T(8,128)(2,1)}, bf16[512,2,128]{2,0,1:T(8,128)(2,1)S(1)}, u32[]{:S(2)}) copy-start(bf16[512,2,128]{2,0,1:T(8,128)(2,1)S(1)} %fusion.14) | copy-start | bytes 786436
  97.4 2.6 %copy-start.5 = (bf16[2,1536,128]{1,2,0:T(8,128)(2,1)}, bf16[2,1536,128]{1,2,0:T(8,128)(2,1)S(1)}, u32[]{:S(2)}) copy-start(bf16[2,1536,128]{1,2,0:T(8,128)(2,1)S(1)} %maximum_maximum_fusion) | copy-start | bytes 2359300
  98.7 4.0 %copy-start.1 = (f32[1536,512,2]{1,0,2:T(8,128)}, f32[1536,512,2]{1,0,2:T(8,128)S(1)}, u32[]{:S(2)}) copy-start(f32[1536,512,2]{1,0,2:T(8,128)S(1)} %get-tuple-element.238) | copy-start | bytes 18874372
  104.3 6.2 %slice-start = ((s8[6291456]{0:T(1024)(128)(4,1)}), s8[2097152]{0:T(1024)(128)(4,1)S(1)}, s32[]{:S(2)}) async-start(s8[6291456]{0:T(1024)(128)(4,1)} %bitcast.152), calls=%async_computation.2 | async-start | bytes 4194304
  105.5 5.0 %slice-start.1 = ((s8[6291456]{0:T(1024)(128)(4,1)}), s8[4194304]{0:T(1024)(128)(4,1)S(1)}, s32[]{:S(2)}) async-start(s8[6291456]{0:T(1024)(128)(4,1)} %bitcast.152), calls=%async_computation.3 | async-start | bytes 8388608
  105.5 5.0 %copy-start.6 = (bf16[2,1536,128]{1,2,0:T(8,128)(2,1)S(1)}, bf16[2,1536,128]{1,2,0:T(8,128)(2,1)}, u32[]{:S(2)}) copy-start(bf16[2,1536,128]{1,2,0:T(8,128)(2,1)} %copy-done.5) | copy-start | bytes 2359300
  105.5 5.0 %copy-start.18 = (bf16[512,2,128]{0,2,1:T(8,128)(2,1)S(1)}, bf16[512,2,128]{0,2,1:T(8,128)(2,1)}, u32[]{:S(2)}) copy-start(bf16[512,2,128]{0,2,1:T(8,128)(2,1)} %copy.42) | copy-start | bytes 786436
  110.5 5.3 %copy-start.7 = (f32[1,1536,128]{1,2,0:T(8,128)}, f32[1,1536,128]{1,2,0:T(8,128)S(1)}, u32[]{:S(2)}) copy-start(f32[1,1536,128]{1,2,0:T(8,128)S(1)} %convolution_bitcast_fusion) | copy-start | bytes 2359300
  110.5 3.9 %copy-start.14 = (bf16[512,2,128]{2,0,1:T(8,128)(2,1)S(1)}, bf16[512,2,128]{2,0,1:T(8,128)(2,1)}, u32[]{:S(2)}) copy-start(bf16[512,2,128]{2,0,1:T(8,128)(2,1)} %copy-done.13) | copy-start | bytes 786436
  113.0 2.6 %copy-start.10 = (f32[512,64]{1,0:T(8,128)S(1)}, f32[512,64]{1,0:T(8,128)}, u32[]{:S(2)}) copy-start(f32[512,64]{1,0:T(8,128)} %copy-done.9) | copy-start | bytes 393220
  113.0 2.6 %copy-start.12 = (f32[512,64]{1,0:T(8,128)S(1)}, f32[512,64]{1,0:T(8,128)}, u32[]{:S(2)}) copy-start(f32[512,64]{1,0:T(8,128)} %copy-done.11) | copy-start | bytes 393220
  115.8 16.0 %copy-start.4 = (f32[512,512]{0,1:T(8,128)S(1)}, f32[512,512]{0,1:T(8,128)}, u32[]{:S(2)}) copy-start(f32[512,512]{0,1:T(8,128)} %copy-done.3) | copy-start | bytes 3145732
  116.0 14.1 %copy-start.8 = (f32[1,1536,128]{1,2,0:T(8,128)S(1)}, f32[1,1536,128]{1,2,0:T(8,128)}, u32[]{:S(2)}) copy-start(f32[1,1536,128]{1,2,0:T(8,128)} %copy-done.7) | copy-start | bytes 2359300
  116.8 7.2 %collective-permute-start.4 = (bf16[2,512,128]{1,2,0:T(8,128)(2,1)}, bf16[2,512,128]{1,2,0:T(8,128)(2,1)}, u32[]{:S(2)}, u32[]{:S(2)}) collective-permute-start(bf16[2,512,128]{1,2,0:T(8,128)(2,1)} %get-tuple-element.227), channel_id=1, source_target_pairs={{8,0},{16,8},{24,16},{32,24},{40,32},{48,40},{56,48},{64,56},{72,6... | collective-permute-start | bytes 786440 | tf_op jit(solution)/shard_map/ppermute | solution.py:18
  118.7 11.3 %collective-permute-start.5 = (bf16[2,512,128]{1,2,0:T(8,128)(2,1)}, bf16[2,512,128]{1,2,0:T(8,128)(2,1)}, u32[]{:S(2)}, u32[]{:S(2)}) collective-permute-start(bf16[2,512,128]{1,2,0:T(8,128)(2,1)} %get-tuple-element.228), channel_id=1, source_target_pairs={{16,0},{24,8},{32,16},{40,24},{48,32},{56,40},{64,48},{72,56},{80,... | collective-permute-start | bytes 786440 | tf_op jit(solution)/shard_map/ppermute | solution.py:18
  145.9 2.4 %copy-start.2 = (bf16[5376,512]{1,0:T(8,128)(2,1)}, bf16[5376,512]{1,0:T(8,128)(2,1)S(1)}, u32[]{:S(2)}) copy-start(bf16[5376,512]{1,0:T(8,128)(2,1)S(1)} %multiply_convert_fusion) | copy-start | bytes 16515076
  150.0 5.3 %collective-permute-start.6 = (bf16[8,2,168,512]{3,2,1,0:T(8,128)(2,1)}, bf16[8,2,168,512]{3,2,1,0:T(8,128)(2,1)S(1)}, u32[]{:S(2)}, u32[]{:S(2)}) collective-permute-start(bf16[8,2,168,512]{3,2,1,0:T(8,128)(2,1)} %dynamic-slice_bitcast_fusion.2), channel_id=1, source_target_pairs={{0,8},{8,0},{16,24},{24,16},{32,40},{40,32},{48,56},{56,48},{64,72... | collective-permute-start | bytes 8257544 | tf_op jit(solution)/shard_map/ppermute | solution.py:90
  150.0 75.0 %all-to-all-start.1 = ((bf16[8,64,5376]{2,1,0:T(8,128)(2,1)}), bf16[8,64,5376]{2,1,0:T(8,128)(2,1)}, u32[]{:S(2)}, u32[]{:S(2)}) async-start(bf16[8,64,5376]{2,1,0:T(8,128)(2,1)} %bitcast.154), calls=%async_computation.1 | async-start | bytes 11010048 | tf_op jit(solution)/shard_map/all_to_all | solution.py:113
  157.9 2.4 %copy-start = (f32[8,2,168,512]{3,2,1,0:T(8,128)}, f32[8,2,168,512]{3,2,1,0:T(8,128)S(1)}, u32[]{:S(2)}) copy-start(f32[8,2,168,512]{3,2,1,0:T(8,128)S(1)} %convert_add_fusion) | copy-start | bytes 16515076
  160.3 57.2 %copy-start.17 = (bf16[128,2,512]{2,0,1:T(8,128)(2,1)S(1)}, bf16[128,2,512]{2,0,1:T(8,128)(2,1)}, u32[]{:S(2)}) copy-start(bf16[128,2,512]{2,0,1:T(8,128)(2,1)} %get-tuple-element.240) | copy-start | bytes 786436
  160.3 8.2 %collective-permute-start = (bf16[2,168,256]{2,1,0:T(8,128)(2,1)S(1)}, bf16[2,168,256]{2,1,0:T(8,128)(2,1)S(1)}, u32[]{:S(2)}, u32[]{:S(2)}) collective-permute-start(bf16[2,168,256]{2,1,0:T(8,128)(2,1)S(1)} %convert_element_type.199), channel_id=1, source_target_pairs={{0,32},{8,40},{16,48},{24,56},{32,64},{40,72},{48,80},{56,88},{64,... | collective-permute-start | bytes 516104 | tf_op jit(solution)/shard_map/while/body/eval_jaxpr/ppermute | solution.py:75
  164.5 7.5 %collective-permute-start.1 = (bf16[2,168,256]{2,1,0:T(8,128)(2,1)S(1)}, bf16[2,168,256]{2,1,0:T(8,128)(2,1)S(1)}, u32[]{:S(2)}, u32[]{:S(2)}) collective-permute-start(bf16[2,168,256]{2,1,0:T(8,128)(2,1)S(1)} %convert_element_type.200), channel_id=1, source_target_pairs={{0,224},{8,232},{16,240},{24,248},{32,0},{40,8},{48,16},{56,24},{6... | collective-permute-start | bytes 516104 | tf_op jit(solution)/shard_map/while/body/eval_jaxpr/ppermute | solution.py:76
  172.1 5.6 %collective-permute-start = (bf16[2,168,256]{2,1,0:T(8,128)(2,1)S(1)}, bf16[2,168,256]{2,1,0:T(8,128)(2,1)S(1)}, u32[]{:S(2)}, u32[]{:S(2)}) collective-permute-start(bf16[2,168,256]{2,1,0:T(8,128)(2,1)S(1)} %convert_element_type.199), channel_id=1, source_target_pairs={{0,32},{8,40},{16,48},{24,56},{32,64},{40,72},{48,80},{56,88},{64,... | collective-permute-start | bytes 516104 | tf_op jit(solution)/shard_map/while/body/eval_jaxpr/ppermute | solution.py:75
  172.4 6.8 %collective-permute-start.1 = (bf16[2,168,256]{2,1,0:T(8,128)(2,1)S(1)}, bf16[2,168,256]{2,1,0:T(8,128)(2,1)S(1)}, u32[]{:S(2)}, u32[]{:S(2)}) collective-permute-start(bf16[2,168,256]{2,1,0:T(8,128)(2,1)S(1)} %convert_element_type.200), channel_id=1, source_target_pairs={{0,224},{8,232},{16,240},{24,248},{32,0},{40,8},{48,16},{56,24},{6... | collective-permute-start | bytes 516104 | tf_op jit(solution)/shard_map/while/body/eval_jaxpr/ppermute | solution.py:76
  179.3 5.5 %collective-permute-start = (bf16[2,168,256]{2,1,0:T(8,128)(2,1)S(1)}, bf16[2,168,256]{2,1,0:T(8,128)(2,1)S(1)}, u32[]{:S(2)}, u32[]{:S(2)}) collective-permute-start(bf16[2,168,256]{2,1,0:T(8,128)(2,1)S(1)} %convert_element_type.199), channel_id=1, source_target_pairs={{0,32},{8,40},{16,48},{24,56},{32,64},{40,72},{48,80},{56,88},{64,... | collective-permute-start | bytes 516104 | tf_op jit(solution)/shard_map/while/body/eval_jaxpr/ppermute | solution.py:75
  179.6 6.7 %collective-permute-start.1 = (bf16[2,168,256]{2,1,0:T(8,128)(2,1)S(1)}, bf16[2,168,256]{2,1,0:T(8,128)(2,1)S(1)}, u32[]{:S(2)}, u32[]{:S(2)}) collective-permute-start(bf16[2,168,256]{2,1,0:T(8,128)(2,1)S(1)} %convert_element_type.200), channel_id=1, source_target_pairs={{0,224},{8,232},{16,240},{24,248},{32,0},{40,8},{48,16},{56,24},{6... | collective-permute-start | bytes 516104 | tf_op jit(solution)/shard_map/while/body/eval_jaxpr/ppermute | solution.py:76
  186.4 5.5 %collective-permute-start = (bf16[2,168,256]{2,1,0:T(8,128)(2,1)S(1)}, bf16[2,168,256]{2,1,0:T(8,128)(2,1)S(1)}, u32[]{:S(2)}, u32[]{:S(2)}) collective-permute-start(bf16[2,168,256]{2,1,0:T(8,128)(2,1)S(1)} %convert_element_type.199), channel_id=1, source_target_pairs={{0,32},{8,40},{16,48},{24,56},{32,64},{40,72},{48,80},{56,88},{64,... | collective-permute-start | bytes 516104 | tf_op jit(solution)/shard_map/while/body/eval_jaxpr/ppermute | solution.py:75
  186.5 6.7 %collective-permute-start.1 = (bf16[2,168,256]{2,1,0:T(8,128)(2,1)S(1)}, bf16[2,168,256]{2,1,0:T(8,128)(2,1)S(1)}, u32[]{:S(2)}, u32[]{:S(2)}) collective-permute-start(bf16[2,168,256]{2,1,0:T(8,128)(2,1)S(1)} %convert_element_type.200), channel_id=1, source_target_pairs={{0,224},{8,232},{16,240},{24,248},{32,0},{40,8},{48,16},{56,24},{6... | collective-permute-start | bytes 516104 | tf_op jit(solution)/shard_map/while/body/eval_jaxpr/ppermute | solution.py:76
  193.3 5.5 %collective-permute-start = (bf16[2,168,256]{2,1,0:T(8,128)(2,1)S(1)}, bf16[2,168,256]{2,1,0:T(8,128)(2,1)S(1)}, u32[]{:S(2)}, u32[]{:S(2)}) collective-permute-start(bf16[2,168,256]{2,1,0:T(8,128)(2,1)S(1)} %convert_element_type.199), channel_id=1, source_target_pairs={{0,32},{8,40},{16,48},{24,56},{32,64},{40,72},{48,80},{56,88},{64,... | collective-permute-start | bytes 516104 | tf_op jit(solution)/shard_map/while/body/eval_jaxpr/ppermute | solution.py:75
  193.4 6.7 %collective-permute-start.1 = (bf16[2,168,256]{2,1,0:T(8,128)(2,1)S(1)}, bf16[2,168,256]{2,1,0:T(8,128)(2,1)S(1)}, u32[]{:S(2)}, u32[]{:S(2)}) collective-permute-start(bf16[2,168,256]{2,1,0:T(8,128)(2,1)S(1)} %convert_element_type.200), channel_id=1, source_target_pairs={{0,224},{8,232},{16,240},{24,248},{32,0},{40,8},{48,16},{56,24},{6... | collective-permute-start | bytes 516104 | tf_op jit(solution)/shard_map/while/body/eval_jaxpr/ppermute | solution.py:76
  200.2 6.0 %collective-permute-start = (bf16[2,168,256]{2,1,0:T(8,128)(2,1)S(1)}, bf16[2,168,256]{2,1,0:T(8,128)(2,1)S(1)}, u32[]{:S(2)}, u32[]{:S(2)}) collective-permute-start(bf16[2,168,256]{2,1,0:T(8,128)(2,1)S(1)} %convert_element_type.199), channel_id=1, source_target_pairs={{0,32},{8,40},{16,48},{24,56},{32,64},{40,72},{48,80},{56,88},{64,... | collective-permute-start | bytes 516104 | tf_op jit(solution)/shard_map/while/body/eval_jaxpr/ppermute | solution.py:75
  200.3 7.2 %collective-permute-start.1 = (bf16[2,168,256]{2,1,0:T(8,128)(2,1)S(1)}, bf16[2,168,256]{2,1,0:T(8,128)(2,1)S(1)}, u32[]{:S(2)}, u32[]{:S(2)}) collective-permute-start(bf16[2,168,256]{2,1,0:T(8,128)(2,1)S(1)} %convert_element_type.200), channel_id=1, source_target_pairs={{0,224},{8,232},{16,240},{24,248},{32,0},{40,8},{48,16},{56,24},{6... | collective-permute-start | bytes 516104 | tf_op jit(solution)/shard_map/while/body/eval_jaxpr/ppermute | solution.py:76
  207.6 5.5 %collective-permute-start = (bf16[2,168,256]{2,1,0:T(8,128)(2,1)S(1)}, bf16[2,168,256]{2,1,0:T(8,128)(2,1)S(1)}, u32[]{:S(2)}, u32[]{:S(2)}) collective-permute-start(bf16[2,168,256]{2,1,0:T(8,128)(2,1)S(1)} %convert_element_type.199), channel_id=1, source_target_pairs={{0,32},{8,40},{16,48},{24,56},{32,64},{40,72},{48,80},{56,88},{64,... | collective-permute-start | bytes 516104 | tf_op jit(solution)/shard_map/while/body/eval_jaxpr/ppermute | solution.py:75
  208.5 6.7 %collective-permute-start.1 = (bf16[2,168,256]{2,1,0:T(8,128)(2,1)S(1)}, bf16[2,168,256]{2,1,0:T(8,128)(2,1)S(1)}, u32[]{:S(2)}, u32[]{:S(2)}) collective-permute-start(bf16[2,168,256]{2,1,0:T(8,128)(2,1)S(1)} %convert_element_type.200), channel_id=1, source_target_pairs={{0,224},{8,232},{16,240},{24,248},{32,0},{40,8},{48,16},{56,24},{6... | collective-permute-start | bytes 516104 | tf_op jit(solution)/shard_map/while/body/eval_jaxpr/ppermute | solution.py:76
  215.4 8.3 %collective-permute-start.7 = (bf16[168,512]{1,0:T(8,128)(2,1)S(1)}, bf16[168,512]{1,0:T(8,128)(2,1)S(1)}, u32[]{:S(2)}, u32[]{:S(2)}) collective-permute-start(bf16[168,512]{1,0:T(8,128)(2,1)S(1)} %fusion.26), channel_id=1, source_target_pairs={{0,16},{8,24},{16,0},{24,8},{32,48},{40,56},{48,32},{56,40},{64,80... | collective-permute-start | bytes 516104 | tf_op jit(solution)/shard_map/ppermute | solution.py:90

commit v3 on v2

--- a/solution.py
+++ b/solution.py
@@ -54,30 +54,27 @@
     return total
 
 
-def ring_scatter_sum(blocks, axis, count, stride):
+def ring_scatter_sum(blocks, axis, count, stride, lane_stride):
     size = lax.axis_size(axis)
     me = lax.axis_index(axis)
     digit = (me // stride) % count
-    half = blocks.shape[-1] // 2
-
-    def route(step):
-        return [
-            (i, i - ((i // stride) % count) * stride + (((i // stride) % count + step) % count) * stride)
-            for i in range(size)
-        ]
-
-    def chunk(k, step, lo):
-        block = lax.dynamic_index_in_dim(blocks, (digit - step * (k + 1)) % count, 0, keepdims=False)
-        return block[..., lo : lo + half]
-
-    def advance(k, carry):
-        up, down = carry
-        up = lax.ppermute(up.astype(jnp.bfloat16), axis, route(1)).astype(jnp.float32)
-        down = lax.ppermute(down.astype(jnp.bfloat16), axis, route(-1)).astype(jnp.float32)
-        return (up + chunk(k + 1, 1, 0), down + chunk(k + 1, -1, half))
-
-    up, down = lax.fori_loop(0, count - 1, advance, (chunk(0, 1, 0), chunk(0, -1, half)))
-    return jnp.concatenate([up, down], axis=-1)
+    step = 1 - 2 * ((me // lane_stride) % 2)
+
+    def target(i):
+        place = (i // stride) % count
+        turn = 1 - 2 * ((i // lane_stride) % 2)
+        return i + ((place + turn) % count - place) * stride
+
+    route = [(i, target(i)) for i in range(size)]
+
+    def chunk(k):
+        return lax.dynamic_index_in_dim(blocks, (digit - step * (k + 1)) % count, 0, keepdims=False)
+
+    def advance(k, running):
+        received = lax.ppermute(running.astype(jnp.bfloat16), axis, route).astype(jnp.float32)
+        return received + chunk(k + 1)
+
+    return lax.fori_loop(0, count - 1, advance, chunk(0))
 
 
 def pair_scatter_sum(blocks, axis, stride):
@@ -96,7 +93,7 @@
     grid = full.reshape(outer, middle, inner, -1, width)
     grid = jnp.moveaxis(grid, 2, 0)
     grid = pair_scatter_sum(grid, axis, 1)
-    grid = ring_scatter_sum(grid, axis, outer, middle * inner)
+    grid = ring_scatter_sum(grid, axis, outer, middle * inner, 1)
     return pair_scatter_sum(grid, axis, inner)
 
 

time: 231 us -> 244 us (1.056)
  local copies, waits for them, and re-layouts: 33.5 us -> 23.6 us
  starting transfers between devices: 40.1 us -> 48.3 us
  other arithmetic: 19.1 us -> 26.9 us
  waiting for transfers between devices: 101 us -> 106 us
    squeeze x8 -> x1, local copies, waits for them, and re-layouts: 9.98 us -> 0.05 us  [chunk(): lax.dynamic_index_in_dim(blocks, (digit - step * (k + 1)) % count, 0, kee...]
    ppermute x14 -> x7, starting transfers between devices: 17.3 us -> 26.8 us  [advance(): lax.ppermute(running.astype(jnp.bfloat16), axis, route).astype(jnp.float32)]
    add x14 -> x7, other arithmetic: 0.61 us -> 8.29 us  [advance(): return received + chunk(k + 1)]
    ppermute x14 -> x7, waiting for transfers between devices: 26.6 us -> 33.4 us  [advance(): lax.ppermute(running.astype(jnp.bfloat16), axis, route).astype(jnp.float32)]
    unnamed x51 -> x50, local copies, waits for them, and re-layouts: 10.5 us -> 10.6 us
  transfers between devices with their start and end apart: 22 -> 15, of which waited for: 21 -> 14; matrix products, arithmetic and copies ran while one was open for 12% -> 11% of each run, Pallas kernels for 0% -> 0%
where the time goes in v3:
time: 244 us; the launch traced here: 241 us
  waiting for transfers between devices  106 us (43%)
  starting transfers between devices  48.3 us (20%)
  matrix products  34.5 us (14%)
  other arithmetic  26.9 us (11%)
  local copies, waits for them, and re-layouts  23.6 us (10%)
    all_to_all x1, waiting for transfers between devices, gather_all(): received = lax.all_to_all(copies, axis, 0, 0)  52.4 us
    ppermute x7, waiting for transfers between devices, advance(): lax.ppermute(running.astype(jnp.bfloat16), axis, route).astype(jnp.float32)  33.4 us
    ppermute x7, starting transfers between devices, advance(): lax.ppermute(running.astype(jnp.bfloat16), axis, route).astype(jnp.float32)  26.8 us
    ppermute x4, waiting for transfers between devices, passed_along(): return lax.ppermute(block, axis, route)  15.9 us
    unnamed x50, local copies, waits for them, and re-layouts  10.6 us
    ppermute x4, starting transfers between devices, passed_along(): return lax.ppermute(block, axis, route)  8.63 us
    add x7, other arithmetic, advance(): return received + chunk(k + 1)  8.29 us
    dot_general x1, matrix products, per_device(): lax.dot_general(grad_cat, weight_cat, back_contract, preferred_element_ty...  7.49 us
  transfers between devices with their start and end apart: 15, of which 14 were waited for; matrix products, arithmetic and copies ran while one was open for 11% of the time, Pallas kernels for 0%

profile of v3, /device:TPU:96, one launch (start us, length us, event | category | flops | bytes accessed | tf_op | source)
XLA Modules:
  0.0 240.6 jit_solution(1040308716197705837)
XLA Ops:
  0.6 3.9 %broadcast_in_dim.71 = bf16[8,64,5376]{2,1,0:T(8,128)(2,1)} broadcast(bf16[64,5376]{1,0:T(8,128)(2,1)} %param.9), dimensions={1,2} | broadcast | bytes 6193152 | tf_op jit(solution)/shard_map/broadcast_in_dim | solution.py:102
  4.5 7.1 %all-to-all-start = ((bf16[8,64,5376]{2,1,0:T(8,128)(2,1)}), bf16[8,64,5376]{2,1,0:T(8,128)(2,1)}, u32[]{:S(2)}, u32[]{:S(2)}) async-start(bf16[8,64,5376]{2,1,0:T(8,128)(2,1)} %broadcast_in_dim.71), calls=%async_computation | async-start | bytes 11010048 | tf_op jit(solution)/shard_map/all_to_all | solution.py:103
  11.6 0.9 copy.42
  12.6 1.0 multiply_cosine_fusion
  13.6 1.2 fusion.7
  14.8 3.5 %constant_dynamic-update-slice_fusion.2 = bf16[5376,512]{1,0:T(8,128)(2,1)} fusion(bf16[5376,256]{1,0:T(8,128)(2,1)} %param.10), kind=kLoop, calls=%fused_computation.90 | loop fusion | bytes 5505024
  18.3 1.2 constant_dynamic-update-slice_fusion.1
  19.6 2.6 %constant_dynamic-update-slice_fusion = bf16[5376,512]{1,0:T(8,128)(2,1)} fusion(bf16[5376,512]{1,0:T(8,128)(2,1)} %constant_dynamic-update-slice_fusion.1, bf16[5376,128]{1,0:T(8,128)(2,1)} %param.12), kind=kLoop, calls=%fused_computation.88 | loop fusion | bytes 2752512 | tf_op jit(solution)/shard_map/concatenate | solution.py:220
  22.2 52.4 %all-to-all-done = bf16[8,64,5376]{2,1,0:T(8,128)(2,1)} async-done(((bf16[8,64,5376]{2,1,0:T(8,128)(2,1)}), bf16[8,64,5376]{2,1,0:T(8,128)(2,1)}, u32[]{:S(2)}, u32[]{:S(2)}) %all-to-all-start) | async-done | bytes 5505056 | tf_op jit(solution)/shard_map/all_to_all | solution.py:103
  74.6 6.8 %convolution_bitcast_fusion.2 = f32[512,512]{0,1:T(8,128)S(1)} fusion(bf16[5376,512]{1,0:T(8,128)(2,1)} %constant_dynamic-update-slice_fusion, bf16[512,5376]{1,0:T(8,128)(2,1)} %bitcast.3), kind=kOutput, calls=%fused_computation.25 | convolution fusion | flops 2818572288 | bytes 12058624 | tf_op jit(solution)/shard_map/dot_general | solution.py:221
  82.2 0.7 pad_maximum_fusion.2
  82.9 2.5 %collective-permute-start.1 = (bf16[2,512,128]{1,2,0:T(8,128)(2,1)}, bf16[2,512,128]{1,2,0:T(8,128)(2,1)}, u32[]{:S(2)}, u32[]{:S(2)}) collective-permute-start(bf16[2,512,128]{1,2,0:T(8,128)(2,1)} %pad_maximum_fusion.2), channel_id=1, source_target_pairs={{0,16},{8,24},{16,32},{24,40},{32,48},{40,56},{48,64},{56,72},{64,... | collective-permute-start | bytes 786440 | tf_op jit(solution)/shard_map/ppermute | solution.py:18
  85.4 2.1 collective-permute-start.2
  88.6 6.6 %collective-permute-done.1 = bf16[2,512,128]{1,2,0:T(8,128)(2,1)} collective-permute-done((bf16[2,512,128]{1,2,0:T(8,128)(2,1)}, bf16[2,512,128]{1,2,0:T(8,128)(2,1)}, u32[]{:S(2)}, u32[]{:S(2)}) %collective-permute-start.1) | collective-permute-done | bytes 262176 | tf_op jit(solution)/shard_map/ppermute | solution.py:18
  95.2 1.2 collective-permute-done.2
  96.4 1.1 maximum_maximum_fusion
  97.5 1.2 fusion.2
  98.7 1.3 exponential_reduce_fusion
  100.0 2.7 %bitcast_convert_fusion = (f32[2,512,128]{1,2,0:T(8,128)S(1)}, bf16[128,2,512]{2,0,1:T(8,128)(2,1)}) fusion(f32[1536,512,2]{1,0,2:T(8,128)S(1)} %get-tuple-element.232, f32[2,512]{1,0:T(2,128)S(1)} %log_add_fusion, pred[512,1536]{0,1:T(8,128)(4,1)S(1)} %fusion.7, bf16[2,1536,128]{1,2,0:T(8,128)(2,1)S(1)} %maximum_maximum_fusion), kind=kOutput, calls=%fused_computation.63 | convolution fusion | flops 409206784 | bytes 8261632 | tf_op jit(solution)/shard_map/while/body/eval_jaxpr/kgqj,jkd->qkgd/dot_general | solution.py:161
  103.0 1.3 multiply_reduce_fusion
  104.3 1.2 copy.54
  105.5 4.9 %convolution_bitcast_fusion = f32[1,1536,128]{1,2,0:T(8,128)S(1)} fusion(bf16[512,2,128]{0,2,1:T(8,128)(2,1)} %copy.42, f32[1536,512,2]{1,0,2:T(8,128)} %copy-done, f32[2,512]{1,0:T(2,128)S(1)} %log_add_fusion, pred[512,1536]{0,1:T(8,128)(4,1)S(1)} %fusion.7), kind=kOutput, calls=%fused_computation.19 | convolution fusion | flops 408944640 | bytes 8130560 | tf_op jit(solution)/shard_map/while/body/eval_jaxpr/kgqj,qkgd->jkd/dot_general | solution.py:200
  110.5 2.5 %fusion.4 = bf16[2,512,1536]{1,2,0:T(8,128)(2,1)S(1)} fusion(bf16[512,2,128]{0,2,1:T(8,128)(2,1)S(1)} %copy-done.18, f32[1536,512,2]{1,0,2:T(8,128)S(1)} %bitcast.149, f32[2,512]{1,0:T(2,128)S(1)} %copy.54, f32[2,512]{1,0:T(2,128)S(1)} %log_add_fusion, pred[512,1536]{0,1:T(8,128)(4,1)S(1)} %fusion.7, bf16[2,1536,128]{1,2,0:T(8,128)(2,1)S(1)} %copy-done.6), kind=kOutput, calls=%fused_computation.14 | convolution fusion | flops 412090368 | bytes 10887168 | tf_op jit(solution)/shard_map/while/body/eval_jaxpr/qkgd,jkd->kgqj/dot_general | solution.py:190
  113.0 1.4 fusion.9
  114.4 1.2 convolution_bitcast_fusion.1
  116.0 0.8 fusion.43
  116.8 1.9 collective-permute-start.3
  118.8 2.1 collective-permute-start.4
  121.9 2.1 collective-permute-done.3
  124.0 6.0 %collective-permute-done.4 = bf16[2,512,128]{1,2,0:T(8,128)(2,1)} collective-permute-done((bf16[2,512,128]{1,2,0:T(8,128)(2,1)}, bf16[2,512,128]{1,2,0:T(8,128)(2,1)}, u32[]{:S(2)}, u32[]{:S(2)}) %collective-permute-start.4) | collective-permute-done | bytes 262176 | tf_op jit(solution)/shard_map/ppermute | solution.py:18
  130.1 1.1 fusion.13
  132.1 7.5 %convolution_convert_fusion = bf16[512,5376]{1,0:T(8,128)(2,1)} fusion(bf16[5376,512]{1,0:T(8,128)(2,1)} %constant_dynamic-update-slice_fusion, bf16[512,128]{0,1:T(8,128)(2,1)S(1)} %fusion.34, bf16[512,128]{0,1:T(8,128)(2,1)S(1)} %fusion.35, bf16[512,256]{0,1:T(8,128)(2,1)S(1)} %bitcast.155), kind=kOutput, calls=%fused_computation.2 | convolution fusion | flops 2822897664 | bytes 11534336 | tf_op jit(solution)/shard_map/dot_general | solution.py:289
  139.6 6.4 %multiply_convert_fusion = bf16[5376,512]{1,0:T(8,128)(2,1)S(1)} fusion(bf16[512,5376]{1,0:T(8,128)(2,1)} %bitcast.3, bf16[512,128]{0,1:T(8,128)(2,1)S(1)} %fusion.34, bf16[512,128]{0,1:T(8,128)(2,1)S(1)} %fusion.35, bf16[512,256]{0,1:T(8,128)(2,1)S(1)} %bitcast.156), kind=kOutput, calls=%fused_computation.1 | convolution fusion | flops 2825650176 | bytes 11534336 | tf_op jit(solution)/shard_map/dot_general | solution.py:296
  146.0 2.4 copy-done.2
  148.3 1.7 dynamic-slice_bitcast_fusion
  150.0 5.1 %all-to-all-start.1 = ((bf16[8,64,5376]{2,1,0:T(8,128)(2,1)}), bf16[8,64,5376]{2,1,0:T(8,128)(2,1)}, u32[]{:S(2)}, u32[]{:S(2)}) async-start(bf16[8,64,5376]{2,1,0:T(8,128)(2,1)} %bitcast.150), calls=%async_computation.1 | async-start | bytes 11010048 | tf_op jit(solution)/shard_map/all_to_all | solution.py:110
  155.3 2.6 %convert_add_fusion = f32[8,2,168,512]{3,2,1,0:T(8,128)S(1)} fusion(bf16[8,2,168,512]{3,2,1,0:T(8,128)(2,1)S(1)} %collective-permute-done.5, bf16[8,2,2,168,512]{4,3,2,1,0:T(8,128)(2,1)} %bitcast.152, s32[]{:T(128)S(6)} %select_n.93), kind=kLoop, calls=%fused_computation.10 | loop fusion | flops 4128768 | bytes 11010052 | tf_op jit(solution)/shard_map/add | solution.py:87
  158.0 2.3 copy-done.1
  160.3 69.0 %while.10 = (s32[]{:T(128)}, f32[2,168,512]{2,1,0:T(8,128)S(1)}, s32[]{:T(128)}, s32[]{:T(128)}, f32[8,2,168,512]{3,2,1,0:T(8,128)}, /*index=5*/s32[]{:T(128)}, s32[]{:T(128)}, s32[]{:T(128)}, s32[]{:T(128)}, s32[]{:T(128)}) while((s32[]{:T(128)}, f32[2,168,512]{2,1,0:T(8,128)S(1)}, s32[]{:T(128)}, s32[]{:T(128)}, ...), condition=%wide.region_8.9_spmd, body=%wide.region_7.8_spmd.sunk | while | flops 516115 | bytes 4129092 | solution.py:77
  160.3 4.2 %collective-permute-start = (bf16[2,168,512]{2,1,0:T(8,128)(2,1)S(1)}, bf16[2,168,512]{2,1,0:T(8,128)(2,1)S(1)}, u32[]{:S(2)}, u32[]{:S(2)}) collective-permute-start(bf16[2,168,512]{2,1,0:T(8,128)(2,1)S(1)} %convert_element_type.175), channel_id=1, source_target_pairs={{0,32},{8,232},{16,48},{24,248},{32,64},{40,8},{48,80},{56,24},{64... | collective-permute-start | bytes 1032200 | tf_op jit(solution)/shard_map/while/body/eval_jaxpr/ppermute | solution.py:74
  164.5 4.8 %collective-permute-done = bf16[2,168,512]{2,1,0:T(8,128)(2,1)S(1)} collective-permute-done((bf16[2,168,512]{2,1,0:T(8,128)(2,1)S(1)}, bf16[2,168,512]{2,1,0:T(8,128)(2,1)S(1)}, u32[]{:S(2)}, u32[]{:S(2)}) %collective-permute-start) | collective-permute-done | bytes 344096 | tf_op jit(solution)/shard_map/while/body/eval_jaxpr/ppermute | solution.py:74
  169.3 1.2 bitcast_add_fusion.3
  170.5 3.8 %collective-permute-start = (bf16[2,168,512]{2,1,0:T(8,128)(2,1)S(1)}, bf16[2,168,512]{2,1,0:T(8,128)(2,1)S(1)}, u32[]{:S(2)}, u32[]{:S(2)}) collective-permute-start(bf16[2,168,512]{2,1,0:T(8,128)(2,1)S(1)} %convert_element_type.175), channel_id=1, source_target_pairs={{0,32},{8,232},{16,48},{24,248},{32,64},{40,8},{48,80},{56,24},{64... | collective-permute-start | bytes 1032200 | tf_op jit(solution)/shard_map/while/body/eval_jaxpr/ppermute | solution.py:74
  174.3 4.8 %collective-permute-done = bf16[2,168,512]{2,1,0:T(8,128)(2,1)S(1)} collective-permute-done((bf16[2,168,512]{2,1,0:T(8,128)(2,1)S(1)}, bf16[2,168,512]{2,1,0:T(8,128)(2,1)S(1)}, u32[]{:S(2)}, u32[]{:S(2)}) %collective-permute-start) | collective-permute-done | bytes 344096 | tf_op jit(solution)/shard_map/while/body/eval_jaxpr/ppermute | solution.py:74
  179.1 1.2 bitcast_add_fusion.3
  180.3 3.8 %collective-permute-start = (bf16[2,168,512]{2,1,0:T(8,128)(2,1)S(1)}, bf16[2,168,512]{2,1,0:T(8,128)(2,1)S(1)}, u32[]{:S(2)}, u32[]{:S(2)}) collective-permute-start(bf16[2,168,512]{2,1,0:T(8,128)(2,1)S(1)} %convert_element_type.175), channel_id=1, source_target_pairs={{0,32},{8,232},{16,48},{24,248},{32,64},{40,8},{48,80},{56,24},{64... | collective-permute-start | bytes 1032200 | tf_op jit(solution)/shard_map/while/body/eval_jaxpr/ppermute | solution.py:74
  184.1 4.8 %collective-permute-done = bf16[2,168,512]{2,1,0:T(8,128)(2,1)S(1)} collective-permute-done((bf16[2,168,512]{2,1,0:T(8,128)(2,1)S(1)}, bf16[2,168,512]{2,1,0:T(8,128)(2,1)S(1)}, u32[]{:S(2)}, u32[]{:S(2)}) %collective-permute-start) | collective-permute-done | bytes 344096 | tf_op jit(solution)/shard_map/while/body/eval_jaxpr/ppermute | solution.py:74
  188.9 1.2 bitcast_add_fusion.3
  190.1 3.8 %collective-permute-start = (bf16[2,168,512]{2,1,0:T(8,128)(2,1)S(1)}, bf16[2,168,512]{2,1,0:T(8,128)(2,1)S(1)}, u32[]{:S(2)}, u32[]{:S(2)}) collective-permute-start(bf16[2,168,512]{2,1,0:T(8,128)(2,1)S(1)} %convert_element_type.175), channel_id=1, source_target_pairs={{0,32},{8,232},{16,48},{24,248},{32,64},{40,8},{48,80},{56,24},{64... | collective-permute-start | bytes 1032200 | tf_op jit(solution)/shard_map/while/body/eval_jaxpr/ppermute | solution.py:74
  193.9 4.8 %collective-permute-done = bf16[2,168,512]{2,1,0:T(8,128)(2,1)S(1)} collective-permute-done((bf16[2,168,512]{2,1,0:T(8,128)(2,1)S(1)}, bf16[2,168,512]{2,1,0:T(8,128)(2,1)S(1)}, u32[]{:S(2)}, u32[]{:S(2)}) %collective-permute-start) | collective-permute-done | bytes 344096 | tf_op jit(solution)/shard_map/while/body/eval_jaxpr/ppermute | solution.py:74
  198.7 1.2 bitcast_add_fusion.3
  199.9 3.8 %collective-permute-start = (bf16[2,168,512]{2,1,0:T(8,128)(2,1)S(1)}, bf16[2,168,512]{2,1,0:T(8,128)(2,1)S(1)}, u32[]{:S(2)}, u32[]{:S(2)}) collective-permute-start(bf16[2,168,512]{2,1,0:T(8,128)(2,1)S(1)} %convert_element_type.175), channel_id=1, source_target_pairs={{0,32},{8,232},{16,48},{24,248},{32,64},{40,8},{48,80},{56,24},{64... | collective-permute-start | bytes 1032200 | tf_op jit(solution)/shard_map/while/body/eval_jaxpr/ppermute | solution.py:74
  203.7 4.8 %collective-permute-done = bf16[2,168,512]{2,1,0:T(8,128)(2,1)S(1)} collective-permute-done((bf16[2,168,512]{2,1,0:T(8,128)(2,1)S(1)}, bf16[2,168,512]{2,1,0:T(8,128)(2,1)S(1)}, u32[]{:S(2)}, u32[]{:S(2)}) %collective-permute-start) | collective-permute-done | bytes 344096 | tf_op jit(solution)/shard_map/while/body/eval_jaxpr/ppermute | solution.py:74
  208.5 1.2 bitcast_add_fusion.3
  209.7 3.8 %collective-permute-start = (bf16[2,168,512]{2,1,0:T(8,128)(2,1)S(1)}, bf16[2,168,512]{2,1,0:T(8,128)(2,1)S(1)}, u32[]{:S(2)}, u32[]{:S(2)}) collective-permute-start(bf16[2,168,512]{2,1,0:T(8,128)(2,1)S(1)} %convert_element_type.175), channel_id=1, source_target_pairs={{0,32},{8,232},{16,48},{24,248},{32,64},{40,8},{48,80},{56,24},{64... | collective-permute-start | bytes 1032200 | tf_op jit(solution)/shard_map/while/body/eval_jaxpr/ppermute | solution.py:74
  213.5 4.8 %collective-permute-done = bf16[2,168,512]{2,1,0:T(8,128)(2,1)S(1)} collective-permute-done((bf16[2,168,512]{2,1,0:T(8,128)(2,1)S(1)}, bf16[2,168,512]{2,1,0:T(8,128)(2,1)S(1)}, u32[]{:S(2)}, u32[]{:S(2)}) %collective-permute-start) | collective-permute-done | bytes 344096 | tf_op jit(solution)/shard_map/while/body/eval_jaxpr/ppermute | solution.py:74
  218.3 1.2 bitcast_add_fusion.3
  219.5 3.8 %collective-permute-start = (bf16[2,168,512]{2,1,0:T(8,128)(2,1)S(1)}, bf16[2,168,512]{2,1,0:T(8,128)(2,1)S(1)}, u32[]{:S(2)}, u32[]{:S(2)}) collective-permute-start(bf16[2,168,512]{2,1,0:T(8,128)(2,1)S(1)} %convert_element_type.175), channel_id=1, source_target_pairs={{0,32},{8,232},{16,48},{24,248},{32,64},{40,8},{48,80},{56,24},{64... | collective-permute-start | bytes 1032200 | tf_op jit(solution)/shard_map/while/body/eval_jaxpr/ppermute | solution.py:74
  223.3 4.8 %collective-permute-done = bf16[2,168,512]{2,1,0:T(8,128)(2,1)S(1)} collective-permute-done((bf16[2,168,512]{2,1,0:T(8,128)(2,1)S(1)}, bf16[2,168,512]{2,1,0:T(8,128)(2,1)S(1)}, u32[]{:S(2)}, u32[]{:S(2)}) %collective-permute-start) | collective-permute-done | bytes 344096 | tf_op jit(solution)/shard_map/while/body/eval_jaxpr/ppermute | solution.py:74
  228.1 1.2 bitcast_add_fusion.3
  229.3 0.8 collective-permute-start.6
  230.1 0.8 copy.44
  230.9 3.9 %collective-permute-done.6 = bf16[168,512]{1,0:T(8,128)(2,1)S(1)} collective-permute-done((bf16[168,512]{1,0:T(8,128)(2,1)S(1)}, bf16[168,512]{1,0:T(8,128)(2,1)S(1)}, u32[]{:S(2)}, u32[]{:S(2)}) %collective-permute-start.6) | collective-permute-done | bytes 172064 | tf_op jit(solution)/shard_map/ppermute | solution.py:87
  236.2 4.4 %reduce_sum.71 = bf16[64,5376]{1,0:T(8,128)(2,1)} reduce(bf16[8,64,5376]{2,1,0:T(8,128)(2,1)} %all-to-all-done.1, bf16[]{:T(256)} %constant.204.clone.1), dimensions={0}, to_apply=%region_6.7 | reduce | flops 2408448 | bytes 6193154 | tf_op jit(solution)/shard_map/reduce_sum | solution.py:111
  (93 shorter events, 6.4 us)
Async XLA Ops:
  4.5 7.1 %copy-start.16 = (bf16[512,256]{1,0:T(8,128)(2,1)S(1)}, bf16[512,256]{1,0:T(8,128)(2,1)}, u32[]{:S(2)}) copy-start(bf16[512,256]{1,0:T(8,128)(2,1)} %param.15) | copy-start | bytes 786436
  4.5 70.1 %all-to-all-start = ((bf16[8,64,5376]{2,1,0:T(8,128)(2,1)}), bf16[8,64,5376]{2,1,0:T(8,128)(2,1)}, u32[]{:S(2)}, u32[]{:S(2)}) async-start(bf16[8,64,5376]{2,1,0:T(8,128)(2,1)} %broadcast_in_dim.71), calls=%async_computation | async-start | bytes 11010048 | tf_op jit(solution)/shard_map/all_to_all | solution.py:103
  11.6 6.8 %copy-start.15 = (bf16[5376,128]{1,0:T(8,128)(2,1)S(1)}, bf16[5376,128]{1,0:T(8,128)(2,1)}, u32[]{:S(2)}) copy-start(bf16[5376,128]{1,0:T(8,128)(2,1)} %param.11) | copy-start | bytes 4128772
  13.6 74.5 %copy-start.9 = (f32[512,64]{1,0:T(8,128)}, f32[512,64]{1,0:T(8,128)S(1)}, u32[]{:S(2)}) copy-start(f32[512,64]{1,0:T(8,128)S(1)} %get-tuple-element.229) | copy-start | bytes 393220
  13.6 74.5 %copy-start.11 = (f32[512,64]{1,0:T(8,128)}, f32[512,64]{1,0:T(8,128)S(1)}, u32[]{:S(2)}) copy-start(f32[512,64]{1,0:T(8,128)S(1)} %get-tuple-element.230) | copy-start | bytes 393220
  74.6 6.9 %copy-start.19 = (f32[128]{0:T(128)S(1)}, f32[128]{0:T(128)}, u32[]{:S(2)}) copy-start(f32[128]{0:T(128)} %param.14) | copy-start | bytes 1540
  74.6 13.2 %copy-start.20 = (f32[128]{0:T(128)S(1)}, f32[128]{0:T(128)}, u32[]{:S(2)}) copy-start(f32[128]{0:T(128)} %param.13) | copy-start | bytes 1540
  81.4 6.2 %copy-start.3 = (f32[512,512]{0,1:T(8,128)}, f32[512,512]{0,1:T(8,128)S(1)}, u32[]{:S(2)}) copy-start(f32[512,512]{0,1:T(8,128)S(1)} %convolution_bitcast_fusion.2) | copy-start | bytes 3145732
  82.9 12.3 %collective-permute-start.1 = (bf16[2,512,128]{1,2,0:T(8,128)(2,1)}, bf16[2,512,128]{1,2,0:T(8,128)(2,1)}, u32[]{:S(2)}, u32[]{:S(2)}) collective-permute-start(bf16[2,512,128]{1,2,0:T(8,128)(2,1)} %pad_maximum_fusion.2), channel_id=1, source_target_pairs={{0,16},{8,24},{16,32},{24,40},{32,48},{40,56},{48,64},{56,72},{64,... | collective-permute-start | bytes 786440 | tf_op jit(solution)/shard_map/ppermute | solution.py:18
  85.4 11.0 %collective-permute-start.2 = (bf16[2,512,128]{1,2,0:T(8,128)(2,1)}, bf16[2,512,128]{1,2,0:T(8,128)(2,1)}, u32[]{:S(2)}, u32[]{:S(2)}) collective-permute-start(bf16[2,512,128]{1,2,0:T(8,128)(2,1)} %pad_maximum_fusion.2), channel_id=1, source_target_pairs={{0,8},{8,16},{16,24},{24,32},{32,40},{40,48},{48,56},{56,64},{64,7... | collective-permute-start | bytes 786440 | tf_op jit(solution)/shard_map/ppermute | solution.py:18
  88.5 8.9 %copy-start.13 = (bf16[512,2,128]{2,0,1:T(8,128)(2,1)}, bf16[512,2,128]{2,0,1:T(8,128)(2,1)S(1)}, u32[]{:S(2)}) copy-start(bf16[512,2,128]{2,0,1:T(8,128)(2,1)S(1)} %fusion.14) | copy-start | bytes 786436
  97.5 2.6 %copy-start.5 = (bf16[2,1536,128]{1,2,0:T(8,128)(2,1)}, bf16[2,1536,128]{1,2,0:T(8,128)(2,1)S(1)}, u32[]{:S(2)}) copy-start(bf16[2,1536,128]{1,2,0:T(8,128)(2,1)S(1)} %maximum_maximum_fusion) | copy-start | bytes 2359300
  98.7 4.0 %copy-start = (f32[1536,512,2]{1,0,2:T(8,128)}, f32[1536,512,2]{1,0,2:T(8,128)S(1)}, u32[]{:S(2)}) copy-start(f32[1536,512,2]{1,0,2:T(8,128)S(1)} %get-tuple-element.232) | copy-start | bytes 18874372
  104.3 6.2 %slice-start = ((s8[6291456]{0:T(1024)(128)(4,1)}), s8[2097152]{0:T(1024)(128)(4,1)S(1)}, s32[]{:S(2)}) async-start(s8[6291456]{0:T(1024)(128)(4,1)} %bitcast.148), calls=%async_computation.2 | async-start | bytes 4194304
  105.5 5.0 %slice-start.1 = ((s8[6291456]{0:T(1024)(128)(4,1)}), s8[4194304]{0:T(1024)(128)(4,1)S(1)}, s32[]{:S(2)}) async-start(s8[6291456]{0:T(1024)(128)(4,1)} %bitcast.148), calls=%async_computation.3 | async-start | bytes 8388608
  105.5 5.0 %copy-start.6 = (bf16[2,1536,128]{1,2,0:T(8,128)(2,1)S(1)}, bf16[2,1536,128]{1,2,0:T(8,128)(2,1)}, u32[]{:S(2)}) copy-start(bf16[2,1536,128]{1,2,0:T(8,128)(2,1)} %copy-done.5) | copy-start | bytes 2359300
  105.5 5.0 %copy-start.18 = (bf16[512,2,128]{0,2,1:T(8,128)(2,1)S(1)}, bf16[512,2,128]{0,2,1:T(8,128)(2,1)}, u32[]{:S(2)}) copy-start(bf16[512,2,128]{0,2,1:T(8,128)(2,1)} %copy.42) | copy-start | bytes 786436
  110.5 5.4 %copy-start.7 = (f32[1,1536,128]{1,2,0:T(8,128)}, f32[1,1536,128]{1,2,0:T(8,128)S(1)}, u32[]{:S(2)}) copy-start(f32[1,1536,128]{1,2,0:T(8,128)S(1)} %convolution_bitcast_fusion) | copy-start | bytes 2359300
  110.5 3.9 %copy-start.14 = (bf16[512,2,128]{2,0,1:T(8,128)(2,1)S(1)}, bf16[512,2,128]{2,0,1:T(8,128)(2,1)}, u32[]{:S(2)}) copy-start(bf16[512,2,128]{2,0,1:T(8,128)(2,1)} %copy-done.13) | copy-start | bytes 786436
  113.0 2.6 %copy-start.10 = (f32[512,64]{1,0:T(8,128)S(1)}, f32[512,64]{1,0:T(8,128)}, u32[]{:S(2)}) copy-start(f32[512,64]{1,0:T(8,128)} %copy-done.9) | copy-start | bytes 393220
  113.0 2.6 %copy-start.12 = (f32[512,64]{1,0:T(8,128)S(1)}, f32[512,64]{1,0:T(8,128)}, u32[]{:S(2)}) copy-start(f32[512,64]{1,0:T(8,128)} %copy-done.11) | copy-start | bytes 393220
  115.9 16.0 %copy-start.4 = (f32[512,512]{0,1:T(8,128)S(1)}, f32[512,512]{0,1:T(8,128)}, u32[]{:S(2)}) copy-start(f32[512,512]{0,1:T(8,128)} %copy-done.3) | copy-start | bytes 3145732
  116.0 14.1 %copy-start.8 = (f32[1,1536,128]{1,2,0:T(8,128)S(1)}, f32[1,1536,128]{1,2,0:T(8,128)}, u32[]{:S(2)}) copy-start(f32[1,1536,128]{1,2,0:T(8,128)} %copy-done.7) | copy-start | bytes 2359300
  116.8 7.2 %collective-permute-start.3 = (bf16[2,512,128]{1,2,0:T(8,128)(2,1)}, bf16[2,512,128]{1,2,0:T(8,128)(2,1)}, u32[]{:S(2)}, u32[]{:S(2)}) collective-permute-start(bf16[2,512,128]{1,2,0:T(8,128)(2,1)} %get-tuple-element.221), channel_id=1, source_target_pairs={{8,0},{16,8},{24,16},{32,24},{40,32},{48,40},{56,48},{64,56},{72,6... | collective-permute-start | bytes 786440 | tf_op jit(solution)/shard_map/ppermute | solution.py:18
  118.8 11.3 %collective-permute-start.4 = (bf16[2,512,128]{1,2,0:T(8,128)(2,1)}, bf16[2,512,128]{1,2,0:T(8,128)(2,1)}, u32[]{:S(2)}, u32[]{:S(2)}) collective-permute-start(bf16[2,512,128]{1,2,0:T(8,128)(2,1)} %get-tuple-element.222), channel_id=1, source_target_pairs={{16,0},{24,8},{32,16},{40,24},{48,32},{56,40},{64,48},{72,56},{80,... | collective-permute-start | bytes 786440 | tf_op jit(solution)/shard_map/ppermute | solution.py:18
  145.9 2.4 copy-start.2
  150.0 5.3 %collective-permute-start.5 = (bf16[8,2,168,512]{3,2,1,0:T(8,128)(2,1)}, bf16[8,2,168,512]{3,2,1,0:T(8,128)(2,1)S(1)}, u32[]{:S(2)}, u32[]{:S(2)}) collective-permute-start(bf16[8,2,168,512]{3,2,1,0:T(8,128)(2,1)} %dynamic-slice_bitcast_fusion), channel_id=1, source_target_pairs={{0,8},{8,0},{16,24},{24,16},{32,40},{40,32},{48,56},{56,48},{64,72... | collective-permute-start | bytes 8257544 | tf_op jit(solution)/shard_map/ppermute | solution.py:87
  150.0 86.2 %all-to-all-start.1 = ((bf16[8,64,5376]{2,1,0:T(8,128)(2,1)}), bf16[8,64,5376]{2,1,0:T(8,128)(2,1)}, u32[]{:S(2)}, u32[]{:S(2)}) async-start(bf16[8,64,5376]{2,1,0:T(8,128)(2,1)} %bitcast.150), calls=%async_computation.1 | async-start | bytes 11010048 | tf_op jit(solution)/shard_map/all_to_all | solution.py:110
  157.9 2.4 copy-start.1
  160.3 69.8 %copy-start.17 = (bf16[128,2,512]{2,0,1:T(8,128)(2,1)S(1)}, bf16[128,2,512]{2,0,1:T(8,128)(2,1)}, u32[]{:S(2)}) copy-start(bf16[128,2,512]{2,0,1:T(8,128)(2,1)} %get-tuple-element.234) | copy-start | bytes 786436
  160.3 8.9 %collective-permute-start = (bf16[2,168,512]{2,1,0:T(8,128)(2,1)S(1)}, bf16[2,168,512]{2,1,0:T(8,128)(2,1)S(1)}, u32[]{:S(2)}, u32[]{:S(2)}) collective-permute-start(bf16[2,168,512]{2,1,0:T(8,128)(2,1)S(1)} %convert_element_type.175), channel_id=1, source_target_pairs={{0,32},{8,232},{16,48},{24,248},{32,64},{40,8},{48,80},{56,24},{64... | collective-permute-start | bytes 1032200 | tf_op jit(solution)/shard_map/while/body/eval_jaxpr/ppermute | solution.py:74
  170.5 8.5 %collective-permute-start = (bf16[2,168,512]{2,1,0:T(8,128)(2,1)S(1)}, bf16[2,168,512]{2,1,0:T(8,128)(2,1)S(1)}, u32[]{:S(2)}, u32[]{:S(2)}) collective-permute-start(bf16[2,168,512]{2,1,0:T(8,128)(2,1)S(1)} %convert_element_type.175), channel_id=1, source_target_pairs={{0,32},{8,232},{16,48},{24,248},{32,64},{40,8},{48,80},{56,24},{64... | collective-permute-start | bytes 1032200 | tf_op jit(solution)/shard_map/while/body/eval_jaxpr/ppermute | solution.py:74
  180.3 8.5 %collective-permute-start = (bf16[2,168,512]{2,1,0:T(8,128)(2,1)S(1)}, bf16[2,168,512]{2,1,0:T(8,128)(2,1)S(1)}, u32[]{:S(2)}, u32[]{:S(2)}) collective-permute-start(bf16[2,168,512]{2,1,0:T(8,128)(2,1)S(1)} %convert_element_type.175), channel_id=1, source_target_pairs={{0,32},{8,232},{16,48},{24,248},{32,64},{40,8},{48,80},{56,24},{64... | collective-permute-start | bytes 1032200 | tf_op jit(solution)/shard_map/while/body/eval_jaxpr/ppermute | solution.py:74
  190.1 8.5 %collective-permute-start = (bf16[2,168,512]{2,1,0:T(8,128)(2,1)S(1)}, bf16[2,168,512]{2,1,0:T(8,128)(2,1)S(1)}, u32[]{:S(2)}, u32[]{:S(2)}) collective-permute-start(bf16[2,168,512]{2,1,0:T(8,128)(2,1)S(1)} %convert_element_type.175), channel_id=1, source_target_pairs={{0,32},{8,232},{16,48},{24,248},{32,64},{40,8},{48,80},{56,24},{64... | collective-permute-start | bytes 1032200 | tf_op jit(solution)/shard_map/while/body/eval_jaxpr/ppermute | solution.py:74
  199.9 8.5 %collective-permute-start = (bf16[2,168,512]{2,1,0:T(8,128)(2,1)S(1)}, bf16[2,168,512]{2,1,0:T(8,128)(2,1)S(1)}, u32[]{:S(2)}, u32[]{:S(2)}) collective-permute-start(bf16[2,168,512]{2,1,0:T(8,128)(2,1)S(1)} %convert_element_type.175), channel_id=1, source_target_pairs={{0,32},{8,232},{16,48},{24,248},{32,64},{40,8},{48,80},{56,24},{64... | collective-permute-start | bytes 1032200 | tf_op jit(solution)/shard_map/while/body/eval_jaxpr/ppermute | solution.py:74
  209.7 8.5 %collective-permute-start = (bf16[2,168,512]{2,1,0:T(8,128)(2,1)S(1)}, bf16[2,168,512]{2,1,0:T(8,128)(2,1)S(1)}, u32[]{:S(2)}, u32[]{:S(2)}) collective-permute-start(bf16[2,168,512]{2,1,0:T(8,128)(2,1)S(1)} %convert_element_type.175), channel_id=1, source_target_pairs={{0,32},{8,232},{16,48},{24,248},{32,64},{40,8},{48,80},{56,24},{64... | collective-permute-start | bytes 1032200 | tf_op jit(solution)/shard_map/while/body/eval_jaxpr/ppermute | solution.py:74
  219.5 8.5 %collective-permute-start = (bf16[2,168,512]{2,1,0:T(8,128)(2,1)S(1)}, bf16[2,168,512]{2,1,0:T(8,128)(2,1)S(1)}, u32[]{:S(2)}, u32[]{:S(2)}) collective-permute-start(bf16[2,168,512]{2,1,0:T(8,128)(2,1)S(1)} %convert_element_type.175), channel_id=1, source_target_pairs={{0,32},{8,232},{16,48},{24,248},{32,64},{40,8},{48,80},{56,24},{64... | collective-permute-start | bytes 1032200 | tf_op jit(solution)/shard_map/while/body/eval_jaxpr/ppermute | solution.py:74
  229.3 5.5 %collective-permute-start.6 = (bf16[168,512]{1,0:T(8,128)(2,1)S(1)}, bf16[168,512]{1,0:T(8,128)(2,1)S(1)}, u32[]{:S(2)}, u32[]{:S(2)}) collective-permute-start(bf16[168,512]{1,0:T(8,128)(2,1)S(1)} %fusion.26), channel_id=1, source_target_pairs={{0,16},{8,24},{16,0},{24,8},{32,48},{40,56},{48,32},{56,40},{64,80... | collective-permute-start | bytes 516104 | tf_op jit(solution)/shard_map/ppermute | solution.py:87

commit v4 on v2

--- a/solution.py
+++ b/solution.py
@@ -279,6 +279,14 @@
     grad_query = query_back(query_acc)[0].astype(jnp.bfloat16)
     grad_scale = float(lax.axis_size("ctx") * token_count) ** (-0.5)
     contract = (((0,), (0,)), ((), ()))
+    query_product = (
+        lax.dot_general(gathered, grad_query, contract, preferred_element_type=jnp.float32)
+        * grad_scale
+    ).astype(jnp.bfloat16)
+    query_product, pair_acc = lax.optimization_barrier((query_product, pair_acc))
+    query_weight_grad = lax.psum_scatter(
+        query_product, "ctx", scatter_dimension=0, tiled=True
+    ).astype(jnp.float32)
     own_pair = pair_acc[:, reach_blocks * token_count :]
     for distance in range(1, reach_blocks + 1):
         lower_row = (reach_blocks - distance) * token_count
@@ -294,17 +302,21 @@
     ).astype(jnp.bfloat16)
     input_partial, hidden_late = lax.optimization_barrier((input_partial, gathered))
     input_grad = exchange_sum(input_partial, "heads").astype(jnp.bfloat16)
-    summed = ctx_scatter_sum(
+    pair_weight_grad = ctx_scatter_sum(
         (
-            lax.dot_general(hidden_late, grad_cat, contract, preferred_element_type=jnp.float32)
+            lax.dot_general(
+                hidden_late,
+                jnp.concatenate([grad_key, grad_value], axis=1),
+                contract,
+                preferred_element_type=jnp.float32,
+            )
             * grad_scale
         ).astype(jnp.bfloat16),
         "ctx",
         (lax.axis_size("ctx") // 4, 2, 2),
     )
-    query_weight_grad = summed[:, :query_width]
-    key_weight_grad = summed[:, query_width : query_width + key_width]
-    value_weight_grad = summed[:, query_width + key_width :]
+    key_weight_grad = pair_weight_grad[:, :key_width]
+    value_weight_grad = pair_weight_grad[:, key_width:]
     return (attention, input_grad, query_weight_grad, key_weight_grad, value_weight_grad)
 
 

time: 231 us -> 307 us (1.33)
  the two profiles are of different devices: /device:TPU:96 before, /device:TPU:4 now
where the time goes in v4:
time: 307 us; the launch traced here: 306 us
  waiting for transfers between devices  155 us (50%)
  starting transfers between devices  50.3 us (16%)
  matrix products  40.1 us (13%)
  local copies, waits for them, and re-layouts  24.4 us (8%)
  other arithmetic  21 us (7%)
  between operations  14.6 us (5%)
    all_to_all x1, waiting for transfers between devices, gather_all(): received = lax.all_to_all(copies, axis, 0, 0)  53.5 us
    unnamed x2, waiting for transfers between devices  33.4 us
    ppermute x2, waiting for transfers between devices, pair_scatter_sum(): lax.ppermute(other.astype(jnp.bfloat16), axis, route).astype(jnp.float32)  28.9 us
    ppermute x7, waiting for transfers between devices, advance(): lax.ppermute(up.astype(jnp.bfloat16), axis, route(1)).astype(jnp.float32)  17.2 us
    ppermute x4, waiting for transfers between devices, passed_along(): return lax.ppermute(block, axis, route)  16.4 us
    ppermute x7, starting transfers between devices, advance(): lax.ppermute(down.astype(jnp.bfloat16), axis, route(-1)).astype(jnp.float32)  16.3 us
    unnamed x56, local copies, waits for them, and re-layouts  12.6 us
    ppermute x7, starting transfers between devices, advance(): lax.ppermute(up.astype(jnp.bfloat16), axis, route(1)).astype(jnp.float32)  12.2 us
  transfers between devices with their start and end apart: 23, of which 17 were waited for; matrix products, arithmetic and copies ran while one was open for 7% of the time, Pallas kernels for 0%

profile of v4, /device:TPU:4, one launch (start us, length us, event | category | flops | bytes accessed | tf_op | source)
XLA Modules:
  0.0 305.9 jit_solution(7990370296686799795)
XLA Ops:
  7.2 3.8 %broadcast_in_dim.71 = bf16[8,64,5376]{2,1,0:T(8,128)(2,1)} broadcast(bf16[64,5376]{1,0:T(8,128)(2,1)} %param.9), dimensions={1,2} | broadcast | bytes 6193152 | tf_op jit(solution)/shard_map/broadcast_in_dim | solution.py:105
  11.0 7.7 %all-to-all-start = ((bf16[8,64,5376]{2,1,0:T(8,128)(2,1)}), bf16[8,64,5376]{2,1,0:T(8,128)(2,1)}, u32[]{:S(2)}, u32[]{:S(2)}) async-start(bf16[8,64,5376]{2,1,0:T(8,128)(2,1)} %broadcast_in_dim.71), calls=%async_computation | async-start | bytes 11010048 | tf_op jit(solution)/shard_map/all_to_all | solution.py:106
  20.0 1.8 multiply_cosine_fusion
  21.8 1.2 fusion.10
  23.0 1.8 constant_dynamic-update-slice_fusion.2
  24.8 1.2 constant_dynamic-update-slice_fusion.1
  26.0 1.2 constant_dynamic-update-slice_fusion
  27.3 53.5 %all-to-all-done = bf16[8,64,5376]{2,1,0:T(8,128)(2,1)} async-done(((bf16[8,64,5376]{2,1,0:T(8,128)(2,1)}), bf16[8,64,5376]{2,1,0:T(8,128)(2,1)}, u32[]{:S(2)}, u32[]{:S(2)}) %all-to-all-start) | async-done | bytes 5505056 | tf_op jit(solution)/shard_map/all_to_all | solution.py:106
  80.8 6.8 %convolution_bitcast_fusion.2 = f32[512,512]{0,1:T(8,128)S(1)} fusion(bf16[5376,512]{1,0:T(8,128)(2,1)} %constant_dynamic-update-slice_fusion, bf16[512,5376]{1,0:T(8,128)(2,1)} %bitcast.4), kind=kOutput, calls=%fused_computation.29 | convolution fusion | flops 2818572288 | bytes 12058624 | tf_op jit(solution)/shard_map/dot_general | solution.py:224
  89.2 2.3 collective-permute-start.3
  91.6 3.4 %collective-permute-start.2 = (bf16[2,512,128]{1,2,0:T(8,128)(2,1)}, bf16[2,512,128]{1,2,0:T(8,128)(2,1)}, u32[]{:S(2)}, u32[]{:S(2)}) collective-permute-start(bf16[2,512,128]{1,2,0:T(8,128)(2,1)} %pad_maximum_fusion.1), channel_id=1, source_target_pairs={{0,16},{8,24},{16,32},{24,40},{32,48},{40,56},{48,64},{56,72},{64,... | collective-permute-start | bytes 786440 | tf_op jit(solution)/shard_map/ppermute | solution.py:18
  95.2 0.9 multiply_multiply_fusion
  96.6 3.9 %collective-permute-done.2 = bf16[2,512,128]{1,2,0:T(8,128)(2,1)} collective-permute-done((bf16[2,512,128]{1,2,0:T(8,128)(2,1)}, bf16[2,512,128]{1,2,0:T(8,128)(2,1)}, u32[]{:S(2)}, u32[]{:S(2)}) %collective-permute-start.2) | collective-permute-done | bytes 262176 | tf_op jit(solution)/shard_map/ppermute | solution.py:18
  100.5 1.2 maximum_maximum_fusion
  101.7 1.2 fusion.5
  102.9 1.3 exponential_reduce_fusion
  104.3 3.1 convolution_bitcast_fusion
  107.3 2.9 bitcast_convert_fusion
  110.2 2.0 copy.72
  112.2 2.4 multiply_reduce_fusion
  114.7 1.1 copy.73
  115.7 4.6 %fusion.7 = bf16[2,512,1536]{1,2,0:T(8,128)(2,1)S(1)} fusion(f32[1536,512,2]{1,0,2:T(8,128)} %copy-done, f32[2,512]{1,0:T(2,128)S(1)} %copy.73, f32[2,512]{1,0:T(2,128)S(1)} %log_add_fusion, pred[512,1536]{0,1:T(8,128)(4,1)S(1)} %fusion.10, bf16[2,1536,128]{1,2,0:T(8,128)(2,1)S(1)} %maximum_maximum_fusion, bf16[512,256]{1,0:T(8,128)(2,1)} %param.15), kind=kOutput, calls=%fused_computation.20 | convolution fusion | flops 412090368 | bytes 10887168 | tf_op jit(solution)/shard_map/while/body/eval_jaxpr/qkgd,jkd->kgqj/dot_general | solution.py:193
  120.3 1.4 fusion.11
  121.7 1.2 convolution_bitcast_fusion.1
  124.9 5.7 %fusion.2 = bf16[5376,256]{0,1:T(8,128)(2,1)} fusion(bf16[512,256]{0,1:T(8,128)(2,1)S(1)} %bitcast.170, bf16[512,5376]{1,0:T(8,128)(2,1)} %bitcast.4), kind=kOutput, calls=%fused_computation.9 | convolution fusion | flops 1412038656 | bytes 8519680 | tf_op jit(solution)/shard_map/dot_general | solution.py:283
  131.6 1.3 collective-permute-start.4
  132.9 1.3 collective-permute-start.5
  134.2 1.6 collective-permute-done.4
  135.9 10.8 %collective-permute-done.5 = bf16[2,512,128]{1,2,0:T(8,128)(2,1)} collective-permute-done((bf16[2,512,128]{1,2,0:T(8,128)(2,1)S(1)}, bf16[2,512,128]{1,2,0:T(8,128)(2,1)}, u32[]{:S(2)}, u32[]{:S(2)}) %collective-permute-start.5) | collective-permute-done | bytes 262176 | tf_op jit(solution)/shard_map/ppermute | solution.py:18
  146.7 1.0 convert_add_fusion.1
  148.7 7.4 %convolution_convert_fusion = bf16[512,5376]{1,0:T(8,128)(2,1)} fusion(bf16[5376,512]{1,0:T(8,128)(2,1)} %constant_dynamic-update-slice_fusion, bf16[512,128]{0,1:T(8,128)(2,1)S(1)} %fusion.44, bf16[512,128]{0,1:T(8,128)(2,1)S(1)} %fusion.45, bf16[512,256]{0,1:T(8,128)(2,1)S(1)} %bitcast.171), kind=kOutput, calls=%fused_computation.4 | convolution fusion | flops 2822897664 | bytes 11534336 | tf_op jit(solution)/shard_map/dot_general | solution.py:300
  156.1 5.9 %fusion.1 = bf16[5376,256]{1,0:T(8,128)(2,1)} fusion(bf16[512,5376]{1,0:T(8,128)(2,1)} %bitcast.4, bf16[512,128]{0,1:T(8,128)(2,1)S(1)} %fusion.44, bf16[512,128]{0,1:T(8,128)(2,1)S(1)} %fusion.45), kind=kOutput, calls=%fused_computation.8 | convolution fusion | flops 1412562944 | bytes 8519680 | tf_op jit(solution)/shard_map/dot_general | solution.py:307
  162.0 2.6 dynamic-slice_bitcast_fusion.2
  164.6 2.8 copy.82
  167.4 5.7 %all-to-all-start.1 = ((bf16[8,64,5376]{2,1,0:T(8,128)(2,1)}), bf16[8,64,5376]{2,1,0:T(8,128)(2,1)}, u32[]{:S(2)}, u32[]{:S(2)}) async-start(bf16[8,64,5376]{2,1,0:T(8,128)(2,1)} %bitcast.167), calls=%async_computation.1 | async-start | bytes 11010048 | tf_op jit(solution)/shard_map/all_to_all | solution.py:113
  173.1 2.1 convert_add_fusion
  175.3 52.6 %while.11 = (s32[]{:T(128)}, f32[2,168,128]{2,1,0:T(8,128)S(1)}, f32[2,168,128]{2,1,0:T(8,128)S(1)}, s32[]{:T(128)}, f32[8,2,168,256]{3,2,1,0:T(8,128)S(1)}, /*i...) while((s32[]{:T(128)}, f32[2,168,128]{2,1,0:T(8,128)S(1)}, ...), condition=%wide.region_9.10_spmd, body=%wide.region_8.9_spmd.sunk | while | flops 258082 | bytes 3441171 | solution.py:79
  175.4 3.7 %collective-permute-start = (bf16[2,168,128]{2,1,0:T(8,128)(2,1)S(1)}, bf16[2,168,128]{2,1,0:T(8,128)(2,1)S(1)}, u32[]{:S(2)}, u32[]{:S(2)}) collective-permute-start(bf16[2,168,128]{2,1,0:T(8,128)(2,1)S(1)} %convert_element_type.215), channel_id=1, source_target_pairs={{0,32},{8,40},{16,48},{24,56},{32,64},{40,72},{48,80},{56,88},{64,... | collective-permute-start | bytes 258056 | tf_op jit(solution)/shard_map/while/body/eval_jaxpr/ppermute | solution.py:75
  179.1 4.0 %collective-permute-start.1 = (bf16[2,168,128]{2,1,0:T(8,128)(2,1)S(1)}, bf16[2,168,128]{2,1,0:T(8,128)(2,1)S(1)}, u32[]{:S(2)}, u32[]{:S(2)}) collective-permute-start(bf16[2,168,128]{2,1,0:T(8,128)(2,1)S(1)} %convert_element_type.216), channel_id=1, source_target_pairs={{0,224},{8,232},{16,240},{24,248},{32,0},{40,8},{48,16},{56,24},{6... | collective-permute-start | bytes 258056 | tf_op jit(solution)/shard_map/while/body/eval_jaxpr/ppermute | solution.py:76
  183.2 2.6 collective-permute-done
  186.0 3.6 %collective-permute-start.1 = (bf16[2,168,128]{2,1,0:T(8,128)(2,1)S(1)}, bf16[2,168,128]{2,1,0:T(8,128)(2,1)S(1)}, u32[]{:S(2)}, u32[]{:S(2)}) collective-permute-start(bf16[2,168,128]{2,1,0:T(8,128)(2,1)S(1)} %convert_element_type.216), channel_id=1, source_target_pairs={{0,224},{8,232},{16,240},{24,248},{32,0},{40,8},{48,16},{56,24},{6... | collective-permute-start | bytes 258056 | tf_op jit(solution)/shard_map/while/body/eval_jaxpr/ppermute | solution.py:76
  189.6 2.3 collective-permute-done
  192.0 1.3 collective-permute-done.1
  193.3 3.0 collective-permute-start
  196.8 2.3 collective-permute-done
  199.1 2.5 collective-permute-done.1
  201.7 1.9 collective-permute-start
  203.6 1.5 collective-permute-start.1
  205.1 2.3 collective-permute-done
  207.5 0.8 collective-permute-done.1
  208.4 1.7 collective-permute-start
  210.0 1.7 collective-permute-start.1
  211.8 2.5 collective-permute-done
  214.3 1.2 collective-permute-done.1
  215.5 1.0 collective-permute-start
  216.6 2.4 collective-permute-start.1
  219.0 2.9 collective-permute-done
  222.7 2.8 collective-permute-start.1
  225.6 2.3 collective-permute-done
  228.1 1.8 copy.62
  229.9 28.9 %collective-permute-done.7 = bf16[168,256]{1,0:T(8,128)(2,1)S(1)} collective-permute-done((bf16[168,256]{1,0:T(8,128)(2,1)S(1)}, bf16[168,256]{1,0:T(8,128)(2,1)S(1)}, u32[]{:S(2)}, u32[]{:S(2)}) %collective-permute-start.7) | collective-permute-done | bytes 86048 | tf_op jit(solution)/shard_map/ppermute | solution.py:90
  259.5 4.4 %reduce_sum.71 = bf16[64,5376]{1,0:T(8,128)(2,1)} reduce(bf16[8,64,5376]{2,1,0:T(8,128)(2,1)} %all-to-all-done.1, bf16[]{:T(256)} %constant.224.clone.1), dimensions={0}, to_apply=%region_6.7 | reduce | flops 2408448 | bytes 6193154 | tf_op jit(solution)/shard_map/reduce_sum | solution.py:114
  263.9 33.4 %reduce-scatter.4.cloned.1.call-done = bf16[168,256]{1,0:T(8,128)(2,1)} async-done(((bf16[5376,256]{1,0:T(8,128)(2,1)}), bf16[168,256]{1,0:T(8,128)(2,1)}) %reduce-scatter.4.cloned.1.call-update) | async-done | bytes 86032
  297.3 1.0 copy.83
  (139 shorter events, 11.0 us)
Async XLA Ops:
  11.0 7.7 %copy-start.12 = (bf16[512,256]{1,0:T(8,128)(2,1)S(1)}, bf16[512,256]{1,0:T(8,128)(2,1)}, u32[]{:S(2)}) copy-start(bf16[512,256]{1,0:T(8,128)(2,1)} %param.15) | copy-start | bytes 786436
  11.0 12.0 %copy-start.1 = (bf16[5376,256]{1,0:T(8,128)(2,1)S(1)}, bf16[5376,256]{1,0:T(8,128)(2,1)}, u32[]{:S(2)}) copy-start(bf16[5376,256]{1,0:T(8,128)(2,1)} %param.10) | copy-start | bytes 8257540
  11.0 69.8 %all-to-all-start = ((bf16[8,64,5376]{2,1,0:T(8,128)(2,1)}), bf16[8,64,5376]{2,1,0:T(8,128)(2,1)}, u32[]{:S(2)}, u32[]{:S(2)}) async-start(bf16[8,64,5376]{2,1,0:T(8,128)(2,1)} %broadcast_in_dim.71), calls=%async_computation | async-start | bytes 11010048 | tf_op jit(solution)/shard_map/all_to_all | solution.py:106
  18.7 278.6 %reduce-scatter.4.cloned.1.call-start = ((), (), s32[]{:S(2)}) async-start(), calls=%async_computation.3 | async-start | bytes 2838528
  19.5 5.3 %copy-start.8 = (bf16[5376,128]{1,0:T(8,128)(2,1)S(1)}, bf16[5376,128]{1,0:T(8,128)(2,1)}, u32[]{:S(2)}) copy-start(bf16[5376,128]{1,0:T(8,128)(2,1)} %param.11) | copy-start | bytes 4128772
  19.5 6.6 %copy-start.9 = (bf16[5376,128]{1,0:T(8,128)(2,1)S(1)}, bf16[5376,128]{1,0:T(8,128)(2,1)}, u32[]{:S(2)}) copy-start(bf16[5376,128]{1,0:T(8,128)(2,1)} %param.12) | copy-start | bytes 4128772
  19.5 0.5 copy-start.18
  80.8 7.0 %copy-start.21 = (f32[128]{0:T(128)S(1)}, f32[128]{0:T(128)}, u32[]{:S(2)}) copy-start(f32[128]{0:T(128)} %param.14) | copy-start | bytes 1540
  80.8 7.1 %copy-start.19 = (f32[64]{0:T(128)S(1)}, f32[64]{0:T(128)}, u32[]{:S(2)}) copy-start(f32[64]{0:T(128)} %copy-done.18) | copy-start | bytes 772
  87.6 8.5 %copy-start.3 = (f32[512,64]{1,0:T(8,128)S(1)}, f32[512,64]{1,0:T(8,128)}, u32[]{:S(2)}) copy-start(f32[512,64]{1,0:T(8,128)} %get-tuple-element.244) | copy-start | bytes 393220
  87.6 8.5 %copy-start.4 = (f32[512,64]{1,0:T(8,128)S(1)}, f32[512,64]{1,0:T(8,128)}, u32[]{:S(2)}) copy-start(f32[512,64]{1,0:T(8,128)} %get-tuple-element.245) | copy-start | bytes 393220
  87.7 7.3 %copy-start.16 = (f32[512]{0:T(512)}, f32[512]{0:T(512)S(1)}, u32[]{:S(2)}) copy-start(f32[512]{0:T(512)S(1)} %multiply_reduce_fusion.3) | copy-start | bytes 6148
  88.5 6.5 %copy-start.10 = (bf16[1,512,128]{1,2,0:T(8,128)(2,1)}, bf16[1,512,128]{1,2,0:T(8,128)(2,1)S(1)}, u32[]{:S(2)}) copy-start(bf16[1,512,128]{1,2,0:T(8,128)(2,1)S(1)} %maximum_bitcast_fusion) | copy-start | bytes 393220
  89.2 7.4 %collective-permute-start.3 = (bf16[2,512,128]{1,2,0:T(8,128)(2,1)}, bf16[2,512,128]{1,2,0:T(8,128)(2,1)}, u32[]{:S(2)}, u32[]{:S(2)}) collective-permute-start(bf16[2,512,128]{1,2,0:T(8,128)(2,1)} %pad_maximum_fusion.1), channel_id=1, source_target_pairs={{0,8},{8,16},{16,24},{24,32},{32,40},{40,48},{48,56},{56,64},{64,7... | collective-permute-start | bytes 786440 | tf_op jit(solution)/shard_map/ppermute | solution.py:18
  91.6 9.0 %collective-permute-start.2 = (bf16[2,512,128]{1,2,0:T(8,128)(2,1)}, bf16[2,512,128]{1,2,0:T(8,128)(2,1)}, u32[]{:S(2)}, u32[]{:S(2)}) collective-permute-start(bf16[2,512,128]{1,2,0:T(8,128)(2,1)} %pad_maximum_fusion.1), channel_id=1, source_target_pairs={{0,16},{8,24},{16,32},{24,40},{32,48},{40,56},{48,64},{56,72},{64,... | collective-permute-start | bytes 786440 | tf_op jit(solution)/shard_map/ppermute | solution.py:18
  96.6 5.1 %copy-start.6 = (bf16[512,2,128]{2,0,1:T(8,128)(2,1)}, bf16[512,2,128]{2,0,1:T(8,128)(2,1)S(1)}, u32[]{:S(2)}) copy-start(bf16[512,2,128]{2,0,1:T(8,128)(2,1)S(1)} %fusion.13) | copy-start | bytes 786436
  101.7 2.6 copy-start.13
  102.9 4.4 %copy-start = (f32[1536,512,2]{1,0,2:T(8,128)}, f32[1536,512,2]{1,0,2:T(8,128)S(1)}, u32[]{:S(2)}) copy-start(f32[1536,512,2]{1,0,2:T(8,128)S(1)} %get-tuple-element.247) | copy-start | bytes 18874372
  115.7 6.0 %copy-start.7 = (bf16[512,2,128]{2,0,1:T(8,128)(2,1)S(1)}, bf16[512,2,128]{2,0,1:T(8,128)(2,1)}, u32[]{:S(2)}) copy-start(bf16[512,2,128]{2,0,1:T(8,128)(2,1)} %copy-done.6) | copy-start | bytes 786436
  120.3 2.6 copy-start.5
  120.3 2.9 copy-start.23
  124.2 0.7 copy-start.14
  124.2 6.4 %copy-start.11 = (f32[1,1536,128]{1,2,0:T(8,128)S(1)}, f32[1,1536,128]{1,2,0:T(8,128)}, u32[]{:S(2)}) copy-start(f32[1,1536,128]{1,2,0:T(8,128)} %convolution_bitcast_fusion) | copy-start | bytes 2359300
  130.6 17.2 %copy-start.20 = (f32[64]{0:T(128)S(1)}, f32[64]{0:T(128)}, u32[]{:S(2)}) copy-start(f32[64]{0:T(128)} %copy-done.18) | copy-start | bytes 772
  130.6 17.8 %copy-start.22 = (f32[128]{0:T(128)S(1)}, f32[128]{0:T(128)}, u32[]{:S(2)}) copy-start(f32[128]{0:T(128)} %param.14) | copy-start | bytes 1540
  130.6 17.9 %copy-start.17 = (f32[512]{0:T(512)S(1)}, f32[512]{0:T(512)}, u32[]{:S(2)}) copy-start(f32[512]{0:T(512)} %copy-done.16) | copy-start | bytes 6148
  130.8 17.9 %copy-start.15 = (bf16[512,2,128]{0,2,1:T(8,128)(2,1)S(1)}, bf16[512,2,128]{0,2,1:T(8,128)(2,1)}, u32[]{:S(2)}) copy-start(bf16[512,2,128]{0,2,1:T(8,128)(2,1)} %copy-done.14) | copy-start | bytes 786436
  131.6 4.3 %collective-permute-start.4 = (bf16[2,512,128]{1,2,0:T(8,128)(2,1)}, bf16[2,512,128]{1,2,0:T(8,128)(2,1)S(1)}, u32[]{:S(2)}, u32[]{:S(2)}) collective-permute-start(bf16[2,512,128]{1,2,0:T(8,128)(2,1)} %get-tuple-element.236), channel_id=1, source_target_pairs={{8,0},{16,8},{24,16},{32,24},{40,32},{48,40},{56,48},{64,56},{72,6... | collective-permute-start | bytes 786440 | tf_op jit(solution)/shard_map/ppermute | solution.py:18
  132.9 13.8 %collective-permute-start.5 = (bf16[2,512,128]{1,2,0:T(8,128)(2,1)S(1)}, bf16[2,512,128]{1,2,0:T(8,128)(2,1)}, u32[]{:S(2)}, u32[]{:S(2)}) collective-permute-start(bf16[2,512,128]{1,2,0:T(8,128)(2,1)S(1)} %get-tuple-element.237), channel_id=1, source_target_pairs={{16,0},{24,8},{32,16},{40,24},{48,32},{56,40},{64,48},{72,56},{80,... | collective-permute-start | bytes 786440 | tf_op jit(solution)/shard_map/ppermute | solution.py:18
  156.1 8.5 %copy-start.2 = (bf16[5376,256]{0,1:T(8,128)(2,1)S(1)}, bf16[5376,256]{0,1:T(8,128)(2,1)}, u32[]{:S(2)}) copy-start(bf16[5376,256]{0,1:T(8,128)(2,1)} %fusion.2) | copy-start | bytes 8257540
  164.6 8.5 %collective-permute-start.6 = (bf16[8,2,168,256]{3,2,1,0:T(8,128)(2,1)}, bf16[8,2,168,256]{3,2,1,0:T(8,128)(2,1)}, u32[]{:S(2)}, u32[]{:S(2)}) collective-permute-start(bf16[8,2,168,256]{3,2,1,0:T(8,128)(2,1)} %dynamic-slice_bitcast_fusion.2), channel_id=1, source_target_pairs={{0,8},{8,0},{16,24},{24,16},{32,40},{40,32},{48,56},{56,48},{64,72... | collective-permute-start | bytes 4128776 | tf_op jit(solution)/shard_map/ppermute | solution.py:90
  167.4 92.1 %all-to-all-start.1 = ((bf16[8,64,5376]{2,1,0:T(8,128)(2,1)}), bf16[8,64,5376]{2,1,0:T(8,128)(2,1)}, u32[]{:S(2)}, u32[]{:S(2)}) async-start(bf16[8,64,5376]{2,1,0:T(8,128)(2,1)} %bitcast.167), calls=%async_computation.1 | async-start | bytes 11010048 | tf_op jit(solution)/shard_map/all_to_all | solution.py:113
  175.4 10.4 %collective-permute-start = (bf16[2,168,128]{2,1,0:T(8,128)(2,1)S(1)}, bf16[2,168,128]{2,1,0:T(8,128)(2,1)S(1)}, u32[]{:S(2)}, u32[]{:S(2)}) collective-permute-start(bf16[2,168,128]{2,1,0:T(8,128)(2,1)S(1)} %convert_element_type.215), channel_id=1, source_target_pairs={{0,32},{8,40},{16,48},{24,56},{32,64},{40,72},{48,80},{56,88},{64,... | collective-permute-start | bytes 258056 | tf_op jit(solution)/shard_map/while/body/eval_jaxpr/ppermute | solution.py:75
  179.1 6.7 %collective-permute-start.1 = (bf16[2,168,128]{2,1,0:T(8,128)(2,1)S(1)}, bf16[2,168,128]{2,1,0:T(8,128)(2,1)S(1)}, u32[]{:S(2)}, u32[]{:S(2)}) collective-permute-start(bf16[2,168,128]{2,1,0:T(8,128)(2,1)S(1)} %convert_element_type.216), channel_id=1, source_target_pairs={{0,224},{8,232},{16,240},{24,248},{32,0},{40,8},{48,16},{56,24},{6... | collective-permute-start | bytes 258056 | tf_op jit(solution)/shard_map/while/body/eval_jaxpr/ppermute | solution.py:76
  185.9 6.0 %collective-permute-start = (bf16[2,168,128]{2,1,0:T(8,128)(2,1)S(1)}, bf16[2,168,128]{2,1,0:T(8,128)(2,1)S(1)}, u32[]{:S(2)}, u32[]{:S(2)}) collective-permute-start(bf16[2,168,128]{2,1,0:T(8,128)(2,1)S(1)} %convert_element_type.215), channel_id=1, source_target_pairs={{0,32},{8,40},{16,48},{24,56},{32,64},{40,72},{48,80},{56,88},{64,... | collective-permute-start | bytes 258056 | tf_op jit(solution)/shard_map/while/body/eval_jaxpr/ppermute | solution.py:75
  186.0 7.2 %collective-permute-start.1 = (bf16[2,168,128]{2,1,0:T(8,128)(2,1)S(1)}, bf16[2,168,128]{2,1,0:T(8,128)(2,1)S(1)}, u32[]{:S(2)}, u32[]{:S(2)}) collective-permute-start(bf16[2,168,128]{2,1,0:T(8,128)(2,1)S(1)} %convert_element_type.216), channel_id=1, source_target_pairs={{0,224},{8,232},{16,240},{24,248},{32,0},{40,8},{48,16},{56,24},{6... | collective-permute-start | bytes 258056 | tf_op jit(solution)/shard_map/while/body/eval_jaxpr/ppermute | solution.py:76
  193.3 5.8 %collective-permute-start = (bf16[2,168,128]{2,1,0:T(8,128)(2,1)S(1)}, bf16[2,168,128]{2,1,0:T(8,128)(2,1)S(1)}, u32[]{:S(2)}, u32[]{:S(2)}) collective-permute-start(bf16[2,168,128]{2,1,0:T(8,128)(2,1)S(1)} %convert_element_type.215), channel_id=1, source_target_pairs={{0,32},{8,40},{16,48},{24,56},{32,64},{40,72},{48,80},{56,88},{64,... | collective-permute-start | bytes 258056 | tf_op jit(solution)/shard_map/while/body/eval_jaxpr/ppermute | solution.py:75
  196.4 5.2 %collective-permute-start.1 = (bf16[2,168,128]{2,1,0:T(8,128)(2,1)S(1)}, bf16[2,168,128]{2,1,0:T(8,128)(2,1)S(1)}, u32[]{:S(2)}, u32[]{:S(2)}) collective-permute-start(bf16[2,168,128]{2,1,0:T(8,128)(2,1)S(1)} %convert_element_type.216), channel_id=1, source_target_pairs={{0,224},{8,232},{16,240},{24,248},{32,0},{40,8},{48,16},{56,24},{6... | collective-permute-start | bytes 258056 | tf_op jit(solution)/shard_map/while/body/eval_jaxpr/ppermute | solution.py:76
  201.7 5.8 %collective-permute-start = (bf16[2,168,128]{2,1,0:T(8,128)(2,1)S(1)}, bf16[2,168,128]{2,1,0:T(8,128)(2,1)S(1)}, u32[]{:S(2)}, u32[]{:S(2)}) collective-permute-start(bf16[2,168,128]{2,1,0:T(8,128)(2,1)S(1)} %convert_element_type.215), channel_id=1, source_target_pairs={{0,32},{8,40},{16,48},{24,56},{32,64},{40,72},{48,80},{56,88},{64,... | collective-permute-start | bytes 258056 | tf_op jit(solution)/shard_map/while/body/eval_jaxpr/ppermute | solution.py:75
  203.6 4.7 %collective-permute-start.1 = (bf16[2,168,128]{2,1,0:T(8,128)(2,1)S(1)}, bf16[2,168,128]{2,1,0:T(8,128)(2,1)S(1)}, u32[]{:S(2)}, u32[]{:S(2)}) collective-permute-start(bf16[2,168,128]{2,1,0:T(8,128)(2,1)S(1)} %convert_element_type.216), channel_id=1, source_target_pairs={{0,224},{8,232},{16,240},{24,248},{32,0},{40,8},{48,16},{56,24},{6... | collective-permute-start | bytes 258056 | tf_op jit(solution)/shard_map/while/body/eval_jaxpr/ppermute | solution.py:76
  208.4 5.9 %collective-permute-start = (bf16[2,168,128]{2,1,0:T(8,128)(2,1)S(1)}, bf16[2,168,128]{2,1,0:T(8,128)(2,1)S(1)}, u32[]{:S(2)}, u32[]{:S(2)}) collective-permute-start(bf16[2,168,128]{2,1,0:T(8,128)(2,1)S(1)} %convert_element_type.215), channel_id=1, source_target_pairs={{0,32},{8,40},{16,48},{24,56},{32,64},{40,72},{48,80},{56,88},{64,... | collective-permute-start | bytes 258056 | tf_op jit(solution)/shard_map/while/body/eval_jaxpr/ppermute | solution.py:75
  210.0 5.4 %collective-permute-start.1 = (bf16[2,168,128]{2,1,0:T(8,128)(2,1)S(1)}, bf16[2,168,128]{2,1,0:T(8,128)(2,1)S(1)}, u32[]{:S(2)}, u32[]{:S(2)}) collective-permute-start(bf16[2,168,128]{2,1,0:T(8,128)(2,1)S(1)} %convert_element_type.216), channel_id=1, source_target_pairs={{0,224},{8,232},{16,240},{24,248},{32,0},{40,8},{48,16},{56,24},{6... | collective-permute-start | bytes 258056 | tf_op jit(solution)/shard_map/while/body/eval_jaxpr/ppermute | solution.py:76
  215.5 6.4 %collective-permute-start = (bf16[2,168,128]{2,1,0:T(8,128)(2,1)S(1)}, bf16[2,168,128]{2,1,0:T(8,128)(2,1)S(1)}, u32[]{:S(2)}, u32[]{:S(2)}) collective-permute-start(bf16[2,168,128]{2,1,0:T(8,128)(2,1)S(1)} %convert_element_type.215), channel_id=1, source_target_pairs={{0,32},{8,40},{16,48},{24,56},{32,64},{40,72},{48,80},{56,88},{64,... | collective-permute-start | bytes 258056 | tf_op jit(solution)/shard_map/while/body/eval_jaxpr/ppermute | solution.py:75
  216.6 5.4 %collective-permute-start.1 = (bf16[2,168,128]{2,1,0:T(8,128)(2,1)S(1)}, bf16[2,168,128]{2,1,0:T(8,128)(2,1)S(1)}, u32[]{:S(2)}, u32[]{:S(2)}) collective-permute-start(bf16[2,168,128]{2,1,0:T(8,128)(2,1)S(1)} %convert_element_type.216), channel_id=1, source_target_pairs={{0,224},{8,232},{16,240},{24,248},{32,0},{40,8},{48,16},{56,24},{6... | collective-permute-start | bytes 258056 | tf_op jit(solution)/shard_map/while/body/eval_jaxpr/ppermute | solution.py:76
  222.0 5.9 %collective-permute-start = (bf16[2,168,128]{2,1,0:T(8,128)(2,1)S(1)}, bf16[2,168,128]{2,1,0:T(8,128)(2,1)S(1)}, u32[]{:S(2)}, u32[]{:S(2)}) collective-permute-start(bf16[2,168,128]{2,1,0:T(8,128)(2,1)S(1)} %convert_element_type.215), channel_id=1, source_target_pairs={{0,32},{8,40},{16,48},{24,56},{32,64},{40,72},{48,80},{56,88},{64,... | collective-permute-start | bytes 258056 | tf_op jit(solution)/shard_map/while/body/eval_jaxpr/ppermute | solution.py:75
  222.7 5.2 %collective-permute-start.1 = (bf16[2,168,128]{2,1,0:T(8,128)(2,1)S(1)}, bf16[2,168,128]{2,1,0:T(8,128)(2,1)S(1)}, u32[]{:S(2)}, u32[]{:S(2)}) collective-permute-start(bf16[2,168,128]{2,1,0:T(8,128)(2,1)S(1)} %convert_element_type.216), channel_id=1, source_target_pairs={{0,224},{8,232},{16,240},{24,248},{32,0},{40,8},{48,16},{56,24},{6... | collective-permute-start | bytes 258056 | tf_op jit(solution)/shard_map/while/body/eval_jaxpr/ppermute | solution.py:76
  228.0 30.8 %collective-permute-start.7 = (bf16[168,256]{1,0:T(8,128)(2,1)S(1)}, bf16[168,256]{1,0:T(8,128)(2,1)S(1)}, u32[]{:S(2)}, u32[]{:S(2)}) collective-permute-start(bf16[168,256]{1,0:T(8,128)(2,1)S(1)} %fusion.46), channel_id=1, source_target_pairs={{0,16},{8,24},{16,0},{24,8},{32,48},{40,56},{48,32},{56,40},{64,80... | collective-permute-start | bytes 258056 | tf_op jit(solution)/shard_map/ppermute | solution.py:90
Sparse Core Ops, SparseCore 0:
  167.5 129.6 reduce-scatter.3

commit v5 on v4

--- a/solution.py
+++ b/solution.py
@@ -284,9 +284,7 @@
         * grad_scale
     ).astype(jnp.bfloat16)
     query_product, pair_acc = lax.optimization_barrier((query_product, pair_acc))
-    query_weight_grad = lax.psum_scatter(
-        query_product, "ctx", scatter_dimension=0, tiled=True
-    ).astype(jnp.float32)
+    query_weight_grad = exchange_sum(query_product, "ctx")
     own_pair = pair_acc[:, reach_blocks * token_count :]
     for distance in range(1, reach_blocks + 1):
         lower_row = (reach_blocks - distance) * token_count
@@ -300,7 +298,9 @@
     input_partial = lax.dot_general(
         grad_cat, weight_cat, back_contract, preferred_element_type=jnp.float32
     ).astype(jnp.bfloat16)
-    input_partial, hidden_late = lax.optimization_barrier((input_partial, gathered))
+    input_partial, hidden_late, query_weight_grad = lax.optimization_barrier(
+        (input_partial, gathered, query_weight_grad)
+    )
     input_grad = exchange_sum(input_partial, "heads").astype(jnp.bfloat16)
     pair_weight_grad = ctx_scatter_sum(
         (

time: 307 us -> 305 us (level)
  the two profiles are of different devices: /device:TPU:4 before, /device:TPU:96 now
where the time goes in v5:
time: 305 us; the launch traced here: 303 us
  waiting for transfers between devices  163 us (53%)
  starting transfers between devices  50.1 us (16%)
  matrix products  38.5 us (13%)
  local copies, waits for them, and re-layouts  26.2 us (9%)
  other arithmetic  24.3 us (8%)
    ppermute x4, waiting for transfers between devices, passed_along(): return lax.ppermute(block, axis, route)  68.6 us
    all_to_all x1, waiting for transfers between devices, gather_all(): received = lax.all_to_all(copies, axis, 0, 0)  51.2 us
    ppermute x7, waiting for transfers between devices, advance(): lax.ppermute(up.astype(jnp.bfloat16), axis, route(1)).astype(jnp.float32)  16.4 us
    ppermute x2, waiting for transfers between devices, pair_scatter_sum(): lax.ppermute(other.astype(jnp.bfloat16), axis, route).astype(jnp.float32)  14.1 us
    all_to_all x2, starting transfers between devices, exchange_sum(): received = lax.all_to_all(pieces, axis, 0, 0)  13.8 us
    ppermute x7, waiting for transfers between devices, advance(): lax.ppermute(down.astype(jnp.bfloat16), axis, route(-1)).astype(jnp.float32)  12.3 us
    ppermute x7, starting transfers between devices, advance(): lax.ppermute(down.astype(jnp.bfloat16), axis, route(-1)).astype(jnp.float32)  11.6 us
    unnamed x19, local copies, waits for them, and re-layouts  10.9 us
  transfers between devices with their start and end apart: 23, of which 20 were waited for; matrix products, arithmetic and copies ran while one was open for 11% of the time, Pallas kernels for 0%

profile of v5, /device:TPU:96, one launch (start us, length us, event | category | flops | bytes accessed | tf_op | source)
XLA Modules:
  0.0 303.3 jit_solution(8984220724633140726)
XLA Ops:
  0.6 3.9 %broadcast_in_dim.71 = bf16[8,64,5376]{2,1,0:T(8,128)(2,1)} broadcast(bf16[64,5376]{1,0:T(8,128)(2,1)} %param.9), dimensions={1,2} | broadcast | bytes 6193152 | tf_op jit(solution)/shard_map/broadcast_in_dim | solution.py:105
  4.5 7.1 %all-to-all-start = ((bf16[8,64,5376]{2,1,0:T(8,128)(2,1)}), bf16[8,64,5376]{2,1,0:T(8,128)(2,1)}, u32[]{:S(2)}, u32[]{:S(2)}) async-start(bf16[8,64,5376]{2,1,0:T(8,128)(2,1)} %broadcast_in_dim.71), calls=%async_computation | async-start | bytes 11010048 | tf_op jit(solution)/shard_map/all_to_all | solution.py:106
  13.4 1.2 fusion.10
  14.6 3.5 %constant_dynamic-update-slice_fusion.2 = bf16[5376,512]{1,0:T(8,128)(2,1)} fusion(bf16[5376,256]{1,0:T(8,128)(2,1)} %param.10), kind=kLoop, calls=%fused_computation.105 | loop fusion | bytes 5505024
  18.1 2.6 constant_dynamic-update-slice_fusion.1
  20.7 2.6 constant_dynamic-update-slice_fusion
  23.4 51.2 %all-to-all-done = bf16[8,64,5376]{2,1,0:T(8,128)(2,1)} async-done(((bf16[8,64,5376]{2,1,0:T(8,128)(2,1)}), bf16[8,64,5376]{2,1,0:T(8,128)(2,1)}, u32[]{:S(2)}, u32[]{:S(2)}) %all-to-all-start) | async-done | bytes 5505056 | tf_op jit(solution)/shard_map/all_to_all | solution.py:106
  74.6 6.8 %convolution_bitcast_fusion.2 = f32[512,512]{0,1:T(8,128)S(1)} fusion(bf16[5376,512]{1,0:T(8,128)(2,1)} %constant_dynamic-update-slice_fusion, bf16[512,5376]{1,0:T(8,128)(2,1)} %bitcast.4), kind=kOutput, calls=%fused_computation.30 | convolution fusion | flops 2818572288 | bytes 12058624 | tf_op jit(solution)/shard_map/dot_general | solution.py:224
  82.3 1.9 collective-permute-start.3
  84.2 2.7 collective-permute-start.2
  87.9 3.4 %collective-permute-done.3 = bf16[2,512,128]{1,2,0:T(8,128)(2,1)} collective-permute-done((bf16[2,512,128]{1,2,0:T(8,128)(2,1)S(1)}, bf16[2,512,128]{1,2,0:T(8,128)(2,1)}, u32[]{:S(2)}, u32[]{:S(2)}) %collective-permute-start.3) | collective-permute-done | bytes 262176 | tf_op jit(solution)/shard_map/ppermute | solution.py:18
  91.3 5.0 %collective-permute-done.2 = bf16[2,512,128]{1,2,0:T(8,128)(2,1)} collective-permute-done((bf16[2,512,128]{1,2,0:T(8,128)(2,1)S(1)}, bf16[2,512,128]{1,2,0:T(8,128)(2,1)}, u32[]{:S(2)}, u32[]{:S(2)}) %collective-permute-start.2) | collective-permute-done | bytes 262176 | tf_op jit(solution)/shard_map/ppermute | solution.py:18
  96.3 1.1 maximum_maximum_fusion
  97.4 1.2 fusion.5
  98.6 1.3 exponential_reduce_fusion
  99.9 3.0 %convolution_bitcast_fusion = f32[1,1536,128]{1,2,0:T(8,128)} fusion(f32[1536,512,2]{1,0,2:T(8,128)S(1)} %get-tuple-element.244, f32[2,512]{1,0:T(2,128)S(1)} %log_add_fusion, pred[512,1536]{0,1:T(8,128)(4,1)S(1)} %fusion.10, bf16[512,256]{1,0:T(8,128)(2,1)S(1)} %copy-done.4), kind=kOutput, calls=%fused_computation.26 | convolution fusion | flops 408944640 | bytes 8130560 | tf_op jit(solution)/shard_map/while/body/eval_jaxpr/kgqj,qkgd->jkd/dot_general | solution.py:203
  103.0 2.9 bitcast_convert_fusion
  105.8 1.3 copy.54
  107.1 2.3 multiply_reduce_fusion
  110.5 4.6 %fusion.7 = bf16[2,512,1536]{1,2,0:T(8,128)(2,1)S(1)} fusion(f32[1536,512,2]{1,0,2:T(8,128)} %copy-done, f32[2,512]{1,0:T(2,128)S(1)} %copy.55, f32[2,512]{1,0:T(2,128)S(1)} %log_add_fusion, pred[512,1536]{0,1:T(8,128)(4,1)S(1)} %fusion.10, bf16[2,1536,128]{1,2,0:T(8,128)(2,1)S(1)} %maximum_maximum_fusion, bf16[512,256]{1,0:T(8,128)(2,1)} %param.15), kind=kOutput, calls=%fused_computation.21 | convolution fusion | flops 412090368 | bytes 10887168 | tf_op jit(solution)/shard_map/while/body/eval_jaxpr/qkgd,jkd->kgqj/dot_general | solution.py:193
  115.0 1.4 fusion.11
  116.4 1.2 convolution_bitcast_fusion.1
  118.9 5.8 %fusion.2 = bf16[5376,256]{0,1:T(8,128)(2,1)} fusion(bf16[512,256]{0,1:T(8,128)(2,1)S(1)} %bitcast.173, bf16[512,5376]{1,0:T(8,128)(2,1)} %bitcast.4), kind=kOutput, calls=%fused_computation.9 | convolution fusion | flops 1412038656 | bytes 8519680 | tf_op jit(solution)/shard_map/dot_general | solution.py:283
  124.7 1.3 pad_maximum_fusion
  126.0 4.6 %copy.43 = bf16[5376,256]{1,0:T(8,128)(2,1)} copy(bf16[5376,256]{0,1:T(8,128)(2,1)} %fusion.2) | data formatting | bytes 5505024 | tf_op jit(solution)/shard_map/optimization_barrier | solution.py:286
  130.6 9.0 %all-to-all-start.1 = ((bf16[32,168,256]{2,1,0:T(8,128)(2,1)}), bf16[32,168,256]{2,1,0:T(8,128)(2,1)S(1)}, u32[]{:S(2)}, u32[]{:S(2)}) async-start(bf16[32,168,256]{2,1,0:T(8,128)(2,1)} %bitcast.167), calls=%async_computation.1 | async-start | bytes 5505024 | tf_op jit(solution)/shard_map/all_to_all | solution.py:113
  139.6 1.5 convert.21
  141.9 3.1 %collective-permute-start.4 = (bf16[2,512,128]{1,2,0:T(8,128)(2,1)}, bf16[2,512,128]{1,2,0:T(8,128)(2,1)S(1)}, u32[]{:S(2)}, u32[]{:S(2)}) collective-permute-start(bf16[2,512,128]{1,2,0:T(8,128)(2,1)} %get-tuple-element.233), channel_id=1, source_target_pairs={{8,0},{16,8},{24,16},{32,24},{40,32},{48,40},{56,48},{64,56},{72,6... | collective-permute-start | bytes 786440 | tf_op jit(solution)/shard_map/ppermute | solution.py:18
  145.0 2.5 collective-permute-start.5
  147.5 57.5 %collective-permute-done.4 = bf16[2,512,128]{1,2,0:T(8,128)(2,1)S(1)} collective-permute-done((bf16[2,512,128]{1,2,0:T(8,128)(2,1)}, bf16[2,512,128]{1,2,0:T(8,128)(2,1)S(1)}, u32[]{:S(2)}, u32[]{:S(2)}) %collective-permute-start.4) | collective-permute-done | bytes 262176 | tf_op jit(solution)/shard_map/ppermute | solution.py:18
  205.0 2.7 collective-permute-done.5
  207.7 1.2 convert_add_fusion.1
  210.6 1.1 fusion.45
  211.7 7.5 %convolution_convert_fusion = bf16[512,5376]{1,0:T(8,128)(2,1)} fusion(bf16[5376,512]{1,0:T(8,128)(2,1)} %constant_dynamic-update-slice_fusion, bf16[512,128]{0,1:T(8,128)(2,1)S(1)} %fusion.44, bf16[512,128]{0,1:T(8,128)(2,1)S(1)} %fusion.45, bf16[512,256]{0,1:T(8,128)(2,1)S(1)} %bitcast.174), kind=kOutput, calls=%fused_computation.4 | convolution fusion | flops 2822897664 | bytes 11534336 | tf_op jit(solution)/shard_map/dot_general | solution.py:298
  220.2 4.2 %fusion.1 = bf16[5376,256]{1,0:T(8,128)(2,1)S(1)} fusion(bf16[512,5376]{1,0:T(8,128)(2,1)} %bitcast.4, bf16[512,128]{0,1:T(8,128)(2,1)S(1)} %fusion.44, bf16[512,128]{0,1:T(8,128)(2,1)S(1)} %fusion.45), kind=kOutput, calls=%fused_computation.8 | convolution fusion | flops 1412562944 | bytes 8519680 | tf_op jit(solution)/shard_map/dot_general | solution.py:307
  224.5 1.7 copy-done.2
  226.7 4.8 %all-to-all-start.2 = ((bf16[8,64,5376]{2,1,0:T(8,128)(2,1)}), bf16[8,64,5376]{2,1,0:T(8,128)(2,1)}, u32[]{:S(2)}, u32[]{:S(2)}) async-start(bf16[8,64,5376]{2,1,0:T(8,128)(2,1)} %bitcast.168), calls=%async_computation.2 | async-start | bytes 11010048 | tf_op jit(solution)/shard_map/all_to_all | solution.py:113
  231.5 2.1 convert_add_fusion
  233.7 45.7 %while.11 = (s32[]{:T(128)}, f32[2,168,128]{2,1,0:T(8,128)S(1)}, f32[2,168,128]{2,1,0:T(8,128)S(1)}, s32[]{:T(128)}, f32[8,2,168,256]{3,2,1,0:T(8,128)S(1)}, /*i...) while((s32[]{:T(128)}, f32[2,168,128]{2,1,0:T(8,128)S(1)}, ...), condition=%wide.region_9.10_spmd, body=%wide.region_8.9_spmd.sunk | while | flops 258082 | bytes 3441171 | solution.py:79
  233.7 2.7 collective-permute-start
  236.7 2.0 collective-permute-done
  238.7 3.5 %collective-permute-done.1 = bf16[2,168,128]{2,1,0:T(8,128)(2,1)S(1)} collective-permute-done((bf16[2,168,128]{2,1,0:T(8,128)(2,1)S(1)}, bf16[2,168,128]{2,1,0:T(8,128)(2,1)S(1)}, u32[]{:S(2)}, u32[]{:S(2)}) %collective-permute-start.1) | collective-permute-done | bytes 86048 | tf_op jit(solution)/shard_map/while/body/eval_jaxpr/ppermute | solution.py:76
  242.6 1.9 collective-permute-start.1
  244.6 2.3 collective-permute-done
  246.9 1.5 collective-permute-done.1
  248.6 2.1 collective-permute-start.1
  250.7 2.3 collective-permute-done
  253.0 1.3 collective-permute-done.1
  254.5 2.1 collective-permute-start.1
  256.6 2.3 collective-permute-done
  259.0 1.3 collective-permute-done.1
  260.4 2.1 collective-permute-start.1
  262.6 2.3 collective-permute-done
  264.9 1.3 collective-permute-done.1
  266.4 2.1 collective-permute-start.1
  268.5 2.7 collective-permute-done
  271.3 1.3 collective-permute-done.1
  273.6 1.3 collective-permute-start.1
  274.9 2.3 collective-permute-done
  277.2 2.1 collective-permute-done.1
  279.5 2.9 collective-permute-start.7
  282.4 1.8 copy.45
  284.1 14.1 %collective-permute-done.7 = bf16[168,256]{1,0:T(8,128)(2,1)S(1)} collective-permute-done((bf16[168,256]{1,0:T(8,128)(2,1)S(1)}, bf16[168,256]{1,0:T(8,128)(2,1)S(1)}, u32[]{:S(2)}, u32[]{:S(2)}) %collective-permute-start.7) | collective-permute-done | bytes 86048 | tf_op jit(solution)/shard_map/ppermute | solution.py:90
  299.0 4.4 %reduce_sum.81 = bf16[64,5376]{1,0:T(8,128)(2,1)} reduce(bf16[8,64,5376]{2,1,0:T(8,128)(2,1)} %all-to-all-done.2, bf16[]{:T(256)} %constant.224.clone.1), dimensions={0}, to_apply=%region_7.8 | reduce | flops 2408448 | bytes 6193154 | tf_op jit(solution)/shard_map/reduce_sum | solution.py:114
  (103 shorter events, 13.1 us)
Async XLA Ops:
  4.5 7.1 %copy-start.4 = (bf16[512,256]{1,0:T(8,128)(2,1)S(1)}, bf16[512,256]{1,0:T(8,128)(2,1)}, u32[]{:S(2)}) copy-start(bf16[512,256]{1,0:T(8,128)(2,1)} %param.15) | copy-start | bytes 786436
  4.5 70.1 %all-to-all-start = ((bf16[8,64,5376]{2,1,0:T(8,128)(2,1)}), bf16[8,64,5376]{2,1,0:T(8,128)(2,1)}, u32[]{:S(2)}, u32[]{:S(2)}) async-start(bf16[8,64,5376]{2,1,0:T(8,128)(2,1)} %broadcast_in_dim.71), calls=%async_computation | async-start | bytes 11010048 | tf_op jit(solution)/shard_map/all_to_all | solution.py:106
  74.6 7.0 %copy-start.5 = (f32[128]{0:T(128)S(1)}, f32[128]{0:T(128)}, u32[]{:S(2)}) copy-start(f32[128]{0:T(128)} %param.14) | copy-start | bytes 1540
  74.6 12.6 %copy-start.6 = (f32[128]{0:T(128)S(1)}, f32[128]{0:T(128)}, u32[]{:S(2)}) copy-start(f32[128]{0:T(128)} %param.13) | copy-start | bytes 1540
  81.4 5.6 %copy-start.1 = (f32[512,512]{0,1:T(8,128)}, f32[512,512]{0,1:T(8,128)S(1)}, u32[]{:S(2)}) copy-start(f32[512,512]{0,1:T(8,128)S(1)} %convolution_bitcast_fusion.2) | copy-start | bytes 3145732
  82.3 9.0 %collective-permute-start.3 = (bf16[2,512,128]{1,2,0:T(8,128)(2,1)S(1)}, bf16[2,512,128]{1,2,0:T(8,128)(2,1)}, u32[]{:S(2)}, u32[]{:S(2)}) collective-permute-start(bf16[2,512,128]{1,2,0:T(8,128)(2,1)S(1)} %pad_maximum_fusion.1), channel_id=1, source_target_pairs={{0,8},{8,16},{16,24},{24,32},{32,40},{40,48},{48,56},{56,64},{64,7... | collective-permute-start | bytes 786440 | tf_op jit(solution)/shard_map/ppermute | solution.py:18
  84.2 12.1 %collective-permute-start.2 = (bf16[2,512,128]{1,2,0:T(8,128)(2,1)S(1)}, bf16[2,512,128]{1,2,0:T(8,128)(2,1)}, u32[]{:S(2)}, u32[]{:S(2)}) collective-permute-start(bf16[2,512,128]{1,2,0:T(8,128)(2,1)S(1)} %pad_maximum_fusion.1), channel_id=1, source_target_pairs={{0,16},{8,24},{16,32},{24,40},{32,48},{40,56},{48,64},{56,72},{64,... | collective-permute-start | bytes 786440 | tf_op jit(solution)/shard_map/ppermute | solution.py:18
  98.6 4.4 %copy-start = (f32[1536,512,2]{1,0,2:T(8,128)}, f32[1536,512,2]{1,0,2:T(8,128)S(1)}, u32[]{:S(2)}) copy-start(f32[1536,512,2]{1,0,2:T(8,128)S(1)} %get-tuple-element.244) | copy-start | bytes 18874372
  118.8 5.9 %copy-start.3 = (f32[1,1536,128]{1,2,0:T(8,128)S(1)}, f32[1,1536,128]{1,2,0:T(8,128)}, u32[]{:S(2)}) copy-start(f32[1,1536,128]{1,2,0:T(8,128)} %convolution_bitcast_fusion) | copy-start | bytes 2359300
  130.6 88.6 %all-to-all-start.1 = ((bf16[32,168,256]{2,1,0:T(8,128)(2,1)}), bf16[32,168,256]{2,1,0:T(8,128)(2,1)S(1)}, u32[]{:S(2)}, u32[]{:S(2)}) async-start(bf16[32,168,256]{2,1,0:T(8,128)(2,1)} %bitcast.167), calls=%async_computation.1 | async-start | bytes 5505024 | tf_op jit(solution)/shard_map/all_to_all | solution.py:113
  141.9 63.1 %collective-permute-start.4 = (bf16[2,512,128]{1,2,0:T(8,128)(2,1)}, bf16[2,512,128]{1,2,0:T(8,128)(2,1)S(1)}, u32[]{:S(2)}, u32[]{:S(2)}) collective-permute-start(bf16[2,512,128]{1,2,0:T(8,128)(2,1)} %get-tuple-element.233), channel_id=1, source_target_pairs={{8,0},{16,8},{24,16},{32,24},{40,32},{48,40},{56,48},{64,56},{72,6... | collective-permute-start | bytes 786440 | tf_op jit(solution)/shard_map/ppermute | solution.py:18
  145.0 62.7 %collective-permute-start.5 = (bf16[2,512,128]{1,2,0:T(8,128)(2,1)S(1)}, bf16[2,512,128]{1,2,0:T(8,128)(2,1)}, u32[]{:S(2)}, u32[]{:S(2)}) collective-permute-start(bf16[2,512,128]{1,2,0:T(8,128)(2,1)S(1)} %get-tuple-element.234), channel_id=1, source_target_pairs={{16,0},{24,8},{32,16},{40,24},{48,32},{56,40},{64,48},{72,56},{80,... | collective-permute-start | bytes 786440 | tf_op jit(solution)/shard_map/ppermute | solution.py:18
  224.5 1.7 copy-start.2
  226.2 5.3 %collective-permute-start.6 = (bf16[8,2,168,256]{3,2,1,0:T(8,128)(2,1)S(1)}, bf16[8,2,168,256]{3,2,1,0:T(8,128)(2,1)}, u32[]{:S(2)}, u32[]{:S(2)}) collective-permute-start(bf16[8,2,168,256]{3,2,1,0:T(8,128)(2,1)S(1)} %dynamic-slice_bitcast_fusion.2), channel_id=1, source_target_pairs={{0,8},{8,0},{16,24},{24,16},{32,40},{40,32},{48,56},{56,48},{64,72... | collective-permute-start | bytes 4128776 | tf_op jit(solution)/shard_map/ppermute | solution.py:90
  226.7 72.3 %all-to-all-start.2 = ((bf16[8,64,5376]{2,1,0:T(8,128)(2,1)}), bf16[8,64,5376]{2,1,0:T(8,128)(2,1)}, u32[]{:S(2)}, u32[]{:S(2)}) async-start(bf16[8,64,5376]{2,1,0:T(8,128)(2,1)} %bitcast.168), calls=%async_computation.2 | async-start | bytes 11010048 | tf_op jit(solution)/shard_map/all_to_all | solution.py:113
  233.7 5.0 %collective-permute-start = (bf16[2,168,128]{2,1,0:T(8,128)(2,1)S(1)}, bf16[2,168,128]{2,1,0:T(8,128)(2,1)S(1)}, u32[]{:S(2)}, u32[]{:S(2)}) collective-permute-start(bf16[2,168,128]{2,1,0:T(8,128)(2,1)S(1)} %convert_element_type.216), channel_id=1, source_target_pairs={{0,32},{8,40},{16,48},{24,56},{32,64},{40,72},{48,80},{56,88},{64,... | collective-permute-start | bytes 258056 | tf_op jit(solution)/shard_map/while/body/eval_jaxpr/ppermute | solution.py:75
  236.5 5.8 %collective-permute-start.1 = (bf16[2,168,128]{2,1,0:T(8,128)(2,1)S(1)}, bf16[2,168,128]{2,1,0:T(8,128)(2,1)S(1)}, u32[]{:S(2)}, u32[]{:S(2)}) collective-permute-start(bf16[2,168,128]{2,1,0:T(8,128)(2,1)S(1)} %convert_element_type.217), channel_id=1, source_target_pairs={{0,224},{8,232},{16,240},{24,248},{32,0},{40,8},{48,16},{56,24},{6... | collective-permute-start | bytes 258056 | tf_op jit(solution)/shard_map/while/body/eval_jaxpr/ppermute | solution.py:76
  242.3 4.6 %collective-permute-start = (bf16[2,168,128]{2,1,0:T(8,128)(2,1)S(1)}, bf16[2,168,128]{2,1,0:T(8,128)(2,1)S(1)}, u32[]{:S(2)}, u32[]{:S(2)}) collective-permute-start(bf16[2,168,128]{2,1,0:T(8,128)(2,1)S(1)} %convert_element_type.216), channel_id=1, source_target_pairs={{0,32},{8,40},{16,48},{24,56},{32,64},{40,72},{48,80},{56,88},{64,... | collective-permute-start | bytes 258056 | tf_op jit(solution)/shard_map/while/body/eval_jaxpr/ppermute | solution.py:75
  242.6 5.8 %collective-permute-start.1 = (bf16[2,168,128]{2,1,0:T(8,128)(2,1)S(1)}, bf16[2,168,128]{2,1,0:T(8,128)(2,1)S(1)}, u32[]{:S(2)}, u32[]{:S(2)}) collective-permute-start(bf16[2,168,128]{2,1,0:T(8,128)(2,1)S(1)} %convert_element_type.217), channel_id=1, source_target_pairs={{0,224},{8,232},{16,240},{24,248},{32,0},{40,8},{48,16},{56,24},{6... | collective-permute-start | bytes 258056 | tf_op jit(solution)/shard_map/while/body/eval_jaxpr/ppermute | solution.py:76
  248.4 4.6 %collective-permute-start = (bf16[2,168,128]{2,1,0:T(8,128)(2,1)S(1)}, bf16[2,168,128]{2,1,0:T(8,128)(2,1)S(1)}, u32[]{:S(2)}, u32[]{:S(2)}) collective-permute-start(bf16[2,168,128]{2,1,0:T(8,128)(2,1)S(1)} %convert_element_type.216), channel_id=1, source_target_pairs={{0,32},{8,40},{16,48},{24,56},{32,64},{40,72},{48,80},{56,88},{64,... | collective-permute-start | bytes 258056 | tf_op jit(solution)/shard_map/while/body/eval_jaxpr/ppermute | solution.py:75
  248.6 5.8 %collective-permute-start.1 = (bf16[2,168,128]{2,1,0:T(8,128)(2,1)S(1)}, bf16[2,168,128]{2,1,0:T(8,128)(2,1)S(1)}, u32[]{:S(2)}, u32[]{:S(2)}) collective-permute-start(bf16[2,168,128]{2,1,0:T(8,128)(2,1)S(1)} %convert_element_type.217), channel_id=1, source_target_pairs={{0,224},{8,232},{16,240},{24,248},{32,0},{40,8},{48,16},{56,24},{6... | collective-permute-start | bytes 258056 | tf_op jit(solution)/shard_map/while/body/eval_jaxpr/ppermute | solution.py:76
  254.4 4.6 %collective-permute-start = (bf16[2,168,128]{2,1,0:T(8,128)(2,1)S(1)}, bf16[2,168,128]{2,1,0:T(8,128)(2,1)S(1)}, u32[]{:S(2)}, u32[]{:S(2)}) collective-permute-start(bf16[2,168,128]{2,1,0:T(8,128)(2,1)S(1)} %convert_element_type.216), channel_id=1, source_target_pairs={{0,32},{8,40},{16,48},{24,56},{32,64},{40,72},{48,80},{56,88},{64,... | collective-permute-start | bytes 258056 | tf_op jit(solution)/shard_map/while/body/eval_jaxpr/ppermute | solution.py:75
  254.5 5.8 %collective-permute-start.1 = (bf16[2,168,128]{2,1,0:T(8,128)(2,1)S(1)}, bf16[2,168,128]{2,1,0:T(8,128)(2,1)S(1)}, u32[]{:S(2)}, u32[]{:S(2)}) collective-permute-start(bf16[2,168,128]{2,1,0:T(8,128)(2,1)S(1)} %convert_element_type.217), channel_id=1, source_target_pairs={{0,224},{8,232},{16,240},{24,248},{32,0},{40,8},{48,16},{56,24},{6... | collective-permute-start | bytes 258056 | tf_op jit(solution)/shard_map/while/body/eval_jaxpr/ppermute | solution.py:76
  260.3 4.6 %collective-permute-start = (bf16[2,168,128]{2,1,0:T(8,128)(2,1)S(1)}, bf16[2,168,128]{2,1,0:T(8,128)(2,1)S(1)}, u32[]{:S(2)}, u32[]{:S(2)}) collective-permute-start(bf16[2,168,128]{2,1,0:T(8,128)(2,1)S(1)} %convert_element_type.216), channel_id=1, source_target_pairs={{0,32},{8,40},{16,48},{24,56},{32,64},{40,72},{48,80},{56,88},{64,... | collective-permute-start | bytes 258056 | tf_op jit(solution)/shard_map/while/body/eval_jaxpr/ppermute | solution.py:75
  260.4 5.8 %collective-permute-start.1 = (bf16[2,168,128]{2,1,0:T(8,128)(2,1)S(1)}, bf16[2,168,128]{2,1,0:T(8,128)(2,1)S(1)}, u32[]{:S(2)}, u32[]{:S(2)}) collective-permute-start(bf16[2,168,128]{2,1,0:T(8,128)(2,1)S(1)} %convert_element_type.217), channel_id=1, source_target_pairs={{0,224},{8,232},{16,240},{24,248},{32,0},{40,8},{48,16},{56,24},{6... | collective-permute-start | bytes 258056 | tf_op jit(solution)/shard_map/while/body/eval_jaxpr/ppermute | solution.py:76
  266.3 5.0 %collective-permute-start = (bf16[2,168,128]{2,1,0:T(8,128)(2,1)S(1)}, bf16[2,168,128]{2,1,0:T(8,128)(2,1)S(1)}, u32[]{:S(2)}, u32[]{:S(2)}) collective-permute-start(bf16[2,168,128]{2,1,0:T(8,128)(2,1)S(1)} %convert_element_type.216), channel_id=1, source_target_pairs={{0,32},{8,40},{16,48},{24,56},{32,64},{40,72},{48,80},{56,88},{64,... | collective-permute-start | bytes 258056 | tf_op jit(solution)/shard_map/while/body/eval_jaxpr/ppermute | solution.py:75
  266.4 6.2 %collective-permute-start.1 = (bf16[2,168,128]{2,1,0:T(8,128)(2,1)S(1)}, bf16[2,168,128]{2,1,0:T(8,128)(2,1)S(1)}, u32[]{:S(2)}, u32[]{:S(2)}) collective-permute-start(bf16[2,168,128]{2,1,0:T(8,128)(2,1)S(1)} %convert_element_type.217), channel_id=1, source_target_pairs={{0,224},{8,232},{16,240},{24,248},{32,0},{40,8},{48,16},{56,24},{6... | collective-permute-start | bytes 258056 | tf_op jit(solution)/shard_map/while/body/eval_jaxpr/ppermute | solution.py:76
  272.6 4.6 %collective-permute-start = (bf16[2,168,128]{2,1,0:T(8,128)(2,1)S(1)}, bf16[2,168,128]{2,1,0:T(8,128)(2,1)S(1)}, u32[]{:S(2)}, u32[]{:S(2)}) collective-permute-start(bf16[2,168,128]{2,1,0:T(8,128)(2,1)S(1)} %convert_element_type.216), channel_id=1, source_target_pairs={{0,32},{8,40},{16,48},{24,56},{32,64},{40,72},{48,80},{56,88},{64,... | collective-permute-start | bytes 258056 | tf_op jit(solution)/shard_map/while/body/eval_jaxpr/ppermute | solution.py:75
  273.6 5.8 %collective-permute-start.1 = (bf16[2,168,128]{2,1,0:T(8,128)(2,1)S(1)}, bf16[2,168,128]{2,1,0:T(8,128)(2,1)S(1)}, u32[]{:S(2)}, u32[]{:S(2)}) collective-permute-start(bf16[2,168,128]{2,1,0:T(8,128)(2,1)S(1)} %convert_element_type.217), channel_id=1, source_target_pairs={{0,224},{8,232},{16,240},{24,248},{32,0},{40,8},{48,16},{56,24},{6... | collective-permute-start | bytes 258056 | tf_op jit(solution)/shard_map/while/body/eval_jaxpr/ppermute | solution.py:76
  279.5 18.8 %collective-permute-start.7 = (bf16[168,256]{1,0:T(8,128)(2,1)S(1)}, bf16[168,256]{1,0:T(8,128)(2,1)S(1)}, u32[]{:S(2)}, u32[]{:S(2)}) collective-permute-start(bf16[168,256]{1,0:T(8,128)(2,1)S(1)} %fusion.46), channel_id=1, source_target_pairs={{0,16},{8,24},{16,0},{24,8},{32,48},{40,56},{48,32},{56,40},{64,80... | collective-permute-start | bytes 258056 | tf_op jit(solution)/shard_map/ppermute | solution.py:90

commit v6 on v2

--- a/solution.py
+++ b/solution.py
@@ -96,8 +96,8 @@
     grid = full.reshape(outer, middle, inner, -1, width)
     grid = jnp.moveaxis(grid, 2, 0)
     grid = pair_scatter_sum(grid, axis, 1)
-    grid = ring_scatter_sum(grid, axis, outer, middle * inner)
-    return pair_scatter_sum(grid, axis, inner)
+    grid = pair_scatter_sum(jnp.moveaxis(grid, 1, 0), axis, inner)
+    return ring_scatter_sum(grid, axis, outer, middle * inner)
 
 
 def gather_all(block, axis):

time: 231 us -> 262 us (1.13)
  waiting for transfers between devices: 101 us -> 141 us
  local copies, waits for them, and re-layouts: 33.5 us -> 21.7 us
    ppermute x2, waiting for transfers between devices: 5.61 us -> 30.3 us  [pair_scatter_sum(): lax.ppermute(other.astype(jnp.bfloat16), axis, route).astype(jnp.float32)]
    all_to_all x1, waiting for transfers between devices: 0.01 us -> 14.1 us  [exchange_sum(): received = lax.all_to_all(pieces, axis, 0, 0)]
    squeeze x8, local copies, waits for them, and re-layouts: 9.98 us -> 0.38 us  [chunk(): lax.dynamic_index_in_dim(blocks, (digit - step * (k + 1)) % count, 0, kee...]
    ppermute x7, starting transfers between devices: 5.97 us -> 2 us  [advance(): lax.ppermute(up.astype(jnp.bfloat16), axis, route(1)).astype(jnp.float32)]
    ppermute x7, waiting for transfers between devices: 14.2 us -> 17.3 us  [advance(): lax.ppermute(up.astype(jnp.bfloat16), axis, route(1)).astype(jnp.float32)]
    add x2, other arithmetic: 2.61 us -> 5.38 us  [pair_scatter_sum(): own + lax.ppermute(other.astype(jnp.bfloat16), axis, route).astype(jnp.fl...]
    ppermute x2, starting transfers between devices: 2.08 us -> 4.84 us  [pair_scatter_sum(): lax.ppermute(other.astype(jnp.bfloat16), axis, route).astype(jnp.float32)]
    unnamed x51 -> x50, local copies, waits for them, and re-layouts: 10.5 us -> 8.28 us
  transfers between devices with their start and end apart: 22 -> 22, of which waited for: 21 -> 22; matrix products, arithmetic and copies ran while one was open for 12% -> 7% of each run, Pallas kernels for 0% -> 0%
where the time goes in v6:
time: 262 us; the launch traced here: 261 us
  waiting for transfers between devices  141 us (54%)
  starting transfers between devices  41.2 us (16%)
  matrix products  34.5 us (13%)
  local copies, waits for them, and re-layouts  21.7 us (8%)
  other arithmetic  21.5 us (8%)
    all_to_all x1, waiting for transfers between devices, gather_all(): received = lax.all_to_all(copies, axis, 0, 0)  52.4 us
    ppermute x2, waiting for transfers between devices, pair_scatter_sum(): lax.ppermute(other.astype(jnp.bfloat16), axis, route).astype(jnp.float32)  30.3 us
    ppermute x7, waiting for transfers between devices, advance(): lax.ppermute(up.astype(jnp.bfloat16), axis, route(1)).astype(jnp.float32)  17.3 us
    ppermute x4, waiting for transfers between devices, passed_along(): return lax.ppermute(block, axis, route)  15.9 us
    all_to_all x1, waiting for transfers between devices, exchange_sum(): received = lax.all_to_all(pieces, axis, 0, 0)  14.1 us
    ppermute x7, starting transfers between devices, advance(): lax.ppermute(down.astype(jnp.bfloat16), axis, route(-1)).astype(jnp.float32)  13.2 us
    ppermute x7, waiting for transfers between devices, advance(): lax.ppermute(down.astype(jnp.bfloat16), axis, route(-1)).astype(jnp.float32)  10.5 us
    ppermute x4, starting transfers between devices, passed_along(): return lax.ppermute(block, axis, route)  8.66 us
  transfers between devices with their start and end apart: 22, of which 22 were waited for; matrix products, arithmetic and copies ran while one was open for 7% of the time, Pallas kernels for 0%

profile of v6, /device:TPU:96, one launch (start us, length us, event | category | flops | bytes accessed | tf_op | source)
XLA Modules:
  0.0 261.0 jit_solution(3389964019393630159)
XLA Ops:
  0.6 3.9 %broadcast_in_dim.71 = bf16[8,64,5376]{2,1,0:T(8,128)(2,1)} broadcast(bf16[64,5376]{1,0:T(8,128)(2,1)} %param.9), dimensions={1,2} | broadcast | bytes 6193152 | tf_op jit(solution)/shard_map/broadcast_in_dim | solution.py:105
  4.5 7.1 %all-to-all-start = ((bf16[8,64,5376]{2,1,0:T(8,128)(2,1)}), bf16[8,64,5376]{2,1,0:T(8,128)(2,1)}, u32[]{:S(2)}, u32[]{:S(2)}) async-start(bf16[8,64,5376]{2,1,0:T(8,128)(2,1)} %broadcast_in_dim.71), calls=%async_computation | async-start | bytes 11010048 | tf_op jit(solution)/shard_map/all_to_all | solution.py:106
  11.7 0.9 copy.43
  12.6 1.0 multiply_cosine_fusion
  13.6 1.2 fusion.7
  14.8 3.5 %constant_dynamic-update-slice_fusion.2 = bf16[5376,512]{1,0:T(8,128)(2,1)} fusion(bf16[5376,256]{1,0:T(8,128)(2,1)} %param.10), kind=kLoop, calls=%fused_computation.95 | loop fusion | bytes 5505024
  18.3 1.2 constant_dynamic-update-slice_fusion.1
  19.6 2.6 %constant_dynamic-update-slice_fusion = bf16[5376,512]{1,0:T(8,128)(2,1)} fusion(bf16[5376,512]{1,0:T(8,128)(2,1)} %constant_dynamic-update-slice_fusion.1, bf16[5376,128]{1,0:T(8,128)(2,1)} %param.12), kind=kLoop, calls=%fused_computation.93 | loop fusion | bytes 2752512 | tf_op jit(solution)/shard_map/concatenate | solution.py:223
  22.2 52.4 %all-to-all-done = bf16[8,64,5376]{2,1,0:T(8,128)(2,1)} async-done(((bf16[8,64,5376]{2,1,0:T(8,128)(2,1)}), bf16[8,64,5376]{2,1,0:T(8,128)(2,1)}, u32[]{:S(2)}, u32[]{:S(2)}) %all-to-all-start) | async-done | bytes 5505056 | tf_op jit(solution)/shard_map/all_to_all | solution.py:106
  74.6 6.8 %convolution_bitcast_fusion.2 = f32[512,512]{0,1:T(8,128)S(1)} fusion(bf16[5376,512]{1,0:T(8,128)(2,1)} %constant_dynamic-update-slice_fusion, bf16[512,5376]{1,0:T(8,128)(2,1)} %bitcast.4), kind=kOutput, calls=%fused_computation.32 | convolution fusion | flops 2818572288 | bytes 12058624 | tf_op jit(solution)/shard_map/dot_general | solution.py:224
  82.9 2.5 collective-permute-start.2
  85.4 2.1 collective-permute-start.3
  88.6 6.6 %collective-permute-done.2 = bf16[2,512,128]{1,2,0:T(8,128)(2,1)} collective-permute-done((bf16[2,512,128]{1,2,0:T(8,128)(2,1)}, bf16[2,512,128]{1,2,0:T(8,128)(2,1)}, u32[]{:S(2)}, u32[]{:S(2)}) %collective-permute-start.2) | collective-permute-done | bytes 262176 | tf_op jit(solution)/shard_map/ppermute | solution.py:18
  95.2 1.2 collective-permute-done.3
  96.4 1.1 maximum_maximum_fusion
  97.5 1.2 fusion.2
  98.7 1.3 exponential_reduce_fusion
  100.0 2.7 %bitcast_convert_fusion = (f32[2,512,128]{1,2,0:T(8,128)S(1)}, bf16[128,2,512]{2,0,1:T(8,128)(2,1)}) fusion(f32[1536,512,2]{1,0,2:T(8,128)S(1)} %get-tuple-element.240, f32[2,512]{1,0:T(2,128)S(1)} %log_add_fusion, pred[512,1536]{0,1:T(8,128)(4,1)S(1)} %fusion.7, bf16[2,1536,128]{1,2,0:T(8,128)(2,1)S(1)} %maximum_maximum_fusion), kind=kOutput, calls=%fused_computation.69 | convolution fusion | flops 409206784 | bytes 8261632 | tf_op jit(solution)/shard_map/while/body/eval_jaxpr/kgqj,jkd->qkgd/dot_general | solution.py:164
  103.0 1.3 multiply_reduce_fusion
  104.3 1.2 copy.56
  105.5 4.9 %convolution_bitcast_fusion = f32[1,1536,128]{1,2,0:T(8,128)S(1)} fusion(bf16[512,2,128]{0,2,1:T(8,128)(2,1)} %copy.43, f32[1536,512,2]{1,0,2:T(8,128)} %copy-done, f32[2,512]{1,0:T(2,128)S(1)} %log_add_fusion, pred[512,1536]{0,1:T(8,128)(4,1)S(1)} %fusion.7), kind=kOutput, calls=%fused_computation.25 | convolution fusion | flops 408944640 | bytes 8130560 | tf_op jit(solution)/shard_map/while/body/eval_jaxpr/kgqj,qkgd->jkd/dot_general | solution.py:203
  110.5 2.5 fusion.4
  113.0 1.4 fusion.10
  114.4 1.2 convolution_bitcast_fusion.1
  116.9 1.9 collective-permute-start.4
  118.8 2.1 collective-permute-start.5
  122.0 2.1 collective-permute-done.4
  124.1 6.1 %collective-permute-done.5 = bf16[2,512,128]{1,2,0:T(8,128)(2,1)} collective-permute-done((bf16[2,512,128]{1,2,0:T(8,128)(2,1)}, bf16[2,512,128]{1,2,0:T(8,128)(2,1)}, u32[]{:S(2)}, u32[]{:S(2)}) %collective-permute-start.5) | collective-permute-done | bytes 262176 | tf_op jit(solution)/shard_map/ppermute | solution.py:18
  130.1 1.1 fusion.14
  132.1 7.5 %convolution_convert_fusion = bf16[512,5376]{1,0:T(8,128)(2,1)} fusion(bf16[5376,512]{1,0:T(8,128)(2,1)} %constant_dynamic-update-slice_fusion, bf16[512,128]{0,1:T(8,128)(2,1)S(1)} %fusion.34, bf16[512,128]{0,1:T(8,128)(2,1)S(1)} %fusion.35, bf16[512,256]{0,1:T(8,128)(2,1)S(1)} %bitcast.159), kind=kOutput, calls=%fused_computation.5 | convolution fusion | flops 2822897664 | bytes 11534336 | tf_op jit(solution)/shard_map/dot_general | solution.py:292
  139.6 6.4 %multiply_convert_fusion = bf16[5376,512]{1,0:T(8,128)(2,1)S(1)} fusion(bf16[512,5376]{1,0:T(8,128)(2,1)} %bitcast.4, bf16[512,128]{0,1:T(8,128)(2,1)S(1)} %fusion.34, bf16[512,128]{0,1:T(8,128)(2,1)S(1)} %fusion.35, bf16[512,256]{0,1:T(8,128)(2,1)S(1)} %bitcast.160), kind=kOutput, calls=%fused_computation.4 | convolution fusion | flops 2825650176 | bytes 11534336 | tf_op jit(solution)/shard_map/dot_general | solution.py:299
  146.4 1.8 copy.69
  148.2 5.4 %collective-permute-done.6 = bf16[8,2,168,512]{3,2,0,1:T(8,128)(2,1)} collective-permute-done((bf16[8,2,168,512]{3,2,0,1:T(8,128)(2,1)}, bf16[8,2,168,512]{3,2,0,1:T(8,128)(2,1)}, u32[]{:S(2)}, u32[]{:S(2)}) %collective-permute-start.6) | collective-permute-done | bytes 2752544 | tf_op jit(solution)/shard_map/ppermute | solution.py:90
  153.6 2.7 %convert_add_fusion = f32[8,2,168,512]{3,2,0,1:T(8,128)S(1)} fusion(bf16[8,2,168,512]{3,2,0,1:T(8,128)(2,1)} %collective-permute-done.6, bf16[8,2,1,168,512]{4,3,2,1,0:T(8,128)(2,1)S(1)} %get-tuple-element.221), kind=kLoop, calls=%fused_computation.13 | loop fusion | flops 4128768 | bytes 11010048 | tf_op jit(solution)/shard_map/add | solution.py:90
  156.4 2.4 copy-done.1
  158.9 4.8 %collective-permute-start.7 = (bf16[8,168,512]{2,1,0:T(8,128)(2,1)S(1)}, bf16[8,168,512]{2,1,0:T(8,128)(2,1)}, u32[]{:S(2)}, u32[]{:S(2)}) collective-permute-start(bf16[8,168,512]{2,1,0:T(8,128)(2,1)S(1)} %fusion.9), channel_id=1, source_target_pairs={{0,16},{8,24},{16,0},{24,8},{32,48},{40,56},{48,32},{56,40},{64,80... | collective-permute-start | bytes 4128776 | tf_op jit(solution)/shard_map/ppermute | solution.py:90
  164.6 5.4 %all-to-all-start.1 = ((bf16[8,64,5376]{2,1,0:T(8,128)(2,1)}), bf16[8,64,5376]{2,1,0:T(8,128)(2,1)}, u32[]{:S(2)}, u32[]{:S(2)}) async-start(bf16[8,64,5376]{2,1,0:T(8,128)(2,1)} %bitcast.155), calls=%async_computation.1 | async-start | bytes 11010048 | tf_op jit(solution)/shard_map/all_to_all | solution.py:113
  170.0 24.9 %collective-permute-done.7 = bf16[8,168,512]{2,1,0:T(8,128)(2,1)} collective-permute-done((bf16[8,168,512]{2,1,0:T(8,128)(2,1)S(1)}, bf16[8,168,512]{2,1,0:T(8,128)(2,1)}, u32[]{:S(2)}, u32[]{:S(2)}) %collective-permute-start.7) | collective-permute-done | bytes 1376288 | tf_op jit(solution)/shard_map/ppermute | solution.py:90
  194.9 2.6 %bitcast_add_fusion = f32[8,168,512]{2,1,0:T(8,128)S(1)} fusion(bf16[8,168,512]{2,1,0:T(8,128)(2,1)} %collective-permute-done.7, f32[8,2,168,512]{3,2,0,1:T(8,128)} %copy-done.1, s32[]{:T(128)S(6)} %select_n.122), kind=kLoop, calls=%fused_computation.22 | loop fusion | flops 1376256 | bytes 6881284 | tf_op jit(solution)/shard_map/add | solution.py:90
  197.6 44.1 %while.11 = (s32[]{:T(128)}, f32[168,256]{1,0:T(8,128)S(1)}, f32[168,256]{1,0:T(8,128)S(1)}, s32[]{:T(128)}, f32[8,168,512]{2,1,0:T(8,128)S(1)}, /*index=5*/s32[...) while((s32[]{:T(128)}, f32[168,256]{1,0:T(8,128)S(1)}, ...), condition=%wide.region_8.9_spmd, body=%wide.region_7.8_spmd.sunk | while | flops 258082 | bytes 3441171 | solution.py:79
  197.7 1.3 collective-permute-start
  199.0 0.9 collective-permute-start.1
  199.9 2.3 collective-permute-done
  202.3 2.5 collective-permute-done.1
  204.9 2.1 collective-permute-start.1
  207.1 2.3 collective-permute-done
  209.4 1.3 collective-permute-done.1
  210.9 2.1 collective-permute-start.1
  213.0 2.3 collective-permute-done
  215.4 1.3 collective-permute-done.1
  216.8 2.1 collective-permute-start.1
  219.0 3.1 %collective-permute-done = bf16[168,256]{1,0:T(8,128)(2,1)S(1)} collective-permute-done((bf16[168,256]{1,0:T(8,128)(2,1)S(1)}, bf16[168,256]{1,0:T(8,128)(2,1)S(1)}, u32[]{:S(2)}, u32[]{:S(2)}) %collective-permute-start) | collective-permute-done | bytes 86048 | tf_op jit(solution)/shard_map/while/body/eval_jaxpr/ppermute | solution.py:75
  222.1 1.3 collective-permute-done.1
  223.5 2.1 collective-permute-start.1
  225.7 2.6 %collective-permute-done = bf16[168,256]{1,0:T(8,128)(2,1)S(1)} collective-permute-done((bf16[168,256]{1,0:T(8,128)(2,1)S(1)}, bf16[168,256]{1,0:T(8,128)(2,1)S(1)}, u32[]{:S(2)}, u32[]{:S(2)}) %collective-permute-start) | collective-permute-done | bytes 86048 | tf_op jit(solution)/shard_map/while/body/eval_jaxpr/ppermute | solution.py:75
  228.3 1.3 collective-permute-done.1
  230.0 1.9 collective-permute-start.1
  231.9 2.3 collective-permute-done
  234.3 1.5 collective-permute-done.1
  235.9 2.1 collective-permute-start.1
  238.1 2.3 collective-permute-done
  240.4 1.3 collective-permute-done.1
  242.5 14.1 %all-to-all-done.1 = bf16[8,64,5376]{2,1,0:T(8,128)(2,1)} async-done(((bf16[8,64,5376]{2,1,0:T(8,128)(2,1)}), bf16[8,64,5376]{2,1,0:T(8,128)(2,1)}, u32[]{:S(2)}, u32[]{:S(2)}) %all-to-all-start.1) | async-done | bytes 5505056 | tf_op jit(solution)/shard_map/all_to_all | solution.py:113
  256.6 4.4 %reduce_sum.71 = bf16[64,5376]{1,0:T(8,128)(2,1)} reduce(bf16[8,64,5376]{2,1,0:T(8,128)(2,1)} %all-to-all-done.1, bf16[]{:T(256)} %constant.224.clone.1), dimensions={0}, to_apply=%region_6.7 | reduce | flops 2408448 | bytes 6193154 | tf_op jit(solution)/shard_map/reduce_sum | solution.py:114
  (130 shorter events, 9.7 us)
Async XLA Ops:
  4.5 7.1 %copy-start.16 = (bf16[512,256]{1,0:T(8,128)(2,1)S(1)}, bf16[512,256]{1,0:T(8,128)(2,1)}, u32[]{:S(2)}) copy-start(bf16[512,256]{1,0:T(8,128)(2,1)} %param.15) | copy-start | bytes 786436
  4.5 70.1 %all-to-all-start = ((bf16[8,64,5376]{2,1,0:T(8,128)(2,1)}), bf16[8,64,5376]{2,1,0:T(8,128)(2,1)}, u32[]{:S(2)}, u32[]{:S(2)}) async-start(bf16[8,64,5376]{2,1,0:T(8,128)(2,1)} %broadcast_in_dim.71), calls=%async_computation | async-start | bytes 11010048 | tf_op jit(solution)/shard_map/all_to_all | solution.py:106
  11.6 6.8 %copy-start.15 = (bf16[5376,128]{1,0:T(8,128)(2,1)S(1)}, bf16[5376,128]{1,0:T(8,128)(2,1)}, u32[]{:S(2)}) copy-start(bf16[5376,128]{1,0:T(8,128)(2,1)} %param.11) | copy-start | bytes 4128772
  13.6 74.5 %copy-start.9 = (f32[512,64]{1,0:T(8,128)}, f32[512,64]{1,0:T(8,128)S(1)}, u32[]{:S(2)}) copy-start(f32[512,64]{1,0:T(8,128)S(1)} %get-tuple-element.237) | copy-start | bytes 393220
  13.6 74.5 %copy-start.11 = (f32[512,64]{1,0:T(8,128)}, f32[512,64]{1,0:T(8,128)S(1)}, u32[]{:S(2)}) copy-start(f32[512,64]{1,0:T(8,128)S(1)} %get-tuple-element.238) | copy-start | bytes 393220
  74.6 6.9 %copy-start.19 = (f32[128]{0:T(128)S(1)}, f32[128]{0:T(128)}, u32[]{:S(2)}) copy-start(f32[128]{0:T(128)} %param.14) | copy-start | bytes 1540
  74.6 13.3 %copy-start.20 = (f32[128]{0:T(128)S(1)}, f32[128]{0:T(128)}, u32[]{:S(2)}) copy-start(f32[128]{0:T(128)} %param.13) | copy-start | bytes 1540
  81.4 6.2 %copy-start.3 = (f32[512,512]{0,1:T(8,128)}, f32[512,512]{0,1:T(8,128)S(1)}, u32[]{:S(2)}) copy-start(f32[512,512]{0,1:T(8,128)S(1)} %convolution_bitcast_fusion.2) | copy-start | bytes 3145732
  82.9 12.3 %collective-permute-start.2 = (bf16[2,512,128]{1,2,0:T(8,128)(2,1)}, bf16[2,512,128]{1,2,0:T(8,128)(2,1)}, u32[]{:S(2)}, u32[]{:S(2)}) collective-permute-start(bf16[2,512,128]{1,2,0:T(8,128)(2,1)} %pad_maximum_fusion.2), channel_id=1, source_target_pairs={{0,16},{8,24},{16,32},{24,40},{32,48},{40,56},{48,64},{56,72},{64,... | collective-permute-start | bytes 786440 | tf_op jit(solution)/shard_map/ppermute | solution.py:18
  85.4 10.9 %collective-permute-start.3 = (bf16[2,512,128]{1,2,0:T(8,128)(2,1)}, bf16[2,512,128]{1,2,0:T(8,128)(2,1)}, u32[]{:S(2)}, u32[]{:S(2)}) collective-permute-start(bf16[2,512,128]{1,2,0:T(8,128)(2,1)} %pad_maximum_fusion.2), channel_id=1, source_target_pairs={{0,8},{8,16},{16,24},{24,32},{32,40},{40,48},{48,56},{56,64},{64,7... | collective-permute-start | bytes 786440 | tf_op jit(solution)/shard_map/ppermute | solution.py:18
  88.6 8.9 %copy-start.13 = (bf16[512,2,128]{2,0,1:T(8,128)(2,1)}, bf16[512,2,128]{2,0,1:T(8,128)(2,1)S(1)}, u32[]{:S(2)}) copy-start(bf16[512,2,128]{2,0,1:T(8,128)(2,1)S(1)} %fusion.15) | copy-start | bytes 786436
  97.4 2.6 copy-start.5
  98.7 4.0 %copy-start = (f32[1536,512,2]{1,0,2:T(8,128)}, f32[1536,512,2]{1,0,2:T(8,128)S(1)}, u32[]{:S(2)}) copy-start(f32[1536,512,2]{1,0,2:T(8,128)S(1)} %get-tuple-element.240) | copy-start | bytes 18874372
  104.3 6.2 %slice-start = ((s8[6291456]{0:T(1024)(128)(4,1)}), s8[2097152]{0:T(1024)(128)(4,1)S(1)}, s32[]{:S(2)}) async-start(s8[6291456]{0:T(1024)(128)(4,1)} %bitcast.153), calls=%async_computation.2 | async-start | bytes 4194304
  105.5 5.0 %slice-start.1 = ((s8[6291456]{0:T(1024)(128)(4,1)}), s8[4194304]{0:T(1024)(128)(4,1)S(1)}, s32[]{:S(2)}) async-start(s8[6291456]{0:T(1024)(128)(4,1)} %bitcast.153), calls=%async_computation.3 | async-start | bytes 8388608
  105.5 5.0 %copy-start.6 = (bf16[2,1536,128]{1,2,0:T(8,128)(2,1)S(1)}, bf16[2,1536,128]{1,2,0:T(8,128)(2,1)}, u32[]{:S(2)}) copy-start(bf16[2,1536,128]{1,2,0:T(8,128)(2,1)} %copy-done.5) | copy-start | bytes 2359300
  105.5 5.0 %copy-start.18 = (bf16[512,2,128]{0,2,1:T(8,128)(2,1)S(1)}, bf16[512,2,128]{0,2,1:T(8,128)(2,1)}, u32[]{:S(2)}) copy-start(bf16[512,2,128]{0,2,1:T(8,128)(2,1)} %copy.43) | copy-start | bytes 786436
  110.5 5.4 %copy-start.7 = (f32[1,1536,128]{1,2,0:T(8,128)}, f32[1,1536,128]{1,2,0:T(8,128)S(1)}, u32[]{:S(2)}) copy-start(f32[1,1536,128]{1,2,0:T(8,128)S(1)} %convolution_bitcast_fusion) | copy-start | bytes 2359300
  110.5 3.9 %copy-start.14 = (bf16[512,2,128]{2,0,1:T(8,128)(2,1)S(1)}, bf16[512,2,128]{2,0,1:T(8,128)(2,1)}, u32[]{:S(2)}) copy-start(bf16[512,2,128]{2,0,1:T(8,128)(2,1)} %copy-done.13) | copy-start | bytes 786436
  113.0 2.6 copy-start.10
  113.0 2.6 copy-start.12
  115.9 16.0 %copy-start.4 = (f32[512,512]{0,1:T(8,128)S(1)}, f32[512,512]{0,1:T(8,128)}, u32[]{:S(2)}) copy-start(f32[512,512]{0,1:T(8,128)} %copy-done.3) | copy-start | bytes 3145732
  116.0 14.1 %copy-start.8 = (f32[1,1536,128]{1,2,0:T(8,128)S(1)}, f32[1,1536,128]{1,2,0:T(8,128)}, u32[]{:S(2)}) copy-start(f32[1,1536,128]{1,2,0:T(8,128)} %copy-done.7) | copy-start | bytes 2359300
  116.9 7.2 %collective-permute-start.4 = (bf16[2,512,128]{1,2,0:T(8,128)(2,1)}, bf16[2,512,128]{1,2,0:T(8,128)(2,1)}, u32[]{:S(2)}, u32[]{:S(2)}) collective-permute-start(bf16[2,512,128]{1,2,0:T(8,128)(2,1)} %get-tuple-element.229), channel_id=1, source_target_pairs={{8,0},{16,8},{24,16},{32,24},{40,32},{48,40},{56,48},{64,56},{72,6... | collective-permute-start | bytes 786440 | tf_op jit(solution)/shard_map/ppermute | solution.py:18
  118.8 11.3 %collective-permute-start.5 = (bf16[2,512,128]{1,2,0:T(8,128)(2,1)}, bf16[2,512,128]{1,2,0:T(8,128)(2,1)}, u32[]{:S(2)}, u32[]{:S(2)}) collective-permute-start(bf16[2,512,128]{1,2,0:T(8,128)(2,1)} %get-tuple-element.230), channel_id=1, source_target_pairs={{16,0},{24,8},{32,16},{40,24},{48,32},{56,40},{64,48},{72,56},{80,... | collective-permute-start | bytes 786440 | tf_op jit(solution)/shard_map/ppermute | solution.py:18
  148.2 5.4 %collective-permute-start.6 = (bf16[8,2,168,512]{3,2,0,1:T(8,128)(2,1)}, bf16[8,2,168,512]{3,2,0,1:T(8,128)(2,1)}, u32[]{:S(2)}, u32[]{:S(2)}) collective-permute-start(bf16[8,2,168,512]{3,2,0,1:T(8,128)(2,1)} %bitcast.150), channel_id=1, source_target_pairs={{0,8},{8,0},{16,24},{24,16},{32,40},{40,32},{48,56},{56,48},{64,72... | collective-permute-start | bytes 8257544 | tf_op jit(solution)/shard_map/ppermute | solution.py:90
  153.6 10.1 %copy-start.17 = (bf16[128,2,512]{2,0,1:T(8,128)(2,1)S(1)}, bf16[128,2,512]{2,0,1:T(8,128)(2,1)}, u32[]{:S(2)}) copy-start(bf16[128,2,512]{2,0,1:T(8,128)(2,1)} %get-tuple-element.242) | copy-start | bytes 786436
  156.3 2.4 copy-start.1
  158.9 36.0 %collective-permute-start.7 = (bf16[8,168,512]{2,1,0:T(8,128)(2,1)S(1)}, bf16[8,168,512]{2,1,0:T(8,128)(2,1)}, u32[]{:S(2)}, u32[]{:S(2)}) collective-permute-start(bf16[8,168,512]{2,1,0:T(8,128)(2,1)S(1)} %fusion.9), channel_id=1, source_target_pairs={{0,16},{8,24},{16,0},{24,8},{32,48},{40,56},{48,32},{56,40},{64,80... | collective-permute-start | bytes 4128776 | tf_op jit(solution)/shard_map/ppermute | solution.py:90
  164.6 92.0 %all-to-all-start.1 = ((bf16[8,64,5376]{2,1,0:T(8,128)(2,1)}), bf16[8,64,5376]{2,1,0:T(8,128)(2,1)}, u32[]{:S(2)}, u32[]{:S(2)}) async-start(bf16[8,64,5376]{2,1,0:T(8,128)(2,1)} %bitcast.155), calls=%async_computation.1 | async-start | bytes 11010048 | tf_op jit(solution)/shard_map/all_to_all | solution.py:113
  197.7 4.6 %collective-permute-start = (bf16[168,256]{1,0:T(8,128)(2,1)S(1)}, bf16[168,256]{1,0:T(8,128)(2,1)S(1)}, u32[]{:S(2)}, u32[]{:S(2)}) collective-permute-start(bf16[168,256]{1,0:T(8,128)(2,1)S(1)} %convert_element_type.199), channel_id=1, source_target_pairs={{0,32},{8,40},{16,48},{24,56},{32,64},{40,72},{48,80},{56,88},{64,... | collective-permute-start | bytes 258056 | tf_op jit(solution)/shard_map/while/body/eval_jaxpr/ppermute | solution.py:75
  199.0 5.8 %collective-permute-start.1 = (bf16[168,256]{1,0:T(8,128)(2,1)S(1)}, bf16[168,256]{1,0:T(8,128)(2,1)S(1)}, u32[]{:S(2)}, u32[]{:S(2)}) collective-permute-start(bf16[168,256]{1,0:T(8,128)(2,1)S(1)} %convert_element_type.200), channel_id=1, source_target_pairs={{0,224},{8,232},{16,240},{24,248},{32,0},{40,8},{48,16},{56,24},{6... | collective-permute-start | bytes 258056 | tf_op jit(solution)/shard_map/while/body/eval_jaxpr/ppermute | solution.py:76
  204.8 4.6 %collective-permute-start = (bf16[168,256]{1,0:T(8,128)(2,1)S(1)}, bf16[168,256]{1,0:T(8,128)(2,1)S(1)}, u32[]{:S(2)}, u32[]{:S(2)}) collective-permute-start(bf16[168,256]{1,0:T(8,128)(2,1)S(1)} %convert_element_type.199), channel_id=1, source_target_pairs={{0,32},{8,40},{16,48},{24,56},{32,64},{40,72},{48,80},{56,88},{64,... | collective-permute-start | bytes 258056 | tf_op jit(solution)/shard_map/while/body/eval_jaxpr/ppermute | solution.py:75
  204.9 5.8 %collective-permute-start.1 = (bf16[168,256]{1,0:T(8,128)(2,1)S(1)}, bf16[168,256]{1,0:T(8,128)(2,1)S(1)}, u32[]{:S(2)}, u32[]{:S(2)}) collective-permute-start(bf16[168,256]{1,0:T(8,128)(2,1)S(1)} %convert_element_type.200), channel_id=1, source_target_pairs={{0,224},{8,232},{16,240},{24,248},{32,0},{40,8},{48,16},{56,24},{6... | collective-permute-start | bytes 258056 | tf_op jit(solution)/shard_map/while/body/eval_jaxpr/ppermute | solution.py:76
  210.8 4.6 %collective-permute-start = (bf16[168,256]{1,0:T(8,128)(2,1)S(1)}, bf16[168,256]{1,0:T(8,128)(2,1)S(1)}, u32[]{:S(2)}, u32[]{:S(2)}) collective-permute-start(bf16[168,256]{1,0:T(8,128)(2,1)S(1)} %convert_element_type.199), channel_id=1, source_target_pairs={{0,32},{8,40},{16,48},{24,56},{32,64},{40,72},{48,80},{56,88},{64,... | collective-permute-start | bytes 258056 | tf_op jit(solution)/shard_map/while/body/eval_jaxpr/ppermute | solution.py:75
  210.9 5.8 %collective-permute-start.1 = (bf16[168,256]{1,0:T(8,128)(2,1)S(1)}, bf16[168,256]{1,0:T(8,128)(2,1)S(1)}, u32[]{:S(2)}, u32[]{:S(2)}) collective-permute-start(bf16[168,256]{1,0:T(8,128)(2,1)S(1)} %convert_element_type.200), channel_id=1, source_target_pairs={{0,224},{8,232},{16,240},{24,248},{32,0},{40,8},{48,16},{56,24},{6... | collective-permute-start | bytes 258056 | tf_op jit(solution)/shard_map/while/body/eval_jaxpr/ppermute | solution.py:76
  216.7 5.3 %collective-permute-start = (bf16[168,256]{1,0:T(8,128)(2,1)S(1)}, bf16[168,256]{1,0:T(8,128)(2,1)S(1)}, u32[]{:S(2)}, u32[]{:S(2)}) collective-permute-start(bf16[168,256]{1,0:T(8,128)(2,1)S(1)} %convert_element_type.199), channel_id=1, source_target_pairs={{0,32},{8,40},{16,48},{24,56},{32,64},{40,72},{48,80},{56,88},{64,... | collective-permute-start | bytes 258056 | tf_op jit(solution)/shard_map/while/body/eval_jaxpr/ppermute | solution.py:75
  216.8 6.5 %collective-permute-start.1 = (bf16[168,256]{1,0:T(8,128)(2,1)S(1)}, bf16[168,256]{1,0:T(8,128)(2,1)S(1)}, u32[]{:S(2)}, u32[]{:S(2)}) collective-permute-start(bf16[168,256]{1,0:T(8,128)(2,1)S(1)} %convert_element_type.200), channel_id=1, source_target_pairs={{0,224},{8,232},{16,240},{24,248},{32,0},{40,8},{48,16},{56,24},{6... | collective-permute-start | bytes 258056 | tf_op jit(solution)/shard_map/while/body/eval_jaxpr/ppermute | solution.py:76
  223.4 4.9 %collective-permute-start = (bf16[168,256]{1,0:T(8,128)(2,1)S(1)}, bf16[168,256]{1,0:T(8,128)(2,1)S(1)}, u32[]{:S(2)}, u32[]{:S(2)}) collective-permute-start(bf16[168,256]{1,0:T(8,128)(2,1)S(1)} %convert_element_type.199), channel_id=1, source_target_pairs={{0,32},{8,40},{16,48},{24,56},{32,64},{40,72},{48,80},{56,88},{64,... | collective-permute-start | bytes 258056 | tf_op jit(solution)/shard_map/while/body/eval_jaxpr/ppermute | solution.py:75
  223.5 6.1 %collective-permute-start.1 = (bf16[168,256]{1,0:T(8,128)(2,1)S(1)}, bf16[168,256]{1,0:T(8,128)(2,1)S(1)}, u32[]{:S(2)}, u32[]{:S(2)}) collective-permute-start(bf16[168,256]{1,0:T(8,128)(2,1)S(1)} %convert_element_type.200), channel_id=1, source_target_pairs={{0,224},{8,232},{16,240},{24,248},{32,0},{40,8},{48,16},{56,24},{6... | collective-permute-start | bytes 258056 | tf_op jit(solution)/shard_map/while/body/eval_jaxpr/ppermute | solution.py:76
  229.7 4.6 %collective-permute-start = (bf16[168,256]{1,0:T(8,128)(2,1)S(1)}, bf16[168,256]{1,0:T(8,128)(2,1)S(1)}, u32[]{:S(2)}, u32[]{:S(2)}) collective-permute-start(bf16[168,256]{1,0:T(8,128)(2,1)S(1)} %convert_element_type.199), channel_id=1, source_target_pairs={{0,32},{8,40},{16,48},{24,56},{32,64},{40,72},{48,80},{56,88},{64,... | collective-permute-start | bytes 258056 | tf_op jit(solution)/shard_map/while/body/eval_jaxpr/ppermute | solution.py:75
  230.0 5.8 %collective-permute-start.1 = (bf16[168,256]{1,0:T(8,128)(2,1)S(1)}, bf16[168,256]{1,0:T(8,128)(2,1)S(1)}, u32[]{:S(2)}, u32[]{:S(2)}) collective-permute-start(bf16[168,256]{1,0:T(8,128)(2,1)S(1)} %convert_element_type.200), channel_id=1, source_target_pairs={{0,224},{8,232},{16,240},{24,248},{32,0},{40,8},{48,16},{56,24},{6... | collective-permute-start | bytes 258056 | tf_op jit(solution)/shard_map/while/body/eval_jaxpr/ppermute | solution.py:76
  235.8 4.6 %collective-permute-start = (bf16[168,256]{1,0:T(8,128)(2,1)S(1)}, bf16[168,256]{1,0:T(8,128)(2,1)S(1)}, u32[]{:S(2)}, u32[]{:S(2)}) collective-permute-start(bf16[168,256]{1,0:T(8,128)(2,1)S(1)} %convert_element_type.199), channel_id=1, source_target_pairs={{0,32},{8,40},{16,48},{24,56},{32,64},{40,72},{48,80},{56,88},{64,... | collective-permute-start | bytes 258056 | tf_op jit(solution)/shard_map/while/body/eval_jaxpr/ppermute | solution.py:75
  235.9 5.8 %collective-permute-start.1 = (bf16[168,256]{1,0:T(8,128)(2,1)S(1)}, bf16[168,256]{1,0:T(8,128)(2,1)S(1)}, u32[]{:S(2)}, u32[]{:S(2)}) collective-permute-start(bf16[168,256]{1,0:T(8,128)(2,1)S(1)} %convert_element_type.200), channel_id=1, source_target_pairs={{0,224},{8,232},{16,240},{24,248},{32,0},{40,8},{48,16},{56,24},{6... | collective-permute-start | bytes 258056 | tf_op jit(solution)/shard_map/while/body/eval_jaxpr/ppermute | solution.py:76
  241.8 19.2 %copy-start.2 = (f32[168,256]{1,0:T(8,128)}, f32[168,256]{1,0:T(8,128)S(1)}, u32[]{:S(2)}) copy-start(f32[168,256]{1,0:T(8,128)S(1)} %get-tuple-element.206) | copy-start | bytes 516100

commit v7 on v6

--- a/solution.py
+++ b/solution.py
@@ -96,7 +96,6 @@
     grid = full.reshape(outer, middle, inner, -1, width)
     grid = jnp.moveaxis(grid, 2, 0)
     grid = pair_scatter_sum(grid, axis, 1)
-    grid = pair_scatter_sum(jnp.moveaxis(grid, 1, 0), axis, inner)
     return ring_scatter_sum(grid, axis, outer, middle * inner)
 
 
@@ -293,7 +292,10 @@
         grad_cat, weight_cat, back_contract, preferred_element_type=jnp.float32
     ).astype(jnp.bfloat16)
     input_partial, hidden_late = lax.optimization_barrier((input_partial, gathered))
-    input_grad = exchange_sum(input_partial, "heads").astype(jnp.bfloat16)
+    heads_size = lax.axis_size("heads")
+    received = lax.all_to_all(
+        input_partial.reshape((heads_size, -1) + input_partial.shape[1:]), "heads", 0, 0
+    )
     summed = ctx_scatter_sum(
         (
             lax.dot_general(hidden_late, grad_cat, contract, preferred_element_type=jnp.float32)
@@ -302,6 +304,9 @@
         "ctx",
         (lax.axis_size("ctx") // 4, 2, 2),
     )
+    summed, received = lax.optimization_barrier((summed, received))
+    summed = pair_scatter_sum(summed, "ctx", 2)
+    input_grad = jnp.sum(received.astype(jnp.float32), axis=0).astype(jnp.bfloat16)
     query_weight_grad = summed[:, :query_width]
     key_weight_grad = summed[:, query_width : query_width + key_width]
     value_weight_grad = summed[:, query_width + key_width :]

time: 262 us -> 231 us (0.88)
  waiting for transfers between devices: 141 us -> 98.6 us
  local copies, waits for them, and re-layouts: 21.7 us -> 33.4 us
    ppermute x2, waiting for transfers between devices: 30.3 us -> 0.28 us  [pair_scatter_sum(): lax.ppermute(other.astype(jnp.bfloat16), axis, route).astype(jnp.float32)]
    all_to_all x1, waiting for transfers between devices: 14.1 us -> 3.42 us  [per_device(): lax.all_to_all(input_partial.reshape((heads_size, -1) + input_partial.sha...]
    squeeze x8, local copies, waits for them, and re-layouts: 0.38 us -> 9.98 us  [chunk(): lax.dynamic_index_in_dim(blocks, (digit - step * (k + 1)) % count, 0, kee...]
    ppermute x7, starting transfers between devices: 2 us -> 5.97 us  [advance(): lax.ppermute(up.astype(jnp.bfloat16), axis, route(1)).astype(jnp.float32)]
    ppermute x7, waiting for transfers between devices: 17.3 us -> 14.2 us  [advance(): lax.ppermute(up.astype(jnp.bfloat16), axis, route(1)).astype(jnp.float32)]
    add x2, other arithmetic: 5.38 us -> 2.61 us  [pair_scatter_sum(): own + lax.ppermute(other.astype(jnp.bfloat16), axis, route).astype(jnp.fl...]
  transfers between devices with their start and end apart: 22 -> 22, of which waited for: 22 -> 21; matrix products, arithmetic and copies ran while one was open for 7% -> 14% of each run, Pallas kernels for 0% -> 0%
where the time goes in v7:
time: 231 us; the launch traced here: 230 us
  waiting for transfers between devices  98.6 us (43%)
  starting transfers between devices  42.7 us (18%)
  matrix products  34.5 us (15%)
  local copies, waits for them, and re-layouts  33.4 us (14%)
  other arithmetic  19.2 us (8%)
    all_to_all x1, waiting for transfers between devices, gather_all(): received = lax.all_to_all(copies, axis, 0, 0)  52.4 us
    ppermute x4, waiting for transfers between devices, passed_along(): return lax.ppermute(block, axis, route)  15.9 us
    ppermute x7, waiting for transfers between devices, advance(): lax.ppermute(up.astype(jnp.bfloat16), axis, route(1)).astype(jnp.float32)  14.2 us
    ppermute x7, waiting for transfers between devices, advance(): lax.ppermute(down.astype(jnp.bfloat16), axis, route(-1)).astype(jnp.float32)  12.4 us
    ppermute x7, starting transfers between devices, advance(): lax.ppermute(down.astype(jnp.bfloat16), axis, route(-1)).astype(jnp.float32)  11.3 us
    unnamed x50, local copies, waits for them, and re-layouts  10.4 us
    squeeze x8, local copies, waits for them, and re-layouts, chunk(): lax.dynamic_index_in_dim(blocks, (digit - step * (k + 1)) % count, 0, kee...  9.98 us
    ppermute x4, starting transfers between devices, passed_along(): return lax.ppermute(block, axis, route)  8.65 us
  transfers between devices with their start and end apart: 22, of which 21 were waited for; matrix products, arithmetic and copies ran while one was open for 14% of the time, Pallas kernels for 0%

profile of v7, /device:TPU:96, one launch (start us, length us, event | category | flops | bytes accessed | tf_op | source)
XLA Modules:
  0.0 230.1 jit_solution(9399893300585711226)
XLA Ops:
  0.6 3.8 %broadcast_in_dim.71 = bf16[8,64,5376]{2,1,0:T(8,128)(2,1)} broadcast(bf16[64,5376]{1,0:T(8,128)(2,1)} %param.9), dimensions={1,2} | broadcast | bytes 6193152 | tf_op jit(solution)/shard_map/broadcast_in_dim | solution.py:104
  4.5 7.1 %all-to-all-start = ((bf16[8,64,5376]{2,1,0:T(8,128)(2,1)}), bf16[8,64,5376]{2,1,0:T(8,128)(2,1)}, u32[]{:S(2)}, u32[]{:S(2)}) async-start(bf16[8,64,5376]{2,1,0:T(8,128)(2,1)} %broadcast_in_dim.71), calls=%async_computation | async-start | bytes 11010048 | tf_op jit(solution)/shard_map/all_to_all | solution.py:105
  13.6 1.2 fusion.7
  14.8 3.5 %constant_dynamic-update-slice_fusion.2 = bf16[5376,512]{1,0:T(8,128)(2,1)} fusion(bf16[5376,256]{1,0:T(8,128)(2,1)} %param.10), kind=kLoop, calls=%fused_computation.95 | loop fusion | bytes 5505024
  18.3 1.2 constant_dynamic-update-slice_fusion.1
  19.5 2.6 %constant_dynamic-update-slice_fusion = bf16[5376,512]{1,0:T(8,128)(2,1)} fusion(bf16[5376,512]{1,0:T(8,128)(2,1)} %constant_dynamic-update-slice_fusion.1, bf16[5376,128]{1,0:T(8,128)(2,1)} %param.12), kind=kLoop, calls=%fused_computation.93 | loop fusion | bytes 2752512 | tf_op jit(solution)/shard_map/concatenate | solution.py:222
  22.2 52.4 %all-to-all-done = bf16[8,64,5376]{2,1,0:T(8,128)(2,1)} async-done(((bf16[8,64,5376]{2,1,0:T(8,128)(2,1)}), bf16[8,64,5376]{2,1,0:T(8,128)(2,1)}, u32[]{:S(2)}, u32[]{:S(2)}) %all-to-all-start) | async-done | bytes 5505056 | tf_op jit(solution)/shard_map/all_to_all | solution.py:105
  74.6 6.8 %convolution_bitcast_fusion.2 = f32[512,512]{0,1:T(8,128)S(1)} fusion(bf16[5376,512]{1,0:T(8,128)(2,1)} %constant_dynamic-update-slice_fusion, bf16[512,5376]{1,0:T(8,128)(2,1)} %bitcast.4), kind=kOutput, calls=%fused_computation.28 | convolution fusion | flops 2818572288 | bytes 12058624 | tf_op jit(solution)/shard_map/dot_general | solution.py:223
  82.9 2.5 %collective-permute-start.2 = (bf16[2,512,128]{1,2,0:T(8,128)(2,1)}, bf16[2,512,128]{1,2,0:T(8,128)(2,1)}, u32[]{:S(2)}, u32[]{:S(2)}) collective-permute-start(bf16[2,512,128]{1,2,0:T(8,128)(2,1)} %pad_maximum_fusion.3), channel_id=1, source_target_pairs={{0,16},{8,24},{16,32},{24,40},{32,48},{40,56},{48,64},{56,72},{64,... | collective-permute-start | bytes 786440 | tf_op jit(solution)/shard_map/ppermute | solution.py:18
  85.4 2.1 collective-permute-start.3
  88.6 6.6 %collective-permute-done.2 = bf16[2,512,128]{1,2,0:T(8,128)(2,1)} collective-permute-done((bf16[2,512,128]{1,2,0:T(8,128)(2,1)}, bf16[2,512,128]{1,2,0:T(8,128)(2,1)}, u32[]{:S(2)}, u32[]{:S(2)}) %collective-permute-start.2) | collective-permute-done | bytes 262176 | tf_op jit(solution)/shard_map/ppermute | solution.py:18
  95.2 1.2 collective-permute-done.3
  97.4 1.2 fusion.2
  98.7 1.3 exponential_reduce_fusion
  100.0 2.7 %bitcast_convert_fusion = (f32[2,512,128]{1,2,0:T(8,128)S(1)}, bf16[128,2,512]{2,0,1:T(8,128)(2,1)}) fusion(f32[1536,512,2]{1,0,2:T(8,128)S(1)} %get-tuple-element.242, f32[2,512]{1,0:T(2,128)S(1)} %log_add_fusion, pred[512,1536]{0,1:T(8,128)(4,1)S(1)} %fusion.7, bf16[2,1536,128]{1,2,0:T(8,128)(2,1)S(1)} %maximum_maximum_fusion), kind=kOutput, calls=%fused_computation.68 | convolution fusion | flops 409206784 | bytes 8261632 | tf_op jit(solution)/shard_map/while/body/eval_jaxpr/kgqj,jkd->qkgd/dot_general | solution.py:163
  103.0 1.3 multiply_reduce_fusion
  104.3 1.2 copy.54
  105.5 4.9 %convolution_bitcast_fusion = f32[1,1536,128]{1,2,0:T(8,128)S(1)} fusion(bf16[512,2,128]{0,2,1:T(8,128)(2,1)} %copy.42, f32[1536,512,2]{1,0,2:T(8,128)} %copy-done.1, f32[2,512]{1,0:T(2,128)S(1)} %log_add_fusion, pred[512,1536]{0,1:T(8,128)(4,1)S(1)} %fusion.7), kind=kOutput, calls=%fused_computation.22 | convolution fusion | flops 408944640 | bytes 8130560 | tf_op jit(solution)/shard_map/while/body/eval_jaxpr/kgqj,qkgd->jkd/dot_general | solution.py:202
  110.5 2.4 %fusion.4 = bf16[2,512,1536]{1,2,0:T(8,128)(2,1)S(1)} fusion(bf16[512,2,128]{0,2,1:T(8,128)(2,1)S(1)} %copy-done.18, f32[1536,512,2]{1,0,2:T(8,128)S(1)} %bitcast.153, f32[2,512]{1,0:T(2,128)S(1)} %copy.54, f32[2,512]{1,0:T(2,128)S(1)} %log_add_fusion, pred[512,1536]{0,1:T(8,128)(4,1)S(1)} %fusion.7, bf16[2,1536,128]{1,2,0:T(8,128)(2,1)S(1)} %copy-done.6), kind=kOutput, calls=%fused_computation.17 | convolution fusion | flops 412090368 | bytes 10887168 | tf_op jit(solution)/shard_map/while/body/eval_jaxpr/qkgd,jkd->kgqj/dot_general | solution.py:192
  113.0 1.4 fusion.9
  114.4 1.2 convolution_bitcast_fusion.1
  116.8 1.9 collective-permute-start.4
  118.7 2.1 collective-permute-start.5
  121.9 2.1 collective-permute-done.4
  124.0 6.1 %collective-permute-done.5 = bf16[2,512,128]{1,2,0:T(8,128)(2,1)} collective-permute-done((bf16[2,512,128]{1,2,0:T(8,128)(2,1)}, bf16[2,512,128]{1,2,0:T(8,128)(2,1)}, u32[]{:S(2)}, u32[]{:S(2)}) %collective-permute-start.5) | collective-permute-done | bytes 262176 | tf_op jit(solution)/shard_map/ppermute | solution.py:18
  132.1 7.5 %convolution_convert_fusion = bf16[512,5376]{1,0:T(8,128)(2,1)} fusion(bf16[5376,512]{1,0:T(8,128)(2,1)} %constant_dynamic-update-slice_fusion, bf16[512,128]{0,1:T(8,128)(2,1)S(1)} %fusion.34, bf16[512,128]{0,1:T(8,128)(2,1)S(1)} %fusion.35, bf16[512,256]{0,1:T(8,128)(2,1)S(1)} %bitcast.159), kind=kOutput, calls=%fused_computation.5 | convolution fusion | flops 2822897664 | bytes 11534336 | tf_op jit(solution)/shard_map/dot_general | solution.py:291
  139.6 6.4 %multiply_convert_fusion = bf16[5376,512]{1,0:T(8,128)(2,1)S(1)} fusion(bf16[512,5376]{1,0:T(8,128)(2,1)} %bitcast.4, bf16[512,128]{0,1:T(8,128)(2,1)S(1)} %fusion.34, bf16[512,128]{0,1:T(8,128)(2,1)S(1)} %fusion.35, bf16[512,256]{0,1:T(8,128)(2,1)S(1)} %bitcast.160), kind=kOutput, calls=%fused_computation.4 | convolution fusion | flops 2825650176 | bytes 11534336 | tf_op jit(solution)/shard_map/dot_general | solution.py:301
  145.9 2.4 %copy-done.2 = bf16[5376,512]{1,0:T(8,128)(2,1)} copy-done((bf16[5376,512]{1,0:T(8,128)(2,1)}, bf16[5376,512]{1,0:T(8,128)(2,1)S(1)}, u32[]{:S(2)}) %copy-start.2) | copy-done | bytes 5505048
  148.3 1.7 dynamic-slice_bitcast_fusion.2
  150.0 5.0 %all-to-all-start.1 = ((bf16[8,64,5376]{2,1,0:T(8,128)(2,1)}), bf16[8,64,5376]{2,1,0:T(8,128)(2,1)}, u32[]{:S(2)}, u32[]{:S(2)}) async-start(bf16[8,64,5376]{2,1,0:T(8,128)(2,1)} %bitcast.154), calls=%async_computation.1 | async-start | bytes 11010048 | tf_op jit(solution)/shard_map/all_to_all | solution.py:296
  155.3 2.6 %convert_add_fusion = f32[8,2,168,512]{3,2,1,0:T(8,128)S(1)} fusion(bf16[8,2,168,512]{3,2,1,0:T(8,128)(2,1)S(1)} %collective-permute-done.6, bf16[8,2,2,168,512]{4,3,2,1,0:T(8,128)(2,1)} %bitcast.156, s32[]{:T(128)S(6)} %select_n.118), kind=kLoop, calls=%fused_computation.13 | loop fusion | flops 4128768 | bytes 11010052 | tf_op jit(solution)/shard_map/add | solution.py:90
  158.1 2.2 copy-done
  160.3 55.0 %while.11 = (s32[]{:T(128)}, f32[2,168,256]{2,1,0:T(8,128)S(1)}, f32[2,168,256]{2,1,0:T(8,128)S(1)}, s32[]{:T(128)}, f32[8,2,168,512]{3,2,1,0:T(8,128)}, /*index...) while((s32[]{:T(128)}, f32[2,168,256]{2,1,0:T(8,128)S(1)}, ...), condition=%wide.region_7.8_spmd, body=%wide.region_6.7_spmd.sunk | while | flops 516130 | bytes 6881811 | solution.py:79
  160.3 4.2 %collective-permute-start = (bf16[2,168,256]{2,1,0:T(8,128)(2,1)S(1)}, bf16[2,168,256]{2,1,0:T(8,128)(2,1)S(1)}, u32[]{:S(2)}, u32[]{:S(2)}) collective-permute-start(bf16[2,168,256]{2,1,0:T(8,128)(2,1)S(1)} %convert_element_type.199), channel_id=1, source_target_pairs={{0,32},{8,40},{16,48},{24,56},{32,64},{40,72},{48,80},{56,88},{64,... | collective-permute-start | bytes 516104 | tf_op jit(solution)/shard_map/while/body/eval_jaxpr/ppermute | solution.py:75
  164.6 1.4 dynamic-slice_bitcast_fusion.6
  166.0 2.5 %collective-permute-done = bf16[2,168,256]{2,1,0:T(8,128)(2,1)S(1)} collective-permute-done((bf16[2,168,256]{2,1,0:T(8,128)(2,1)S(1)}, bf16[2,168,256]{2,1,0:T(8,128)(2,1)S(1)}, u32[]{:S(2)}, u32[]{:S(2)}) %collective-permute-start) | collective-permute-done | bytes 172064 | tf_op jit(solution)/shard_map/while/body/eval_jaxpr/ppermute | solution.py:75
  168.5 3.5 %collective-permute-done.1 = bf16[2,168,256]{2,1,0:T(8,128)(2,1)S(1)} collective-permute-done((bf16[2,168,256]{2,1,0:T(8,128)(2,1)S(1)}, bf16[2,168,256]{2,1,0:T(8,128)(2,1)S(1)}, u32[]{:S(2)}, u32[]{:S(2)}) %collective-permute-start.1) | collective-permute-done | bytes 172064 | tf_op jit(solution)/shard_map/while/body/eval_jaxpr/ppermute | solution.py:76
  172.4 1.9 collective-permute-start.1
  174.3 1.4 dynamic-slice_bitcast_fusion.6
  175.7 1.9 collective-permute-done
  177.7 1.5 collective-permute-done.1
  179.6 1.9 collective-permute-start.1
  181.5 1.4 dynamic-slice_bitcast_fusion.6
  182.9 1.9 collective-permute-done
  184.8 1.5 collective-permute-done.1
  186.5 2.1 collective-permute-start.1
  188.6 1.4 dynamic-slice_bitcast_fusion.6
  190.0 1.9 collective-permute-done
  192.0 1.3 collective-permute-done.1
  193.4 2.1 collective-permute-start.1
  195.5 1.4 dynamic-slice_bitcast_fusion.6
  196.9 1.9 collective-permute-done
  198.8 1.3 collective-permute-done.1
  200.3 2.1 collective-permute-start.1
  202.4 1.4 dynamic-slice_bitcast_fusion.6
  203.8 2.3 %collective-permute-done = bf16[2,168,256]{2,1,0:T(8,128)(2,1)S(1)} collective-permute-done((bf16[2,168,256]{2,1,0:T(8,128)(2,1)S(1)}, bf16[2,168,256]{2,1,0:T(8,128)(2,1)S(1)}, u32[]{:S(2)}, u32[]{:S(2)}) %collective-permute-start) | collective-permute-done | bytes 172064 | tf_op jit(solution)/shard_map/while/body/eval_jaxpr/ppermute | solution.py:75
  206.2 1.3 collective-permute-done.1
  208.5 1.3 collective-permute-start.1
  209.8 1.4 dynamic-slice_bitcast_fusion.6
  211.2 1.9 collective-permute-done
  213.1 2.1 collective-permute-done.1
  215.3 3.4 %all-to-all-done.1 = bf16[8,64,5376]{2,1,0:T(8,128)(2,1)} async-done(((bf16[8,64,5376]{2,1,0:T(8,128)(2,1)}), bf16[8,64,5376]{2,1,0:T(8,128)(2,1)}, u32[]{:S(2)}, u32[]{:S(2)}) %all-to-all-start.1) | async-done | bytes 5505056 | tf_op jit(solution)/shard_map/all_to_all | solution.py:296
  218.8 4.7 %collective-permute-start.7 = (bf16[168,512]{1,0:T(8,128)(2,1)S(1)}, bf16[168,512]{1,0:T(8,128)(2,1)S(1)}, u32[]{:S(2)}, u32[]{:S(2)}) collective-permute-start(bf16[168,512]{1,0:T(8,128)(2,1)S(1)} %fusion.26), channel_id=1, source_target_pairs={{0,16},{8,24},{16,0},{24,8},{32,48},{40,56},{48,32},{56,40},{64,80... | collective-permute-start | bytes 516104 | tf_op jit(solution)/shard_map/ppermute | solution.py:90
  224.3 4.4 %reduce_sum.71 = bf16[64,5376]{1,0:T(8,128)(2,1)} reduce(bf16[8,64,5376]{2,1,0:T(8,128)(2,1)} %all-to-all-done.1, bf16[]{:T(256)} %constant.230.clone.1), dimensions={0}, to_apply=%region_8.9 | reduce | flops 2408448 | bytes 6193154 | tf_op jit(solution)/shard_map/reduce_sum | solution.py:309
  (131 shorter events, 15.5 us)
Async XLA Ops:
  4.5 7.1 %copy-start.16 = (bf16[512,256]{1,0:T(8,128)(2,1)S(1)}, bf16[512,256]{1,0:T(8,128)(2,1)}, u32[]{:S(2)}) copy-start(bf16[512,256]{1,0:T(8,128)(2,1)} %param.15) | copy-start | bytes 786436
  4.5 70.1 %all-to-all-start = ((bf16[8,64,5376]{2,1,0:T(8,128)(2,1)}), bf16[8,64,5376]{2,1,0:T(8,128)(2,1)}, u32[]{:S(2)}, u32[]{:S(2)}) async-start(bf16[8,64,5376]{2,1,0:T(8,128)(2,1)} %broadcast_in_dim.71), calls=%async_computation | async-start | bytes 11010048 | tf_op jit(solution)/shard_map/all_to_all | solution.py:105
  11.5 6.8 %copy-start.15 = (bf16[5376,128]{1,0:T(8,128)(2,1)S(1)}, bf16[5376,128]{1,0:T(8,128)(2,1)}, u32[]{:S(2)}) copy-start(bf16[5376,128]{1,0:T(8,128)(2,1)} %param.11) | copy-start | bytes 4128772
  13.5 74.5 %copy-start.9 = (f32[512,64]{1,0:T(8,128)}, f32[512,64]{1,0:T(8,128)S(1)}, u32[]{:S(2)}) copy-start(f32[512,64]{1,0:T(8,128)S(1)} %get-tuple-element.239) | copy-start | bytes 393220
  13.6 74.5 %copy-start.11 = (f32[512,64]{1,0:T(8,128)}, f32[512,64]{1,0:T(8,128)S(1)}, u32[]{:S(2)}) copy-start(f32[512,64]{1,0:T(8,128)S(1)} %get-tuple-element.240) | copy-start | bytes 393220
  74.6 6.9 %copy-start.19 = (f32[128]{0:T(128)S(1)}, f32[128]{0:T(128)}, u32[]{:S(2)}) copy-start(f32[128]{0:T(128)} %param.14) | copy-start | bytes 1540
  74.6 13.3 %copy-start.20 = (f32[128]{0:T(128)S(1)}, f32[128]{0:T(128)}, u32[]{:S(2)}) copy-start(f32[128]{0:T(128)} %param.13) | copy-start | bytes 1540
  81.4 6.2 %copy-start.3 = (f32[512,512]{0,1:T(8,128)}, f32[512,512]{0,1:T(8,128)S(1)}, u32[]{:S(2)}) copy-start(f32[512,512]{0,1:T(8,128)S(1)} %convolution_bitcast_fusion.2) | copy-start | bytes 3145732
  82.9 12.3 %collective-permute-start.2 = (bf16[2,512,128]{1,2,0:T(8,128)(2,1)}, bf16[2,512,128]{1,2,0:T(8,128)(2,1)}, u32[]{:S(2)}, u32[]{:S(2)}) collective-permute-start(bf16[2,512,128]{1,2,0:T(8,128)(2,1)} %pad_maximum_fusion.3), channel_id=1, source_target_pairs={{0,16},{8,24},{16,32},{24,40},{32,48},{40,56},{48,64},{56,72},{64,... | collective-permute-start | bytes 786440 | tf_op jit(solution)/shard_map/ppermute | solution.py:18
  85.4 11.0 %collective-permute-start.3 = (bf16[2,512,128]{1,2,0:T(8,128)(2,1)}, bf16[2,512,128]{1,2,0:T(8,128)(2,1)}, u32[]{:S(2)}, u32[]{:S(2)}) collective-permute-start(bf16[2,512,128]{1,2,0:T(8,128)(2,1)} %pad_maximum_fusion.3), channel_id=1, source_target_pairs={{0,8},{8,16},{16,24},{24,32},{32,40},{40,48},{48,56},{56,64},{64,7... | collective-permute-start | bytes 786440 | tf_op jit(solution)/shard_map/ppermute | solution.py:18
  88.5 8.9 %copy-start.13 = (bf16[512,2,128]{2,0,1:T(8,128)(2,1)}, bf16[512,2,128]{2,0,1:T(8,128)(2,1)S(1)}, u32[]{:S(2)}) copy-start(bf16[512,2,128]{2,0,1:T(8,128)(2,1)S(1)} %fusion.14) | copy-start | bytes 786436
  97.4 2.6 %copy-start.5 = (bf16[2,1536,128]{1,2,0:T(8,128)(2,1)}, bf16[2,1536,128]{1,2,0:T(8,128)(2,1)S(1)}, u32[]{:S(2)}) copy-start(bf16[2,1536,128]{1,2,0:T(8,128)(2,1)S(1)} %maximum_maximum_fusion) | copy-start | bytes 2359300
  98.7 4.0 %copy-start.1 = (f32[1536,512,2]{1,0,2:T(8,128)}, f32[1536,512,2]{1,0,2:T(8,128)S(1)}, u32[]{:S(2)}) copy-start(f32[1536,512,2]{1,0,2:T(8,128)S(1)} %get-tuple-element.242) | copy-start | bytes 18874372
  104.3 6.2 %slice-start = ((s8[6291456]{0:T(1024)(128)(4,1)}), s8[2097152]{0:T(1024)(128)(4,1)S(1)}, s32[]{:S(2)}) async-start(s8[6291456]{0:T(1024)(128)(4,1)} %bitcast.152), calls=%async_computation.2 | async-start | bytes 4194304
  105.5 5.0 %slice-start.1 = ((s8[6291456]{0:T(1024)(128)(4,1)}), s8[4194304]{0:T(1024)(128)(4,1)S(1)}, s32[]{:S(2)}) async-start(s8[6291456]{0:T(1024)(128)(4,1)} %bitcast.152), calls=%async_computation.3 | async-start | bytes 8388608
  105.5 5.0 %copy-start.6 = (bf16[2,1536,128]{1,2,0:T(8,128)(2,1)S(1)}, bf16[2,1536,128]{1,2,0:T(8,128)(2,1)}, u32[]{:S(2)}) copy-start(bf16[2,1536,128]{1,2,0:T(8,128)(2,1)} %copy-done.5) | copy-start | bytes 2359300
  105.5 5.0 %copy-start.18 = (bf16[512,2,128]{0,2,1:T(8,128)(2,1)S(1)}, bf16[512,2,128]{0,2,1:T(8,128)(2,1)}, u32[]{:S(2)}) copy-start(bf16[512,2,128]{0,2,1:T(8,128)(2,1)} %copy.42) | copy-start | bytes 786436
  110.5 5.3 %copy-start.7 = (f32[1,1536,128]{1,2,0:T(8,128)}, f32[1,1536,128]{1,2,0:T(8,128)S(1)}, u32[]{:S(2)}) copy-start(f32[1,1536,128]{1,2,0:T(8,128)S(1)} %convolution_bitcast_fusion) | copy-start | bytes 2359300
  110.5 3.9 %copy-start.14 = (bf16[512,2,128]{2,0,1:T(8,128)(2,1)S(1)}, bf16[512,2,128]{2,0,1:T(8,128)(2,1)}, u32[]{:S(2)}) copy-start(bf16[512,2,128]{2,0,1:T(8,128)(2,1)} %copy-done.13) | copy-start | bytes 786436
  113.0 2.6 %copy-start.10 = (f32[512,64]{1,0:T(8,128)S(1)}, f32[512,64]{1,0:T(8,128)}, u32[]{:S(2)}) copy-start(f32[512,64]{1,0:T(8,128)} %copy-done.9) | copy-start | bytes 393220
  113.0 2.6 %copy-start.12 = (f32[512,64]{1,0:T(8,128)S(1)}, f32[512,64]{1,0:T(8,128)}, u32[]{:S(2)}) copy-start(f32[512,64]{1,0:T(8,128)} %copy-done.11) | copy-start | bytes 393220
  115.8 16.0 %copy-start.4 = (f32[512,512]{0,1:T(8,128)S(1)}, f32[512,512]{0,1:T(8,128)}, u32[]{:S(2)}) copy-start(f32[512,512]{0,1:T(8,128)} %copy-done.3) | copy-start | bytes 3145732
  116.0 14.1 %copy-start.8 = (f32[1,1536,128]{1,2,0:T(8,128)S(1)}, f32[1,1536,128]{1,2,0:T(8,128)}, u32[]{:S(2)}) copy-start(f32[1,1536,128]{1,2,0:T(8,128)} %copy-done.7) | copy-start | bytes 2359300
  116.8 7.2 %collective-permute-start.4 = (bf16[2,512,128]{1,2,0:T(8,128)(2,1)}, bf16[2,512,128]{1,2,0:T(8,128)(2,1)}, u32[]{:S(2)}, u32[]{:S(2)}) collective-permute-start(bf16[2,512,128]{1,2,0:T(8,128)(2,1)} %get-tuple-element.231), channel_id=1, source_target_pairs={{8,0},{16,8},{24,16},{32,24},{40,32},{48,40},{56,48},{64,56},{72,6... | collective-permute-start | bytes 786440 | tf_op jit(solution)/shard_map/ppermute | solution.py:18
  118.7 11.3 %collective-permute-start.5 = (bf16[2,512,128]{1,2,0:T(8,128)(2,1)}, bf16[2,512,128]{1,2,0:T(8,128)(2,1)}, u32[]{:S(2)}, u32[]{:S(2)}) collective-permute-start(bf16[2,512,128]{1,2,0:T(8,128)(2,1)} %get-tuple-element.232), channel_id=1, source_target_pairs={{16,0},{24,8},{32,16},{40,24},{48,32},{56,40},{64,48},{72,56},{80,... | collective-permute-start | bytes 786440 | tf_op jit(solution)/shard_map/ppermute | solution.py:18
  145.9 2.4 %copy-start.2 = (bf16[5376,512]{1,0:T(8,128)(2,1)}, bf16[5376,512]{1,0:T(8,128)(2,1)S(1)}, u32[]{:S(2)}) copy-start(bf16[5376,512]{1,0:T(8,128)(2,1)S(1)} %multiply_convert_fusion) | copy-start | bytes 16515076
  150.0 5.3 %collective-permute-start.6 = (bf16[8,2,168,512]{3,2,1,0:T(8,128)(2,1)}, bf16[8,2,168,512]{3,2,1,0:T(8,128)(2,1)S(1)}, u32[]{:S(2)}, u32[]{:S(2)}) collective-permute-start(bf16[8,2,168,512]{3,2,1,0:T(8,128)(2,1)} %dynamic-slice_bitcast_fusion.2), channel_id=1, source_target_pairs={{0,8},{8,0},{16,24},{24,16},{32,40},{40,32},{48,56},{56,48},{64,72... | collective-permute-start | bytes 8257544 | tf_op jit(solution)/shard_map/ppermute | solution.py:90
  150.0 68.7 %all-to-all-start.1 = ((bf16[8,64,5376]{2,1,0:T(8,128)(2,1)}), bf16[8,64,5376]{2,1,0:T(8,128)(2,1)}, u32[]{:S(2)}, u32[]{:S(2)}) async-start(bf16[8,64,5376]{2,1,0:T(8,128)(2,1)} %bitcast.154), calls=%async_computation.1 | async-start | bytes 11010048 | tf_op jit(solution)/shard_map/all_to_all | solution.py:296
  157.9 2.4 %copy-start = (f32[8,2,168,512]{3,2,1,0:T(8,128)}, f32[8,2,168,512]{3,2,1,0:T(8,128)S(1)}, u32[]{:S(2)}) copy-start(f32[8,2,168,512]{3,2,1,0:T(8,128)S(1)} %convert_add_fusion) | copy-start | bytes 16515076
  160.3 63.2 %copy-start.17 = (bf16[128,2,512]{2,0,1:T(8,128)(2,1)S(1)}, bf16[128,2,512]{2,0,1:T(8,128)(2,1)}, u32[]{:S(2)}) copy-start(bf16[128,2,512]{2,0,1:T(8,128)(2,1)} %get-tuple-element.244) | copy-start | bytes 786436
  160.3 8.2 %collective-permute-start = (bf16[2,168,256]{2,1,0:T(8,128)(2,1)S(1)}, bf16[2,168,256]{2,1,0:T(8,128)(2,1)S(1)}, u32[]{:S(2)}, u32[]{:S(2)}) collective-permute-start(bf16[2,168,256]{2,1,0:T(8,128)(2,1)S(1)} %convert_element_type.199), channel_id=1, source_target_pairs={{0,32},{8,40},{16,48},{24,56},{32,64},{40,72},{48,80},{56,88},{64,... | collective-permute-start | bytes 516104 | tf_op jit(solution)/shard_map/while/body/eval_jaxpr/ppermute | solution.py:75
  164.5 7.5 %collective-permute-start.1 = (bf16[2,168,256]{2,1,0:T(8,128)(2,1)S(1)}, bf16[2,168,256]{2,1,0:T(8,128)(2,1)S(1)}, u32[]{:S(2)}, u32[]{:S(2)}) collective-permute-start(bf16[2,168,256]{2,1,0:T(8,128)(2,1)S(1)} %convert_element_type.200), channel_id=1, source_target_pairs={{0,224},{8,232},{16,240},{24,248},{32,0},{40,8},{48,16},{56,24},{6... | collective-permute-start | bytes 516104 | tf_op jit(solution)/shard_map/while/body/eval_jaxpr/ppermute | solution.py:76
  172.1 5.6 %collective-permute-start = (bf16[2,168,256]{2,1,0:T(8,128)(2,1)S(1)}, bf16[2,168,256]{2,1,0:T(8,128)(2,1)S(1)}, u32[]{:S(2)}, u32[]{:S(2)}) collective-permute-start(bf16[2,168,256]{2,1,0:T(8,128)(2,1)S(1)} %convert_element_type.199), channel_id=1, source_target_pairs={{0,32},{8,40},{16,48},{24,56},{32,64},{40,72},{48,80},{56,88},{64,... | collective-permute-start | bytes 516104 | tf_op jit(solution)/shard_map/while/body/eval_jaxpr/ppermute | solution.py:75
  172.4 6.8 %collective-permute-start.1 = (bf16[2,168,256]{2,1,0:T(8,128)(2,1)S(1)}, bf16[2,168,256]{2,1,0:T(8,128)(2,1)S(1)}, u32[]{:S(2)}, u32[]{:S(2)}) collective-permute-start(bf16[2,168,256]{2,1,0:T(8,128)(2,1)S(1)} %convert_element_type.200), channel_id=1, source_target_pairs={{0,224},{8,232},{16,240},{24,248},{32,0},{40,8},{48,16},{56,24},{6... | collective-permute-start | bytes 516104 | tf_op jit(solution)/shard_map/while/body/eval_jaxpr/ppermute | solution.py:76
  179.3 5.5 %collective-permute-start = (bf16[2,168,256]{2,1,0:T(8,128)(2,1)S(1)}, bf16[2,168,256]{2,1,0:T(8,128)(2,1)S(1)}, u32[]{:S(2)}, u32[]{:S(2)}) collective-permute-start(bf16[2,168,256]{2,1,0:T(8,128)(2,1)S(1)} %convert_element_type.199), channel_id=1, source_target_pairs={{0,32},{8,40},{16,48},{24,56},{32,64},{40,72},{48,80},{56,88},{64,... | collective-permute-start | bytes 516104 | tf_op jit(solution)/shard_map/while/body/eval_jaxpr/ppermute | solution.py:75
  179.6 6.7 %collective-permute-start.1 = (bf16[2,168,256]{2,1,0:T(8,128)(2,1)S(1)}, bf16[2,168,256]{2,1,0:T(8,128)(2,1)S(1)}, u32[]{:S(2)}, u32[]{:S(2)}) collective-permute-start(bf16[2,168,256]{2,1,0:T(8,128)(2,1)S(1)} %convert_element_type.200), channel_id=1, source_target_pairs={{0,224},{8,232},{16,240},{24,248},{32,0},{40,8},{48,16},{56,24},{6... | collective-permute-start | bytes 516104 | tf_op jit(solution)/shard_map/while/body/eval_jaxpr/ppermute | solution.py:76
  186.4 5.5 %collective-permute-start = (bf16[2,168,256]{2,1,0:T(8,128)(2,1)S(1)}, bf16[2,168,256]{2,1,0:T(8,128)(2,1)S(1)}, u32[]{:S(2)}, u32[]{:S(2)}) collective-permute-start(bf16[2,168,256]{2,1,0:T(8,128)(2,1)S(1)} %convert_element_type.199), channel_id=1, source_target_pairs={{0,32},{8,40},{16,48},{24,56},{32,64},{40,72},{48,80},{56,88},{64,... | collective-permute-start | bytes 516104 | tf_op jit(solution)/shard_map/while/body/eval_jaxpr/ppermute | solution.py:75
  186.5 6.7 %collective-permute-start.1 = (bf16[2,168,256]{2,1,0:T(8,128)(2,1)S(1)}, bf16[2,168,256]{2,1,0:T(8,128)(2,1)S(1)}, u32[]{:S(2)}, u32[]{:S(2)}) collective-permute-start(bf16[2,168,256]{2,1,0:T(8,128)(2,1)S(1)} %convert_element_type.200), channel_id=1, source_target_pairs={{0,224},{8,232},{16,240},{24,248},{32,0},{40,8},{48,16},{56,24},{6... | collective-permute-start | bytes 516104 | tf_op jit(solution)/shard_map/while/body/eval_jaxpr/ppermute | solution.py:76
  193.3 5.5 %collective-permute-start = (bf16[2,168,256]{2,1,0:T(8,128)(2,1)S(1)}, bf16[2,168,256]{2,1,0:T(8,128)(2,1)S(1)}, u32[]{:S(2)}, u32[]{:S(2)}) collective-permute-start(bf16[2,168,256]{2,1,0:T(8,128)(2,1)S(1)} %convert_element_type.199), channel_id=1, source_target_pairs={{0,32},{8,40},{16,48},{24,56},{32,64},{40,72},{48,80},{56,88},{64,... | collective-permute-start | bytes 516104 | tf_op jit(solution)/shard_map/while/body/eval_jaxpr/ppermute | solution.py:75
  193.4 6.7 %collective-permute-start.1 = (bf16[2,168,256]{2,1,0:T(8,128)(2,1)S(1)}, bf16[2,168,256]{2,1,0:T(8,128)(2,1)S(1)}, u32[]{:S(2)}, u32[]{:S(2)}) collective-permute-start(bf16[2,168,256]{2,1,0:T(8,128)(2,1)S(1)} %convert_element_type.200), channel_id=1, source_target_pairs={{0,224},{8,232},{16,240},{24,248},{32,0},{40,8},{48,16},{56,24},{6... | collective-permute-start | bytes 516104 | tf_op jit(solution)/shard_map/while/body/eval_jaxpr/ppermute | solution.py:76
  200.2 6.0 %collective-permute-start = (bf16[2,168,256]{2,1,0:T(8,128)(2,1)S(1)}, bf16[2,168,256]{2,1,0:T(8,128)(2,1)S(1)}, u32[]{:S(2)}, u32[]{:S(2)}) collective-permute-start(bf16[2,168,256]{2,1,0:T(8,128)(2,1)S(1)} %convert_element_type.199), channel_id=1, source_target_pairs={{0,32},{8,40},{16,48},{24,56},{32,64},{40,72},{48,80},{56,88},{64,... | collective-permute-start | bytes 516104 | tf_op jit(solution)/shard_map/while/body/eval_jaxpr/ppermute | solution.py:75
  200.3 7.2 %collective-permute-start.1 = (bf16[2,168,256]{2,1,0:T(8,128)(2,1)S(1)}, bf16[2,168,256]{2,1,0:T(8,128)(2,1)S(1)}, u32[]{:S(2)}, u32[]{:S(2)}) collective-permute-start(bf16[2,168,256]{2,1,0:T(8,128)(2,1)S(1)} %convert_element_type.200), channel_id=1, source_target_pairs={{0,224},{8,232},{16,240},{24,248},{32,0},{40,8},{48,16},{56,24},{6... | collective-permute-start | bytes 516104 | tf_op jit(solution)/shard_map/while/body/eval_jaxpr/ppermute | solution.py:76
  207.6 5.5 %collective-permute-start = (bf16[2,168,256]{2,1,0:T(8,128)(2,1)S(1)}, bf16[2,168,256]{2,1,0:T(8,128)(2,1)S(1)}, u32[]{:S(2)}, u32[]{:S(2)}) collective-permute-start(bf16[2,168,256]{2,1,0:T(8,128)(2,1)S(1)} %convert_element_type.199), channel_id=1, source_target_pairs={{0,32},{8,40},{16,48},{24,56},{32,64},{40,72},{48,80},{56,88},{64,... | collective-permute-start | bytes 516104 | tf_op jit(solution)/shard_map/while/body/eval_jaxpr/ppermute | solution.py:75
  208.5 6.7 %collective-permute-start.1 = (bf16[2,168,256]{2,1,0:T(8,128)(2,1)S(1)}, bf16[2,168,256]{2,1,0:T(8,128)(2,1)S(1)}, u32[]{:S(2)}, u32[]{:S(2)}) collective-permute-start(bf16[2,168,256]{2,1,0:T(8,128)(2,1)S(1)} %convert_element_type.200), channel_id=1, source_target_pairs={{0,224},{8,232},{16,240},{24,248},{32,0},{40,8},{48,16},{56,24},{6... | collective-permute-start | bytes 516104 | tf_op jit(solution)/shard_map/while/body/eval_jaxpr/ppermute | solution.py:76
  218.8 9.9 %collective-permute-start.7 = (bf16[168,512]{1,0:T(8,128)(2,1)S(1)}, bf16[168,512]{1,0:T(8,128)(2,1)S(1)}, u32[]{:S(2)}, u32[]{:S(2)}) collective-permute-start(bf16[168,512]{1,0:T(8,128)(2,1)S(1)} %fusion.26), channel_id=1, source_target_pairs={{0,16},{8,24},{16,0},{24,8},{32,48},{40,56},{48,32},{56,40},{64,80... | collective-permute-start | bytes 516104 | tf_op jit(solution)/shard_map/ppermute | solution.py:90
